TPU v7x, 512 devices: a whole 4x8x8 slice. The times are simulated.
512 devices in a mesh: pb: 32 (over y, x), ka: 16 (over z, core).
Axes of the slice: x: 4, y: 8, z: 8, core: 2. Of those that a mesh axis runs over, the one named last changes fastest.
Arguments:
- queries: bfloat16 [65536, 1536], P(('pb', 'ka')), may hold values from -6 to 6
- keys: bfloat16 [65536, 1536], P(('pb', 'ka')), may hold values from -6 to 6
- values: bfloat16 [65536, 1536], P(('pb', 'ka')), may hold values from -6 to 6
- adjacency: int32 [512, 24], P(('pb', 'ka')), may hold values from -1 to 511, as said below
- counts: int32 [512], P(('pb', 'ka')), may hold values from 1 to 24, as said below
Outputs:
- attended: bfloat16 [65536, 1536], P(('pb', 'ka'))
Inputs may be any that keep to these rules, and one draw needn't show every extreme that they name: adjacency[i, 0] = i; entries 1 to counts[i] - 1 are distinct blocks from i - 31 to i - 1; the other entries are -1. counts[i] is at most min(i + 1, 32); the last block lists exactly 24.
All inputs are finite; a program needn't handle non-finite values.
Results may differ from a plain program's by a relative error of at most 0.0053.
Values may be sent and summed in bfloat16 or wider, within the bound.
No kernel may reach another device: no remote copies, remote signals or barrier semaphores. Data moves between devices by JAX's collectives and lax.ppermute only.
A program may use at most 128 MiB of HBM per device.

v0:
```python
import math

import jax
import jax.numpy as jnp
from jax import lax
from jax.sharding import PartitionSpec as P

DH = 128


NEG_FILL = -1e30


def passed_along(block, axis, distance):
    devices = range(lax.axis_size(axis))
    route = [(i - distance, i) for i in devices if i - distance in devices]
    return lax.ppermute(block, axis, route)


def tile_partials(query_rows, permitted, position, anchors, kv_window, current):
    sources, item_count, feature_width = query_rows.shape
    span_count = kv_window.shape[1]
    block_len = kv_window.shape[2]
    head_count = feature_width // DH
    grouped = math.gcd(sources, max(1, 512 // item_count))
    head_step = math.gcd(head_count, 4)
    scaling = 1.0 / math.sqrt(DH)
    key_window = kv_window[0].reshape(span_count, block_len, head_count, DH)
    value_window = kv_window[1].reshape(span_count, block_len, head_count, DH)
    leading = jnp.arange(span_count) == 0
    key_pos = jnp.arange(block_len, dtype=jnp.int32)

    def one_group(pieces):
        q_group, allow_group, pos_group, anchor_group = pieces
        q_group = q_group.reshape(grouped, item_count, head_count, DH)
        causal = key_pos[None, None, None, :] <= pos_group[:, :, None, None]
        own_block = (anchor_group == current)[:, None] & leading[None, :]
        allowed = (allow_group[:, :, :, None] != 0) & (
            jnp.logical_not(own_block)[:, None, :, None] | causal
        )
        part_list = []
        max_list = []
        total_list = []
        for head_lo in range(0, head_count, head_step):
            head_hi = head_lo + head_step
            scores = (
                jnp.einsum(
                    "gthd,auhd->ghtau",
                    q_group[:, :, head_lo:head_hi],
                    key_window[:, :, head_lo:head_hi],
                    preferred_element_type=jnp.float32,
                )
                * scaling
            )
            masked = jnp.where(allowed[:, None], scores, NEG_FILL)
            highest = jnp.max(masked, axis=(3, 4))
            weights = jnp.where(allowed[:, None], jnp.exp(masked - highest[..., None, None]), 0.0)
            total_list.append(jnp.sum(weights, axis=(3, 4)))
            max_list.append(highest)
            blended = jnp.einsum(
                "ghtau,auhd->gthd",
                weights.astype(jnp.bfloat16),
                value_window[:, :, head_lo:head_hi],
                preferred_element_type=jnp.float32,
            )
            part_list.append(blended.astype(jnp.bfloat16))
        partial_out = jnp.concatenate(part_list, axis=2).reshape(grouped, item_count, feature_width)
        class_max = jnp.transpose(jnp.concatenate(max_list, axis=1), (0, 2, 1))
        class_total = jnp.transpose(jnp.concatenate(total_list, axis=1), (0, 2, 1))
        return (partial_out, class_max, class_total)

    outer = sources // grouped
    reshaped = (
        query_rows.reshape(outer, grouped, item_count, feature_width),
        permitted.reshape(outer, grouped, item_count, span_count),
        position.reshape(outer, grouped, item_count),
        anchors.reshape(outer, grouped),
    )
    partial_out, class_max, class_total = lax.map(one_group, reshaped)
    return (
        partial_out.reshape(sources, item_count, feature_width).astype(jnp.float32),
        class_max.reshape(sources, item_count, head_count),
        class_total.reshape(sources, item_count, head_count),
    )


def merge_classes(partial_out, class_max, class_total):
    sources, block_len, feature_width = partial_out.shape
    head_count = class_max.shape[2]
    highest = jnp.max(class_max, axis=0)
    factor = jnp.exp(class_max - highest[None])
    denominator = jnp.sum(factor * class_total, axis=0)
    numerator = jnp.sum(
        factor[..., None] * partial_out.reshape(sources, block_len, head_count, DH), axis=0
    )
    return (
        (numerator / denominator[..., None]).reshape(block_len, feature_width).astype(jnp.bfloat16)
    )


def per_device(queries, keys, values, adjacency, counts):
    block_len, feature_width = queries.shape
    stripe_count = lax.axis_size("ka")
    current = lax.axis_index("ka")
    row_index = lax.axis_index("pb")
    stacked = jnp.stack([keys, values])
    window = [stacked]
    earlier = stacked
    for repeat in range(2):
        earlier = passed_along(earlier, "pb", 1)
        window.append(earlier)
    kv_window = jnp.stack(window, axis=1)
    span_count = len(window)
    lag_ids = jnp.arange(span_count, dtype=jnp.int32)
    slot_ids = jnp.arange(adjacency.shape[1], dtype=jnp.int32)
    positions = jnp.broadcast_to(
        jnp.arange(block_len, dtype=jnp.int32)[None, :], (stripe_count, block_len)
    )
    anchors = jnp.arange(stripe_count, dtype=jnp.int32)
    row_q, row_adj, row_cnt = (
        lax.all_gather(queries, "ka", axis=0, tiled=True),
        lax.all_gather(adjacency, "ka", axis=0, tiled=True),
        lax.all_gather(counts, "ka", axis=0, tiled=True),
    )
    wanted = (row_index - lag_ids) * stripe_count + current
    listed = (row_adj[:, None, :] == wanted[None, :, None]) & (
        slot_ids[None, None, :] < row_cnt[:, None, None]
    )
    present = jnp.any(listed, axis=2).astype(jnp.int32)
    permitted = jnp.broadcast_to(present[:, None, :], (stripe_count, block_len, span_count))
    partial_out, class_max, class_total = tile_partials(
        row_q.reshape(stripe_count, block_len, feature_width),
        permitted,
        positions,
        anchors,
        kv_window,
        current,
    )
    partial_out, class_max, class_total = (
        lax.all_to_all(partial_out, "ka", split_axis=0, concat_axis=0, tiled=True),
        lax.all_to_all(class_max, "ka", split_axis=0, concat_axis=0, tiled=True),
        lax.all_to_all(class_total, "ka", split_axis=0, concat_axis=0, tiled=True),
    )
    return merge_classes(partial_out, class_max, class_total)


def solution(mesh):
    in_specs = (
        P(("pb", "ka"), None),
        P(("pb", "ka"), None),
        P(("pb", "ka"), None),
        P(("pb", "ka"), None),
        P(("pb", "ka")),
    )
    out_specs = P(("pb", "ka"), None)
    return jax.shard_map(
        per_device, mesh=mesh, in_specs=in_specs, out_specs=out_specs, check_vma=False
    )
```

profile of v0, /device:TPU:30, one launch (start us, length us, event | category | flops | bytes accessed | tf_op | source)
XLA Modules:
  0.0 505.4 jit_solution(13718441947726245500)
XLA Ops:
  7.3 1.2 copy.75
  8.5 1.2 copy.76
  9.8 4.6 collective-permute-start
  14.4 16.8 %collective-permute-done = bf16[2,128,1536]{1,2,0:T(8,128)(2,1)S(1)} collective-permute-done((bf16[2,128,1536]{1,2,0:T(8,128)(2,1)S(1)}, bf16[2,128,1536]{1,2,0:T(8,128)(2,1)S(1)}, u32[]{:S(2)}, u32[]{:S(2)}) %collective-permute-start) | collective-permute-done | bytes 786464 | tf_op jit(solution)/shard_map/ppermute | solution.py:17
  31.2 7.7 %collective-permute-start.1 = (bf16[2,128,1536]{1,2,0:T(8,128)(2,1)S(1)}, bf16[2,128,1536]{1,2,0:T(8,128)(2,1)S(1)}, u32[]{:S(2)}, u32[]{:S(2)}) collective-permute-start(bf16[2,128,1536]{1,2,0:T(8,128)(2,1)S(1)} %collective-permute-done), channel_id=1, source_target_pairs={{0,16},{16,32},{32,48},{48,64},{64,80},{80,96},{96,112},{112,128},... | collective-permute-start | bytes 2359304 | tf_op jit(solution)/shard_map/ppermute | solution.py:17
  39.6 1.3 dynamic-slice
  41.5 20.1 %all-reduce = s32[16]{0:T(128)S(1)} all-reduce(s32[16]{0:T(128)S(1)} %dynamic-update-slice), channel_id=1, replica_groups=mesh['pb'=32,'ka'=16] {'ka'}, use_global_device_ids=true, to_apply=%add | all-reduce | flops 16 | bytes 128
  61.6 15.1 %all-gather = s32[16,1,24]{2,1,0:T(1,128)S(1)} all-gather(s32[1,1,24]{2,1,0:T(1,128)S(1)} %bitcast.255), channel_id=1, replica_groups=mesh['pb'=32,'ka'=16] {'ka'}, dimensions={0}, use_global_device_ids=true | all-gather | bytes 1632 | tf_op jit(solution)/shard_map/all_gather | solution.py:122
  77.6 1.4 copy.80
  79.0 1.1 copy.81
  80.2 105.2 %while.15 = (s32[]{:T(128)}, bf16[4,4,128,1536]{2,3,1,0:T(8,128)(2,1)}, f32[4,4,128,12]{2,1,0,3:T(4,128)S(1)}, f32[4,4,128,12]{2,1,0,3:T(4,128)}, s32[4,4,128,3]...) while((s32[]{:T(128)}, ...), condition=%wide.region_8.9_spmd.clone, body=%wide.region_1.8_spmd.clone.sunk | while | flops 1241462272 | bytes 78790904 | solution.py:79
  80.6 1.5 constant_dynamic-slice_fusion.3
  83.0 1.1 fusion.116
  84.1 1.0 copy.119
  85.2 1.7 fusion.117
  86.9 2.0 copy.120
  88.9 4.0 bitcast_reduce_fusion.4
  92.9 2.0 copy.121
  95.0 4.6 fusion.118
  101.5 1.1 fusion.121
  102.6 1.1 fusion.120
  103.7 1.1 fusion.119
  105.2 1.3 constant_dynamic-update-slice_fusion.2
  106.9 1.5 constant_dynamic-slice_fusion.3
  109.3 1.1 fusion.116
  111.5 1.7 fusion.117
  113.2 2.0 copy.120
  115.2 4.0 bitcast_reduce_fusion.4
  119.2 2.0 copy.121
  121.3 4.6 fusion.118
  127.8 1.1 fusion.121
  128.9 1.1 fusion.120
  130.0 1.1 fusion.119
  131.5 1.3 constant_dynamic-update-slice_fusion.2
  133.1 1.5 constant_dynamic-slice_fusion.3
  135.6 1.1 fusion.116
  137.7 1.7 fusion.117
  139.5 2.0 copy.120
  141.5 4.0 bitcast_reduce_fusion.4
  145.5 2.0 copy.121
  147.5 4.6 fusion.118
  154.1 1.1 fusion.121
  155.2 1.1 fusion.120
  156.3 1.1 fusion.119
  157.8 1.3 constant_dynamic-update-slice_fusion.2
  159.4 1.5 constant_dynamic-slice_fusion.3
  161.8 1.1 fusion.116
  164.0 1.7 fusion.117
  165.7 2.0 copy.120
  167.8 4.0 bitcast_reduce_fusion.4
  171.8 2.0 copy.121
  173.8 4.7 fusion.118
  180.4 1.1 fusion.121
  181.5 1.1 fusion.120
  182.6 1.1 fusion.119
  184.1 1.3 constant_dynamic-update-slice_fusion.2
  186.0 3.9 all-to-all-start
  190.0 1.6 copy.85
  191.6 7.1 %all-to-all-done = f32[16,128,12]{1,2,0:T(8,128)S(1)} async-done(((f32[16,128,12]{1,2,0:T(8,128)}), f32[16,128,12]{1,2,0:T(8,128)S(1)}, u32[]{:S(2)}, u32[]{:S(2)}) %all-to-all-start) | async-done | bytes 98336 | tf_op jit(solution)/shard_map/all_to_all | solution.py:141
  198.6 3.7 all-to-all-start.2
  202.3 8.6 %bitcast_convert_fusion = f32[16,128,1536]{1,2,0:T(8,128)} fusion(bf16[4,4,128,1536]{2,3,1,0:T(8,128)(2,1)} %get-tuple-element.75), kind=kLoop, calls=%fused_computation.86 | loop fusion | flops 3145728 | bytes 18874368 | tf_op jit(solution)/shard_map/convert_element_type | solution.py:81
  211.0 7.0 %all-to-all-start.1 = ((f32[16,128,1536]{1,2,0:T(8,128)}), f32[16,128,1536]{1,2,0:T(8,128)}, u32[]{:S(2)}, u32[]{:S(2)}) async-start(f32[16,128,1536]{1,2,0:T(8,128)} %bitcast_convert_fusion), calls=%async_computation.1 | async-start | bytes 25165824 | tf_op jit(solution)/shard_map/all_to_all | solution.py:140
  218.0 274.0 %all-to-all-done.1 = f32[16,128,1536]{1,2,0:T(8,128)} async-done(((f32[16,128,1536]{1,2,0:T(8,128)}), f32[16,128,1536]{1,2,0:T(8,128)}, u32[]{:S(2)}, u32[]{:S(2)}) %all-to-all-start.1) | async-done | bytes 12582944 | tf_op jit(solution)/shard_map/all_to_all | solution.py:140
  492.0 5.6 %fusion.85 = f32[128,1536]{0,1:T(8,128)S(1)} fusion(f32[16,128,1536]{1,2,0:T(8,128)} %all-to-all-done.1, f32[16,128,12]{1,2,0:T(8,128)S(1)} %get-tuple-element.174), kind=kLoop, calls=%fused_computation.85 | loop fusion | flops 6094848 | bytes 13467648 | tf_op jit(solution)/shard_map/reduce_sum | solution.py:93
  (95 shorter events, 21.1 us)
Async XLA Ops:
  6.5 55.1 %copy-start.2 = (s32[1,24]{1,0:T(1,128)S(1)}, s32[1,24]{1,0:T(1,128)}, u32[]{:S(2)}) copy-start(s32[1,24]{1,0:T(1,128)} %param.10) | copy-start | bytes 292
  6.5 73.6 %all-gather.3.cloned.1.call-start = ((), (), s32[]{:S(2)}) async-start(), calls=%async_computation.3 | async-start | bytes 6684672 | tf_op jit(solution)/shard_map/all_gather | solution.py:121
  9.8 21.4 %collective-permute-start = (bf16[2,128,1536]{1,2,0:T(8,128)(2,1)S(1)}, bf16[2,128,1536]{1,2,0:T(8,128)(2,1)S(1)}, u32[]{:S(2)}, u32[]{:S(2)}) collective-permute-start(bf16[2,128,1536]{1,2,0:T(8,128)(2,1)S(1)} %get-tuple-element.185), channel_id=1, source_target_pairs={{0,16},{16,32},{32,48},{48,64},{64,80},{80,96},{96,112},{112,128},... | collective-permute-start | bytes 2359304 | tf_op jit(solution)/shard_map/ppermute | solution.py:17
  31.2 46.0 %collective-permute-start.1 = (bf16[2,128,1536]{1,2,0:T(8,128)(2,1)S(1)}, bf16[2,128,1536]{1,2,0:T(8,128)(2,1)S(1)}, u32[]{:S(2)}, u32[]{:S(2)}) collective-permute-start(bf16[2,128,1536]{1,2,0:T(8,128)(2,1)S(1)} %collective-permute-done), channel_id=1, source_target_pairs={{0,16},{16,32},{32,48},{48,64},{64,80},{80,96},{96,112},{112,128},... | collective-permute-start | bytes 2359304 | tf_op jit(solution)/shard_map/ppermute | solution.py:17
  95.0 6.1 %copy-start.1 = (bf16[3,128,12,128]{1,3,0,2:T(8,128)(2,1)S(1)}, bf16[3,128,12,128]{1,3,0,2:T(8,128)(2,1)}, u32[]{:S(2)}) copy-start(bf16[3,128,12,128]{1,3,0,2:T(8,128)(2,1)} %get-tuple-element.311) | copy-start | bytes 3538948 | tf_op jit(solution)/shard_map/while
  99.6 1.9 copy-start
  121.3 6.1 %copy-start.1 = (bf16[3,128,12,128]{1,3,0,2:T(8,128)(2,1)S(1)}, bf16[3,128,12,128]{1,3,0,2:T(8,128)(2,1)}, u32[]{:S(2)}) copy-start(bf16[3,128,12,128]{1,3,0,2:T(8,128)(2,1)} %get-tuple-element.311) | copy-start | bytes 3538948 | tf_op jit(solution)/shard_map/while
  125.9 1.9 copy-start
  147.5 6.1 %copy-start.1 = (bf16[3,128,12,128]{1,3,0,2:T(8,128)(2,1)S(1)}, bf16[3,128,12,128]{1,3,0,2:T(8,128)(2,1)}, u32[]{:S(2)}) copy-start(bf16[3,128,12,128]{1,3,0,2:T(8,128)(2,1)} %get-tuple-element.311) | copy-start | bytes 3538948 | tf_op jit(solution)/shard_map/while
  152.2 1.9 copy-start
  173.8 6.1 %copy-start.1 = (bf16[3,128,12,128]{1,3,0,2:T(8,128)(2,1)S(1)}, bf16[3,128,12,128]{1,3,0,2:T(8,128)(2,1)}, u32[]{:S(2)}) copy-start(bf16[3,128,12,128]{1,3,0,2:T(8,128)(2,1)} %get-tuple-element.311) | copy-start | bytes 3538948 | tf_op jit(solution)/shard_map/while
  178.5 1.9 copy-start
  186.0 12.6 %all-to-all-start = ((f32[16,128,12]{1,2,0:T(8,128)}), f32[16,128,12]{1,2,0:T(8,128)S(1)}, u32[]{:S(2)}, u32[]{:S(2)}) async-start(f32[16,128,12]{1,2,0:T(8,128)} %copy.83), calls=%async_computation | async-start | bytes 262144 | tf_op jit(solution)/shard_map/all_to_all | solution.py:141
  198.6 12.3 %all-to-all-start.2 = ((f32[16,128,12]{1,2,0:T(8,128)}), f32[16,128,12]{1,2,0:T(8,128)S(1)}, u32[]{:S(2)}, u32[]{:S(2)}) async-start(f32[16,128,12]{1,2,0:T(8,128)} %copy.85), calls=%async_computation.2 | async-start | bytes 262144 | tf_op jit(solution)/shard_map/all_to_all | solution.py:142
  211.0 281.0 %all-to-all-start.1 = ((f32[16,128,1536]{1,2,0:T(8,128)}), f32[16,128,1536]{1,2,0:T(8,128)}, u32[]{:S(2)}, u32[]{:S(2)}) async-start(f32[16,128,1536]{1,2,0:T(8,128)} %bitcast_convert_fusion), calls=%async_computation.1 | async-start | bytes 25165824 | tf_op jit(solution)/shard_map/all_to_all | solution.py:140
Sparse Core Ops, SparseCore 0:
  9.5 53.8 all-gather.2
where the time goes:
time: 507 us; the launch traced here: 505 us
  waiting for transfers between devices  299 us (59%)
  matrix products  54.7 us (11%)
  local copies, waits for them, and re-layouts  52.6 us (10%)
  blocking collectives  35.2 us (7%)
  starting transfers between devices  26.9 us (5%)
  other arithmetic  22.8 us (4%)
  between operations  14.2 us (3%)
    all_to_all x1, waiting for transfers between devices, per_device(): lax.all_to_all(partial_out, 'ka', split_axis=0, concat_axis=0, tiled=True)  274 us
    dot_general x12, matrix products, one_group(): jnp.einsum('gthd,auhd->ghtau', q_group[:, :, head_lo:head_hi], key_window...  41.4 us
    while x28, local copies, waits for them, and re-layouts  22.3 us
    unnamed x1, blocking collectives  20.1 us
    ppermute x2, waiting for transfers between devices, passed_along(): return lax.ppermute(block, axis, route)  16.8 us
    all_gather x1, blocking collectives, per_device(): lax.all_gather(adjacency, 'ka', axis=0, tiled=True)  15.1 us
    dot_general x12, matrix products, one_group(): jnp.einsum('ghtau,auhd->gthd', weights.astype(jnp.bfloat16), value_window...  13.3 us
    ppermute x2, starting transfers between devices, passed_along(): return lax.ppermute(block, axis, route)  12.3 us
  transfers between devices with their start and end apart: 6, of which 3 were waited for; matrix products, arithmetic and copies ran while one was open for 4% of the time, Pallas kernels for 0%

commit v1 on v0

--- a/solution.py
+++ b/solution.py
@@ -78,7 +78,7 @@
     )
     partial_out, class_max, class_total = lax.map(one_group, reshaped)
     return (
-        partial_out.reshape(sources, item_count, feature_width).astype(jnp.float32),
+        partial_out.reshape(sources, item_count, feature_width),
         class_max.reshape(sources, item_count, head_count),
         class_total.reshape(sources, item_count, head_count),
     )
@@ -117,11 +117,11 @@
         jnp.arange(block_len, dtype=jnp.int32)[None, :], (stripe_count, block_len)
     )
     anchors = jnp.arange(stripe_count, dtype=jnp.int32)
-    row_q, row_adj, row_cnt = (
-        lax.all_gather(queries, "ka", axis=0, tiled=True),
-        lax.all_gather(adjacency, "ka", axis=0, tiled=True),
-        lax.all_gather(counts, "ka", axis=0, tiled=True),
+    row_q = lax.all_gather(queries, "ka", axis=0, tiled=True)
+    row_table = lax.all_gather(
+        jnp.concatenate([adjacency, counts[:, None]], axis=1), "ka", axis=0, tiled=True
     )
+    row_adj, row_cnt = row_table[:, :-1], row_table[:, -1]
     wanted = (row_index - lag_ids) * stripe_count + current
     listed = (row_adj[:, None, :] == wanted[None, :, None]) & (
         slot_ids[None, None, :] < row_cnt[:, None, None]
@@ -141,7 +141,7 @@
         lax.all_to_all(class_max, "ka", split_axis=0, concat_axis=0, tiled=True),
         lax.all_to_all(class_total, "ka", split_axis=0, concat_axis=0, tiled=True),
     )
-    return merge_classes(partial_out, class_max, class_total)
+    return merge_classes(partial_out.astype(jnp.float32), class_max, class_total)
 
 
 def solution(mesh):

time: 507 us -> 355 us (0.70)
  the two profiles are of different devices: /device:TPU:30 before, /device:TPU:32 now
where the time goes in v1:
time: 355 us; the launch traced here: 353 us
  waiting for transfers between devices  168 us (47%)
  matrix products  54.6 us (15%)
  local copies, waits for them, and re-layouts  50.5 us (14%)
  blocking collectives  35 us (10%)
  starting transfers between devices  18 us (5%)
  between operations  14.2 us (4%)
  other arithmetic  12.7 us (4%)
    all_to_all x1, waiting for transfers between devices, per_device(): lax.all_to_all(partial_out, 'ka', split_axis=0, concat_axis=0, tiled=True)  139 us
    dot_general x12, matrix products, one_group(): jnp.einsum('gthd,auhd->ghtau', q_group[:, :, head_lo:head_hi], key_window...  41.3 us
    all_gather x1, blocking collectives, per_device(): lax.all_gather(jnp.concatenate([adjacency, counts[:, None]], axis=1), 'ka...  23.4 us
    while x28, local copies, waits for them, and re-layouts  22.5 us
    ppermute x2, waiting for transfers between devices, passed_along(): return lax.ppermute(block, axis, route)  20.4 us
    dot_general x12, matrix products, one_group(): jnp.einsum('ghtau,auhd->gthd', weights.astype(jnp.bfloat16), value_window...  13.3 us
    all_to_all x1, blocking collectives, per_device(): lax.all_to_all(class_total, 'ka', split_axis=0, concat_axis=0, tiled=True)  11.5 us
    dynamic_slice x8, local copies, waits for them, and re-layouts, tile_partials(): partial_out, class_max, class_total = lax.map(one_group, reshaped)  9.66 us
  transfers between devices with their start and end apart: 5, of which 3 were waited for; matrix products, arithmetic and copies ran while one was open for 2% of the time, Pallas kernels for 0%

profile of v1, /device:TPU:32, one launch (start us, length us, event | category | flops | bytes accessed | tf_op | source)
XLA Modules:
  0.0 353.4 jit_solution(4775251045843179692)
XLA Ops:
  7.3 1.2 copy.75
  8.5 1.2 copy.76
  9.8 3.4 collective-permute-start
  13.9 20.4 %collective-permute-done = bf16[2,128,1536]{1,2,0:T(8,128)(2,1)S(1)} collective-permute-done((bf16[2,128,1536]{1,2,0:T(8,128)(2,1)S(1)}, bf16[2,128,1536]{1,2,0:T(8,128)(2,1)S(1)}, u32[]{:S(2)}, u32[]{:S(2)}) %collective-permute-start) | collective-permute-done | bytes 786464 | tf_op jit(solution)/shard_map/ppermute | solution.py:17
  34.3 1.9 collective-permute-start.1
  36.3 23.4 %all-gather = s32[16,1,25]{2,1,0:T(1,128)S(1)} all-gather(s32[1,1,25]{2,1,0:T(1,128)S(1)} %add_bitcast_fusion), channel_id=1, replica_groups=mesh['pb'=32,'ka'=16] {'ka'}, dimensions={0}, use_global_device_ids=true | all-gather | bytes 1700 | tf_op jit(solution)/shard_map/all_gather | solution.py:121
  60.7 1.4 copy.80
  62.2 1.1 copy.81
  63.4 105.3 %while.15 = (s32[]{:T(128)}, bf16[4,4,128,1536]{2,3,1,0:T(8,128)(2,1)}, f32[4,4,128,12]{2,1,0,3:T(4,128)S(1)}, f32[4,4,128,12]{2,1,0,3:T(4,128)}, s32[4,4,128,3]...) while((s32[]{:T(128)}, ...), condition=%wide.region_8.9_spmd.clone, body=%wide.region_1.8_spmd.clone.sunk | while | flops 1241462272 | bytes 78790904 | solution.py:79
  63.7 1.5 constant_dynamic-slice_fusion.3
  66.2 1.1 fusion.116
  67.3 1.1 copy.119
  68.4 1.7 fusion.117
  70.1 2.0 copy.120
  72.1 4.0 %bitcast_reduce_fusion.4 = (f32[4,4,128]{2,0,1:T(4,128)S(1)}, f32[4,4,128]{2,0,1:T(4,128)S(1)}, f32[4,4,128,3,128]{2,4,3,1,0:T(8,128)}) fusion(pred[4,128,3,128]{1,3,2,0:T(8,128)(4,1)S(1)} %or_and_fusion.2, f32[4,4,128,3,128]{2,4,3,1,0:T(8,128)S(1)} %fusion.117, bf16[3,128,12,128]{3,1,0,2:T(8,128)(2,1)} %get-tuple-element.310, ...), kind=kOutput, calls=%fused_computation.11.clone.1 | convolution fusion | flops 206041088 | bytes 7421952 | tf_op jit(solution)/shard_map/while/body/eval_jaxpr/gthd,auhd->ghtau/dot_general | solution.py:47
  76.1 2.0 copy.121
  78.2 4.6 %fusion.118 = (f32[4,4,128]{2,0,1:T(4,128)S(1)}, f32[4,4,128]{2,0,1:T(4,128)S(1)}, f32[4,4,128]{2,0,1:T(4,128)S(1)}, f32[4,4,128,3,128]{2,4,3,1,0:T(8,128)S(1)}) fusion(f32[4,4,128,3,128]{2,4,3,1,0:T(8,128)} %get-tuple-element.267, f32[4,4,128]{2,0,1:T(4,128)S(1)} %get-tuple-element.268, pred[4,128,3,128]{1,3,2,0:T(8,128)(4,1)S(1)} %or_and_fusion.2, ...), kind=kOutput, calls=%fused_computation.17.clone.1 | convolution fusion | flops 211544064 | bytes 10788864 | tf_op jit(solution)/shard_map/while/body/eval_jaxpr/gthd,auhd->ghtau/dot_general | solution.py:47
  84.7 1.1 fusion.121
  85.8 1.1 fusion.120
  86.9 1.1 fusion.119
  88.4 1.3 constant_dynamic-update-slice_fusion.2
  90.0 1.5 constant_dynamic-slice_fusion.3
  92.5 1.1 fusion.116
  93.6 1.1 copy.119
  94.7 1.7 fusion.117
  96.4 2.0 copy.120
  98.4 4.0 %bitcast_reduce_fusion.4 = (f32[4,4,128]{2,0,1:T(4,128)S(1)}, f32[4,4,128]{2,0,1:T(4,128)S(1)}, f32[4,4,128,3,128]{2,4,3,1,0:T(8,128)}) fusion(pred[4,128,3,128]{1,3,2,0:T(8,128)(4,1)S(1)} %or_and_fusion.2, f32[4,4,128,3,128]{2,4,3,1,0:T(8,128)S(1)} %fusion.117, bf16[3,128,12,128]{3,1,0,2:T(8,128)(2,1)} %get-tuple-element.310, ...), kind=kOutput, calls=%fused_computation.11.clone.1 | convolution fusion | flops 206041088 | bytes 7421952 | tf_op jit(solution)/shard_map/while/body/eval_jaxpr/gthd,auhd->ghtau/dot_general | solution.py:47
  102.4 2.0 copy.121
  104.4 4.6 %fusion.118 = (f32[4,4,128]{2,0,1:T(4,128)S(1)}, f32[4,4,128]{2,0,1:T(4,128)S(1)}, f32[4,4,128]{2,0,1:T(4,128)S(1)}, f32[4,4,128,3,128]{2,4,3,1,0:T(8,128)S(1)}) fusion(f32[4,4,128,3,128]{2,4,3,1,0:T(8,128)} %get-tuple-element.267, f32[4,4,128]{2,0,1:T(4,128)S(1)} %get-tuple-element.268, pred[4,128,3,128]{1,3,2,0:T(8,128)(4,1)S(1)} %or_and_fusion.2, ...), kind=kOutput, calls=%fused_computation.17.clone.1 | convolution fusion | flops 211544064 | bytes 10788864 | tf_op jit(solution)/shard_map/while/body/eval_jaxpr/gthd,auhd->ghtau/dot_general | solution.py:47
  111.0 1.1 fusion.121
  112.1 1.1 fusion.120
  113.2 1.1 fusion.119
  114.7 1.3 constant_dynamic-update-slice_fusion.2
  116.4 1.5 constant_dynamic-slice_fusion.3
  118.8 1.1 fusion.116
  120.0 1.1 copy.119
  121.0 1.7 fusion.117
  122.7 2.0 copy.120
  124.8 4.0 %bitcast_reduce_fusion.4 = (f32[4,4,128]{2,0,1:T(4,128)S(1)}, f32[4,4,128]{2,0,1:T(4,128)S(1)}, f32[4,4,128,3,128]{2,4,3,1,0:T(8,128)}) fusion(pred[4,128,3,128]{1,3,2,0:T(8,128)(4,1)S(1)} %or_and_fusion.2, f32[4,4,128,3,128]{2,4,3,1,0:T(8,128)S(1)} %fusion.117, bf16[3,128,12,128]{3,1,0,2:T(8,128)(2,1)} %get-tuple-element.310, ...), kind=kOutput, calls=%fused_computation.11.clone.1 | convolution fusion | flops 206041088 | bytes 7421952 | tf_op jit(solution)/shard_map/while/body/eval_jaxpr/gthd,auhd->ghtau/dot_general | solution.py:47
  128.8 2.0 copy.121
  130.8 4.6 %fusion.118 = (f32[4,4,128]{2,0,1:T(4,128)S(1)}, f32[4,4,128]{2,0,1:T(4,128)S(1)}, f32[4,4,128]{2,0,1:T(4,128)S(1)}, f32[4,4,128,3,128]{2,4,3,1,0:T(8,128)S(1)}) fusion(f32[4,4,128,3,128]{2,4,3,1,0:T(8,128)} %get-tuple-element.267, f32[4,4,128]{2,0,1:T(4,128)S(1)} %get-tuple-element.268, pred[4,128,3,128]{1,3,2,0:T(8,128)(4,1)S(1)} %or_and_fusion.2, ...), kind=kOutput, calls=%fused_computation.17.clone.1 | convolution fusion | flops 211544064 | bytes 10788864 | tf_op jit(solution)/shard_map/while/body/eval_jaxpr/gthd,auhd->ghtau/dot_general | solution.py:47
  137.4 1.1 fusion.121
  138.5 1.1 fusion.120
  139.6 1.1 fusion.119
  141.1 1.3 constant_dynamic-update-slice_fusion.2
  142.7 1.5 constant_dynamic-slice_fusion.3
  145.1 1.1 fusion.116
  146.3 1.1 copy.119
  147.3 1.7 fusion.117
  149.1 2.0 copy.120
  151.1 4.0 %bitcast_reduce_fusion.4 = (f32[4,4,128]{2,0,1:T(4,128)S(1)}, f32[4,4,128]{2,0,1:T(4,128)S(1)}, f32[4,4,128,3,128]{2,4,3,1,0:T(8,128)}) fusion(pred[4,128,3,128]{1,3,2,0:T(8,128)(4,1)S(1)} %or_and_fusion.2, f32[4,4,128,3,128]{2,4,3,1,0:T(8,128)S(1)} %fusion.117, bf16[3,128,12,128]{3,1,0,2:T(8,128)(2,1)} %get-tuple-element.310, ...), kind=kOutput, calls=%fused_computation.11.clone.1 | convolution fusion | flops 206041088 | bytes 7421952 | tf_op jit(solution)/shard_map/while/body/eval_jaxpr/gthd,auhd->ghtau/dot_general | solution.py:47
  155.1 2.0 copy.121
  157.1 4.6 %fusion.118 = (f32[4,4,128]{2,0,1:T(4,128)S(1)}, f32[4,4,128]{2,0,1:T(4,128)S(1)}, f32[4,4,128]{2,0,1:T(4,128)S(1)}, f32[4,4,128,3,128]{2,4,3,1,0:T(8,128)S(1)}) fusion(f32[4,4,128,3,128]{2,4,3,1,0:T(8,128)} %get-tuple-element.267, f32[4,4,128]{2,0,1:T(4,128)S(1)} %get-tuple-element.268, pred[4,128,3,128]{1,3,2,0:T(8,128)(4,1)S(1)} %or_and_fusion.2, ...), kind=kOutput, calls=%fused_computation.17.clone.1 | convolution fusion | flops 211544064 | bytes 10788864 | tf_op jit(solution)/shard_map/while/body/eval_jaxpr/gthd,auhd->ghtau/dot_general | solution.py:47
  163.7 1.1 fusion.121
  164.8 1.1 fusion.120
  165.9 1.1 fusion.119
  167.4 1.2 constant_dynamic-update-slice_fusion.2
  169.3 8.0 %all-to-all-start = ((f32[16,128,12]{1,2,0:T(8,128)}), f32[16,128,12]{1,2,0:T(8,128)S(1)}, u32[]{:S(2)}, u32[]{:S(2)}) async-start(f32[16,128,12]{1,2,0:T(8,128)} %copy.83), calls=%async_computation | async-start | bytes 262144 | tf_op jit(solution)/shard_map/all_to_all | solution.py:141
  177.4 0.9 copy.85
  178.3 7.7 %all-to-all-done = f32[16,128,12]{1,2,0:T(8,128)S(1)} async-done(((f32[16,128,12]{1,2,0:T(8,128)}), f32[16,128,12]{1,2,0:T(8,128)S(1)}, u32[]{:S(2)}, u32[]{:S(2)}) %all-to-all-start) | async-done | bytes 98336 | tf_op jit(solution)/shard_map/all_to_all | solution.py:141
  186.0 11.5 %all_to_all.15 = f32[16,128,12]{1,2,0:T(8,128)S(1)} all-to-all(f32[16,128,12]{1,2,0:T(8,128)S(1)} %copy.85), channel_id=1, replica_groups=mesh['pb'=32,'ka'=16] {'ka'}, dimensions={0} | all-to-all | bytes 196608 | tf_op jit(solution)/shard_map/all_to_all | solution.py:142
  197.6 4.6 %all-to-all-start.1 = ((bf16[16,128,1536]{1,2,0:T(8,128)(2,1)}), bf16[16,128,1536]{1,2,0:T(8,128)(2,1)}, u32[]{:S(2)}, u32[]{:S(2)}) async-start(bf16[16,128,1536]{1,2,0:T(8,128)(2,1)} %bitcast.16), calls=%async_computation.1 | async-start | bytes 12582912 | tf_op jit(solution)/shard_map/all_to_all | solution.py:140
  202.3 139.2 %all-to-all-done.1 = bf16[16,128,1536]{1,2,0:T(8,128)(2,1)} async-done(((bf16[16,128,1536]{1,2,0:T(8,128)(2,1)}), bf16[16,128,1536]{1,2,0:T(8,128)(2,1)}, u32[]{:S(2)}, u32[]{:S(2)}) %all-to-all-start.1) | async-done | bytes 6291488 | tf_op jit(solution)/shard_map/all_to_all | solution.py:140
  341.4 4.1 %fusion.85 = f32[128,1536]{0,1:T(8,128)S(1)} fusion(bf16[16,128,1536]{1,2,0:T(8,128)(2,1)} %all-to-all-done.1, f32[16,128,12]{1,2,0:T(8,128)S(1)} %get-tuple-element.174), kind=kLoop, calls=%fused_computation.85 | loop fusion | flops 9240576 | bytes 7176192 | tf_op jit(solution)/shard_map/reduce_sum | solution.py:93
  (91 shorter events, 17.6 us)
Async XLA Ops:
  6.5 29.7 %copy-start.2 = (s32[1,24]{1,0:T(1,128)S(1)}, s32[1,24]{1,0:T(1,128)}, u32[]{:S(2)}) copy-start(s32[1,24]{1,0:T(1,128)} %param.10) | copy-start | bytes 292
  6.5 56.7 %all-gather.3.cloned.1.call-start = ((), (), s32[]{:S(2)}) async-start(), calls=%async_computation.3 | async-start | bytes 6684672 | tf_op jit(solution)/shard_map/all_gather | solution.py:120
  9.8 24.5 %collective-permute-start = (bf16[2,128,1536]{1,2,0:T(8,128)(2,1)S(1)}, bf16[2,128,1536]{1,2,0:T(8,128)(2,1)S(1)}, u32[]{:S(2)}, u32[]{:S(2)}) collective-permute-start(bf16[2,128,1536]{1,2,0:T(8,128)(2,1)S(1)} %get-tuple-element.185), channel_id=1, source_target_pairs={{0,16},{16,32},{32,48},{48,64},{64,80},{80,96},{96,112},{112,128},... | collective-permute-start | bytes 2359304 | tf_op jit(solution)/shard_map/ppermute | solution.py:17
  34.3 26.0 %collective-permute-start.1 = (bf16[2,128,1536]{1,2,0:T(8,128)(2,1)S(1)}, bf16[2,128,1536]{1,2,0:T(8,128)(2,1)S(1)}, u32[]{:S(2)}, u32[]{:S(2)}) collective-permute-start(bf16[2,128,1536]{1,2,0:T(8,128)(2,1)S(1)} %collective-permute-done), channel_id=1, source_target_pairs={{0,16},{16,32},{32,48},{48,64},{64,80},{80,96},{96,112},{112,128},... | collective-permute-start | bytes 2359304 | tf_op jit(solution)/shard_map/ppermute | solution.py:17
  78.2 6.1 %copy-start.1 = (bf16[3,128,12,128]{1,3,0,2:T(8,128)(2,1)S(1)}, bf16[3,128,12,128]{1,3,0,2:T(8,128)(2,1)}, u32[]{:S(2)}) copy-start(bf16[3,128,12,128]{1,3,0,2:T(8,128)(2,1)} %get-tuple-element.311) | copy-start | bytes 3538948 | tf_op jit(solution)/shard_map/while
  82.8 1.9 copy-start
  104.4 6.1 %copy-start.1 = (bf16[3,128,12,128]{1,3,0,2:T(8,128)(2,1)S(1)}, bf16[3,128,12,128]{1,3,0,2:T(8,128)(2,1)}, u32[]{:S(2)}) copy-start(bf16[3,128,12,128]{1,3,0,2:T(8,128)(2,1)} %get-tuple-element.311) | copy-start | bytes 3538948 | tf_op jit(solution)/shard_map/while
  109.1 1.9 copy-start
  130.8 6.1 %copy-start.1 = (bf16[3,128,12,128]{1,3,0,2:T(8,128)(2,1)S(1)}, bf16[3,128,12,128]{1,3,0,2:T(8,128)(2,1)}, u32[]{:S(2)}) copy-start(bf16[3,128,12,128]{1,3,0,2:T(8,128)(2,1)} %get-tuple-element.311) | copy-start | bytes 3538948 | tf_op jit(solution)/shard_map/while
  135.5 1.9 copy-start
  157.1 6.1 %copy-start.1 = (bf16[3,128,12,128]{1,3,0,2:T(8,128)(2,1)S(1)}, bf16[3,128,12,128]{1,3,0,2:T(8,128)(2,1)}, u32[]{:S(2)}) copy-start(bf16[3,128,12,128]{1,3,0,2:T(8,128)(2,1)} %get-tuple-element.311) | copy-start | bytes 3538948 | tf_op jit(solution)/shard_map/while
  161.8 1.9 copy-start
  169.3 16.7 %all-to-all-start = ((f32[16,128,12]{1,2,0:T(8,128)}), f32[16,128,12]{1,2,0:T(8,128)S(1)}, u32[]{:S(2)}, u32[]{:S(2)}) async-start(f32[16,128,12]{1,2,0:T(8,128)} %copy.83), calls=%async_computation | async-start | bytes 262144 | tf_op jit(solution)/shard_map/all_to_all | solution.py:141
  197.6 143.9 %all-to-all-start.1 = ((bf16[16,128,1536]{1,2,0:T(8,128)(2,1)}), bf16[16,128,1536]{1,2,0:T(8,128)(2,1)}, u32[]{:S(2)}, u32[]{:S(2)}) async-start(bf16[16,128,1536]{1,2,0:T(8,128)(2,1)} %bitcast.16), calls=%async_computation.1 | async-start | bytes 12582912 | tf_op jit(solution)/shard_map/all_to_all | solution.py:140
Sparse Core Ops, SparseCore 0:
  9.5 53.7 all-gather.2

commit v2 on v1

v2 whole, which is shorter than its diff:
```python
import math

import jax
import jax.numpy as jnp
from jax import lax
from jax.experimental import pallas as pl
from jax.experimental.pallas import tpu as pltpu
from jax.sharding import PartitionSpec as P

DH = 128


NEG_FILL = -1e30
LAGS = 3


def passed_along(block, axis, distance):
    devices = range(lax.axis_size(axis))
    route = [(i - distance, i) for i in devices if i - distance in devices]
    return lax.ppermute(block, axis, route)


def class_kernel(info_ref, q_ref, k1_ref, kx_ref, v1_ref, vx_ref, out_ref, max_ref, tot_ref):
    cp = pl.program_id(0)
    current = info_ref[0]
    block_len = q_ref.shape[1]
    head_count = q_ref.shape[2] // DH
    lag_x = jnp.where(current <= cp, 0, 2)
    listed_1 = info_ref[1 + cp * LAGS + 1] != 0
    listed_x = info_ref[1 + cp * LAGS + lag_x] != 0
    diagonal = current == cp
    reach_1 = jnp.where(listed_1, block_len, -2 * block_len)
    reach_x = jnp.where(listed_x, jnp.where(diagonal, 0, block_len), -2 * block_len)
    q_pos = lax.broadcasted_iota(jnp.int32, (block_len, block_len), 0)
    k_pos = lax.broadcasted_iota(jnp.int32, (block_len, block_len), 1)
    allowed_1 = k_pos <= q_pos + reach_1
    allowed_x = k_pos <= q_pos + reach_x
    scaling = 1.0 / math.sqrt(DH)
    nt = (((1,), (1,)), ((), ()))
    for h in range(head_count):
        cols = slice(h * DH, (h + 1) * DH)
        q = q_ref[0, :, cols]
        s1 = lax.dot_general(q, k1_ref[0, :, cols], nt, preferred_element_type=jnp.float32)
        sx = lax.dot_general(q, kx_ref[0, :, cols], nt, preferred_element_type=jnp.float32)
        s1 = jnp.where(allowed_1, s1 * scaling, NEG_FILL)
        sx = jnp.where(allowed_x, sx * scaling, NEG_FILL)
        highest = jnp.maximum(
            jnp.max(s1, axis=1, keepdims=True), jnp.max(sx, axis=1, keepdims=True)
        )
        w1 = jnp.where(allowed_1, jnp.exp(s1 - highest), 0.0)
        wx = jnp.where(allowed_x, jnp.exp(sx - highest), 0.0)
        total = jnp.sum(w1, axis=1, keepdims=True) + jnp.sum(wx, axis=1, keepdims=True)
        blended = jnp.dot(
            w1.astype(jnp.bfloat16), v1_ref[0, :, cols], preferred_element_type=jnp.float32
        ) + jnp.dot(wx.astype(jnp.bfloat16), vx_ref[0, :, cols], preferred_element_type=jnp.float32)
        out_ref[0, :, cols] = blended.astype(jnp.bfloat16)
        max_ref[0, :, h : h + 1] = highest
        tot_ref[0, :, h : h + 1] = total


def class_partials(info, row_q, key_window, value_window):
    sources, block_len, feature_width = row_q.shape
    head_count = feature_width // DH

    def lag_x_map(cp, info_ref):
        return (jnp.where(info_ref[0] <= cp, 0, 2), 0, 0)

    block = (1, block_len, feature_width)
    stat = (1, block_len, head_count)
    grid_spec = pltpu.PrefetchScalarGridSpec(
        num_scalar_prefetch=1,
        grid=(sources,),
        in_specs=[
            pl.BlockSpec(block, lambda cp, info_ref: (cp, 0, 0)),
            pl.BlockSpec(block, lambda cp, info_ref: (1, 0, 0)),
            pl.BlockSpec(block, lag_x_map),
            pl.BlockSpec(block, lambda cp, info_ref: (1, 0, 0)),
            pl.BlockSpec(block, lag_x_map),
        ],
        out_specs=[
            pl.BlockSpec(block, lambda cp, info_ref: (cp, 0, 0)),
            pl.BlockSpec(stat, lambda cp, info_ref: (cp, 0, 0)),
            pl.BlockSpec(stat, lambda cp, info_ref: (cp, 0, 0)),
        ],
    )
    flops = sources * head_count * 4 * 2 * block_len * block_len * DH
    return pl.pallas_call(
        class_kernel,
        grid_spec=grid_spec,
        out_shape=[
            jax.ShapeDtypeStruct((sources, block_len, feature_width), jnp.bfloat16),
            jax.ShapeDtypeStruct((sources, block_len, head_count), jnp.float32),
            jax.ShapeDtypeStruct((sources, block_len, head_count), jnp.float32),
        ],
        cost_estimate=pl.CostEstimate(
            flops=flops,
            transcendentals=sources * head_count * 2 * block_len * block_len,
            bytes_accessed=2 * sources * block_len * feature_width * 2 + 4 * block_len * feature_width * 2,
        ),
    )(info, row_q, key_window, key_window, value_window, value_window)


def per_device(queries, keys, values, adjacency, counts):
    block_len, feature_width = queries.shape
    head_count = feature_width // DH
    chips = lax.axis_size("z")
    cores = lax.axis_size("core")
    stripe_count = chips * cores
    core = lax.axis_index("core")
    current = lax.axis_index("z") * cores + core
    row_index = lax.axis_index("pb")
    key_window = jnp.stack([keys, passed_along(keys, "pb", 1), passed_along(keys, "pb", 2)])
    value_window = jnp.stack(
        [values, passed_along(values, "pb", 1), passed_along(values, "pb", 2)]
    )
    row_q = lax.all_gather(queries, ("z", "core"), axis=0, tiled=True)
    row_table = lax.all_gather(
        jnp.concatenate([adjacency, counts[:, None]], axis=1), ("z", "core"), axis=0, tiled=True
    )
    row_adj, row_cnt = row_table[:, :-1], row_table[:, -1]
    lag_ids = jnp.arange(LAGS, dtype=jnp.int32)
    slot_ids = jnp.arange(adjacency.shape[1], dtype=jnp.int32)
    wanted = (row_index - lag_ids) * stripe_count + current
    listed = (row_adj[:, None, :] == wanted[None, :, None]) & (
        slot_ids[None, None, :] < row_cnt[:, None, None]
    )
    present = jnp.any(listed, axis=2).astype(jnp.int32)
    info = jnp.concatenate([current.reshape(1).astype(jnp.int32), present.reshape(-1)])
    partial_out, class_max, class_total = class_partials(
        info, row_q.reshape(stripe_count, block_len, feature_width), key_window, value_window
    )

    def split(x):
        x = x.reshape((chips, cores) + x.shape[1:])
        keep = lax.dynamic_index_in_dim(x, core, axis=1, keepdims=False)
        give = lax.dynamic_index_in_dim(x, 1 - core, axis=1, keepdims=False)
        return keep, give

    swap = [(0, 1), (1, 0)]
    own_out, give_out = split(partial_out)
    own_max, give_max = split(class_max)
    own_tot, give_tot = split(class_total)
    peer_out = lax.ppermute(give_out, "core", swap)
    peer_stats = lax.ppermute(jnp.concatenate([give_max, give_tot], axis=2), "core", swap)
    peer_max, peer_tot = peer_stats[..., :head_count], peer_stats[..., head_count:]
    pair_max = jnp.maximum(own_max, peer_max)
    own_f = jnp.exp(own_max - pair_max)
    peer_f = jnp.exp(peer_max - pair_max)
    pair_tot = own_f * own_tot + peer_f * peer_tot
    pair_out = (
        own_f[..., None] * own_out.astype(jnp.float32).reshape(chips, block_len, head_count, DH)
        + peer_f[..., None] * peer_out.astype(jnp.float32).reshape(chips, block_len, head_count, DH)
    ).astype(jnp.bfloat16)

    pair_out = lax.all_to_all(pair_out, "z", split_axis=0, concat_axis=0, tiled=True)
    pair_stats = lax.all_to_all(
        jnp.concatenate([pair_max, pair_tot], axis=2), "z", split_axis=0, concat_axis=0, tiled=True
    )
    pair_max, pair_tot = pair_stats[..., :head_count], pair_stats[..., head_count:]
    highest = jnp.max(pair_max, axis=0)
    factor = jnp.exp(pair_max - highest[None])
    denominator = jnp.sum(factor * pair_tot, axis=0)
    numerator = jnp.sum(factor[..., None] * pair_out.astype(jnp.float32), axis=0)
    return (
        (numerator / denominator[..., None]).reshape(block_len, feature_width).astype(jnp.bfloat16)
    )


def solution(mesh):
    pb, ka = mesh.devices.shape
    grid = jax.sharding.Mesh(mesh.devices.reshape(pb, ka // 2, 2), ("pb", "z", "core"))
    rows = P(("pb", "z", "core"), None)
    in_specs = (rows, rows, rows, rows, P(("pb", "z", "core")))
    return jax.shard_map(
        per_device, mesh=grid, in_specs=in_specs, out_specs=rows, check_vma=False
    )
```

time: 355 us -> 247 us (0.70)
  the two profiles are of different devices: /device:TPU:32 before, /device:TPU:1 now
where the time goes in v2:
time: 247 us; the launch traced here: 246 us
  waiting for transfers between devices  86.4 us (35%)
  Pallas kernels  55.8 us (23%)
  starting transfers between devices  28.7 us (12%)
  blocking collectives  25.1 us (10%)
  local copies, waits for them, and re-layouts  22.4 us (9%)
  between operations  14.2 us (6%)
  other arithmetic  13.5 us (5%)
    all_to_all x1, waiting for transfers between devices, per_device(): lax.all_to_all(pair_out, 'z', split_axis=0, concat_axis=0, tiled=True)  74.2 us
    pallas_call x1, Pallas kernels, class_partials(): pl.pallas_call(class_kernel, grid_spec=grid_spec, out_shape=[jax.ShapeDty...  55.8 us
    all_gather x1, blocking collectives, per_device(): lax.all_gather(jnp.concatenate([adjacency, counts[:, None]], axis=1), ('z...  25.1 us
    ppermute x4, starting transfers between devices, passed_along(): return lax.ppermute(block, axis, route)  14.9 us
    all_gather x1, waiting for transfers between devices, per_device(): row_q = lax.all_gather(queries, ('z', 'core'), axis=0, tiled=True)  10.6 us
    dynamic_slice x2, local copies, waits for them, and re-layouts, split(): keep = lax.dynamic_index_in_dim(x, core, axis=1, keepdims=False)  8.01 us
    unnamed x5, local copies, waits for them, and re-layouts  7.79 us
    convert_element_type x1, other arithmetic, per_device(): pair_out = (own_f[..., None] * own_out.astype(jnp.float32).reshape(chips,...  6.58 us
  transfers between devices with their start and end apart: 9, of which 3 were waited for; matrix products, arithmetic and copies ran while one was open for 10% of the time, Pallas kernels for 0%

profile of v2, /device:TPU:1, one launch (start us, length us, event | category | flops | bytes accessed | tf_op | source)
XLA Modules:
  0.0 246.0 jit_solution(6331918174104475748)
XLA Ops:
  6.5 0.0 all-gather.3.cloned.1.call-start
  6.5 0.7 all-gather.3.cloned.1.call-update
  7.3 4.0 %collective-permute-start = (bf16[128,1536]{1,0:T(8,128)(2,1)}, bf16[128,1536]{1,0:T(8,128)(2,1)S(1)}, u32[]{:S(2)}, u32[]{:S(2)}) collective-permute-start(bf16[128,1536]{1,0:T(8,128)(2,1)} %param.6), channel_id=1, source_target_pairs={{0,16},{16,32},{32,48},{48,64},{64,80},{80,96},{96,112},{112,128},... | collective-permute-start | bytes 1179656 | tf_op jit(solution)/shard_map/ppermute | solution.py:20
  11.2 4.4 %collective-permute-start.1 = (bf16[128,1536]{1,0:T(8,128)(2,1)}, bf16[128,1536]{1,0:T(8,128)(2,1)S(1)}, u32[]{:S(2)}, u32[]{:S(2)}) collective-permute-start(bf16[128,1536]{1,0:T(8,128)(2,1)} %param.6), channel_id=1, source_target_pairs={{0,32},{16,48},{32,64},{48,80},{64,96},{80,112},{96,128},{112,144}... | collective-permute-start | bytes 1179656 | tf_op jit(solution)/shard_map/ppermute | solution.py:20
  15.6 3.4 %collective-permute-start.3 = (bf16[128,1536]{1,0:T(8,128)(2,1)}, bf16[128,1536]{1,0:T(8,128)(2,1)S(1)}, u32[]{:S(2)}, u32[]{:S(2)}) collective-permute-start(bf16[128,1536]{1,0:T(8,128)(2,1)} %param.7), channel_id=1, source_target_pairs={{0,32},{16,48},{32,64},{48,80},{64,96},{80,112},{96,128},{112,144}... | collective-permute-start | bytes 1179656 | tf_op jit(solution)/shard_map/ppermute | solution.py:20
  19.0 3.1 %collective-permute-start.2 = (bf16[128,1536]{1,0:T(8,128)(2,1)}, bf16[128,1536]{1,0:T(8,128)(2,1)S(1)}, u32[]{:S(2)}, u32[]{:S(2)}) collective-permute-start(bf16[128,1536]{1,0:T(8,128)(2,1)} %param.7), channel_id=1, source_target_pairs={{0,16},{16,32},{32,48},{48,64},{64,80},{80,96},{96,112},{112,128},... | collective-permute-start | bytes 1179656 | tf_op jit(solution)/shard_map/ppermute | solution.py:20
  22.8 0.7 add_bitcast_fusion
  23.6 25.1 %all-gather = s32[16,1,25]{2,1,0:T(1,128)S(1)} all-gather(s32[1,1,25]{2,1,0:T(1,128)S(1)} %add_bitcast_fusion), channel_id=1, replica_groups=mesh['pb'=32,'z'=8,'core'=2] {'z','core'}, dimensions={0}, use_global_device_ids=true | all-gather | bytes 1700 | tf_op jit(solution)/shard_map/all_gather | solution.py:117
  48.6 0.2 slice_reduce_fusion.1
  48.8 0.1 iota_compare_fusion
  48.9 0.2 and_reduce_fusion
  49.1 0.1 copy.29
  49.2 0.1 reshape.76
  49.3 0.6 pad_add_fusion.info_ref
  49.9 0.0 collective-permute-done
  49.9 0.0 collective-permute-done.1
  49.9 2.2 pad_maximum_fusion.k1_ref.kx_ref
  52.1 0.0 collective-permute-done.3
  52.1 0.0 collective-permute-done.2
  52.1 2.1 pad_maximum_fusion.1.v1_ref.vx_ref
  54.3 10.6 %all-gather.3.cloned.1.call-done = bf16[2048,1536]{1,0:T(8,128)(2,1)} async-done(((bf16[128,1536]{1,0:T(8,128)(2,1)}), bf16[2048,1536]{1,0:T(8,128)(2,1)}) %all-gather.3.cloned.1.call-update) | async-done | bytes 6291472 | tf_op jit(solution)/shard_map/all_gather | solution.py:116
  64.9 55.8 %shard_map.55 = (bf16[16,128,1536]{2,1,0:T(8,128)(2,1)}, f32[16,128,12]{2,1,0:T(8,128)}, f32[16,128,12]{2,1,0:T(8,128)}) custom-call(s32[49]{0:T(128)} %pad_add_fusion.info_ref, bf16[16,128,1536]{2,1,0:T(8,128)(2,1)} %bitcast.52, bf16[3,128,1536]{2,1,0:T(8,128)(2,1)} %pad_maximum_fusion.k1_ref.kx_ref, bf16[3,128,1536]{2,1,0:T(8,128)(2,1)} %pad_maximum_fusion.k1_ref.kx_ref, ...), custom_call_target="tpu_custom_call" | custom-call | flops 3221225472 | bytes 14155776 | tf_op jit(solution)/shard_map/pallas_call | solution.py:87
  120.7 5.1 %constant_dynamic-slice_fusion.1 = (bf16[8,1,128,1536]{3,2,1,0:T(8,128)(2,1)S(1)}, bf16[8,1,128,1536]{3,2,1,0:T(8,128)(2,1)}) fusion(bf16[8,2,128,1536]{3,2,1,0:T(8,128)(2,1)} %bitcast.37, s32[]{:T(128)S(6)} %select_n.12, s32[]{:T(128)S(6)} %select_n.13), kind=kLoop, calls=%fused_computation.25 | loop fusion | bytes 12582920 | tf_op jit(solution)/shard_map/jit(dynamic_index_in_dim)/dynamic_slice | solution.py:135
  125.8 4.7 %copy.38 = bf16[8,1,128,1536]{2,3,0,1:T(8,128)(2,1)} copy(bf16[8,1,128,1536]{3,2,1,0:T(8,128)(2,1)} %get-tuple-element.18) | data formatting | bytes 6291456 | tf_op jit(solution)/shard_map/jit(dynamic_index_in_dim)/dynamic_slice | solution.py:136
  130.4 2.1 collective-permute-start.5
  132.5 2.9 %constant_dynamic-slice_fusion.2 = (f32[8,1,128,12]{3,2,1,0:T(8,128)}, f32[8,1,128,12]{3,2,1,0:T(8,128)}, f32[8,1,128,12]{3,2,1,0:T(8,128)}, f32[8,1,128,12]{3,2,1,0:T(8,128)}) fusion(f32[8,2,128,12]{3,2,1,0:T(8,128)} %bitcast.41, s32[]{:T(128)S(6)} %select_n.12, s32[]{:T(128)S(6)} %select_n.13, f32[8,2,128,12]{3,2,1,0:T(8,128)} %bitcast.40), kind=kLoop, calls=%fused_computation.26 | loop fusion | bytes 393224 | tf_op jit(solution)/shard_map/jit(dynamic_index_in_dim)/dynamic_slice | solution.py:135
  135.4 1.2 copy.41
  136.6 1.2 copy.42
  137.9 2.3 collective-permute-start.4
  140.2 1.2 copy.40
  141.4 1.2 copy.43
  142.6 2.9 %copy.44 = bf16[8,1,128,1536]{2,3,0,1:T(8,128)(2,1)} copy(bf16[8,1,128,1536]{3,2,1,0:T(8,128)(2,1)S(1)} %get-tuple-element.17) | data formatting | bytes 6291456
  145.5 0.0 collective-permute-done.4
  145.5 0.7 copy.34
  146.2 3.7 %all-to-all-start = ((f32[8,128,24]{1,2,0:T(8,128)}), f32[8,128,24]{1,2,0:T(8,128)S(1)}, u32[]{:S(2)}, u32[]{:S(2)}) async-start(f32[8,128,24]{1,2,0:T(8,128)} %copy.34), calls=%async_computation | async-start | bytes 196608 | tf_op jit(solution)/shard_map/all_to_all | solution.py:156
  149.9 0.0 collective-permute-done.5
  149.9 6.6 %fusion.1 = bf16[8,128,12,128]{1,3,2,0:T(8,128)(2,1)} fusion(bf16[8,128,12,128]{1,3,2,0:T(8,128)(2,1)} %bitcast.23, bf16[8,128,12,128]{1,3,2,0:T(8,128)(2,1)} %bitcast.36, f32[8,128,12]{1,2,0:T(8,128)S(1)} %copy.37, f32[8,128,12]{1,2,0:T(8,128)S(1)} %copy.35), kind=kLoop, calls=%fused_computation.2 | loop fusion | flops 9437184 | bytes 9535488 | tf_op jit(solution)/shard_map/convert_element_type | solution.py:153
  156.5 0.8 all-to-all-done
  157.3 5.8 %all-to-all-start.1 = ((bf16[8,128,12,128]{1,3,2,0:T(8,128)(2,1)}), bf16[8,128,12,128]{1,3,2,0:T(8,128)(2,1)S(1)}, u32[]{:S(2)}, u32[]{:S(2)}) async-start(bf16[8,128,12,128]{1,3,2,0:T(8,128)(2,1)} %fusion.1), calls=%async_computation.1 | async-start | bytes 6291456 | tf_op jit(solution)/shard_map/all_to_all | solution.py:155
  163.2 74.2 %all-to-all-done.1 = bf16[8,128,12,128]{1,3,2,0:T(8,128)(2,1)S(1)} async-done(((bf16[8,128,12,128]{1,3,2,0:T(8,128)(2,1)}), bf16[8,128,12,128]{1,3,2,0:T(8,128)(2,1)S(1)}, u32[]{:S(2)}, u32[]{:S(2)}) %all-to-all-start.1) | async-done | bytes 3145760 | tf_op jit(solution)/shard_map/all_to_all | solution.py:155
  237.4 0.8 multiply_reduce_fusion
  238.2 0.1 divide_convert_fusion
  238.3 0.9 copy.39
  (9 shorter events, 0.1 us)
Async XLA Ops:
  6.5 58.3 %all-gather.3.cloned.1.call-start = ((), (), s32[]{:S(2)}) async-start(), calls=%async_computation.2 | async-start | bytes 6684672 | tf_op jit(solution)/shard_map/all_gather | solution.py:116
  7.3 42.6 %collective-permute-start = (bf16[128,1536]{1,0:T(8,128)(2,1)}, bf16[128,1536]{1,0:T(8,128)(2,1)S(1)}, u32[]{:S(2)}, u32[]{:S(2)}) collective-permute-start(bf16[128,1536]{1,0:T(8,128)(2,1)} %param.6), channel_id=1, source_target_pairs={{0,16},{16,32},{32,48},{48,64},{64,80},{80,96},{96,112},{112,128},... | collective-permute-start | bytes 1179656 | tf_op jit(solution)/shard_map/ppermute | solution.py:20
  11.2 38.7 %collective-permute-start.1 = (bf16[128,1536]{1,0:T(8,128)(2,1)}, bf16[128,1536]{1,0:T(8,128)(2,1)S(1)}, u32[]{:S(2)}, u32[]{:S(2)}) collective-permute-start(bf16[128,1536]{1,0:T(8,128)(2,1)} %param.6), channel_id=1, source_target_pairs={{0,32},{16,48},{32,64},{48,80},{64,96},{80,112},{96,128},{112,144}... | collective-permute-start | bytes 1179656 | tf_op jit(solution)/shard_map/ppermute | solution.py:20
  15.6 36.5 %collective-permute-start.3 = (bf16[128,1536]{1,0:T(8,128)(2,1)}, bf16[128,1536]{1,0:T(8,128)(2,1)S(1)}, u32[]{:S(2)}, u32[]{:S(2)}) collective-permute-start(bf16[128,1536]{1,0:T(8,128)(2,1)} %param.7), channel_id=1, source_target_pairs={{0,32},{16,48},{32,64},{48,80},{64,96},{80,112},{96,128},{112,144}... | collective-permute-start | bytes 1179656 | tf_op jit(solution)/shard_map/ppermute | solution.py:20
  19.0 33.1 %collective-permute-start.2 = (bf16[128,1536]{1,0:T(8,128)(2,1)}, bf16[128,1536]{1,0:T(8,128)(2,1)S(1)}, u32[]{:S(2)}, u32[]{:S(2)}) collective-permute-start(bf16[128,1536]{1,0:T(8,128)(2,1)} %param.7), channel_id=1, source_target_pairs={{0,16},{16,32},{32,48},{48,64},{64,80},{80,96},{96,112},{112,128},... | collective-permute-start | bytes 1179656 | tf_op jit(solution)/shard_map/ppermute | solution.py:20
  130.4 19.5 %collective-permute-start.5 = (bf16[8,128,1536]{1,2,0:T(8,128)(2,1)}, bf16[8,128,1536]{1,2,0:T(8,128)(2,1)}, u32[]{:S(2)}, u32[]{:S(2)}) collective-permute-start(bf16[8,128,1536]{1,2,0:T(8,128)(2,1)} %bitcast.38), channel_id=1, source_target_pairs={{0,1},{1,0},{2,3},{3,2},{4,5},{5,4},{6,7},{7,6},{8,9},{9,8},{10,11... | collective-permute-start | bytes 9437192 | tf_op jit(solution)/shard_map/ppermute | solution.py:143
  137.9 7.6 %collective-permute-start.4 = (f32[8,128,24]{1,0,2:T(8,128)S(1)}, f32[8,128,24]{1,0,2:T(8,128)S(1)}, u32[]{:S(2)}, u32[]{:S(2)}) collective-permute-start(f32[8,128,24]{1,0,2:T(8,128)S(1)} %pad_maximum_fusion.2), channel_id=1, source_target_pairs={{0,1},{1,0},{2,3},{3,2},{4,5},{5,4},{6,7},{7,6},{8,9},{9,8},{10,11... | collective-permute-start | bytes 294920 | tf_op jit(solution)/shard_map/ppermute | solution.py:144
  146.2 11.1 %all-to-all-start = ((f32[8,128,24]{1,2,0:T(8,128)}), f32[8,128,24]{1,2,0:T(8,128)S(1)}, u32[]{:S(2)}, u32[]{:S(2)}) async-start(f32[8,128,24]{1,2,0:T(8,128)} %copy.34), calls=%async_computation | async-start | bytes 196608 | tf_op jit(solution)/shard_map/all_to_all | solution.py:156
  157.3 80.1 %all-to-all-start.1 = ((bf16[8,128,12,128]{1,3,2,0:T(8,128)(2,1)}), bf16[8,128,12,128]{1,3,2,0:T(8,128)(2,1)S(1)}, u32[]{:S(2)}, u32[]{:S(2)}) async-start(bf16[8,128,12,128]{1,3,2,0:T(8,128)(2,1)} %fusion.1), calls=%async_computation.1 | async-start | bytes 6291456 | tf_op jit(solution)/shard_map/all_to_all | solution.py:155
Sparse Core Ops, SparseCore 0:
  9.5 55.3 all-gather.2

commit v3 on v2

v3 whole, which is shorter than its diff:
```python
import math

import jax
import jax.numpy as jnp
from jax import lax
from jax.experimental import pallas as pl
from jax.experimental.pallas import tpu as pltpu
from jax.sharding import PartitionSpec as P

DH = 128


NEG_FILL = -1e30
LAGS = 3
CHUNKS = 3


def passed_along(block, axis, distance):
    devices = range(lax.axis_size(axis))
    route = [(i - distance, i) for i in devices if i - distance in devices]
    return lax.ppermute(block, axis, route)


def class_kernel(info_ref, q_ref, k_ref, v_ref, out_ref, stat_ref):
    cp = pl.program_id(0)
    current = info_ref[0]
    block_len = q_ref.shape[0]
    head_count = q_ref.shape[1] // DH
    early = current <= cp
    lag_a = jnp.where(early, 0, 1)
    start = pl.multiple_of(lag_a * block_len, block_len)
    listed_a = info_ref[2 + cp * LAGS + lag_a] != 0
    listed_b = info_ref[3 + cp * LAGS + lag_a] != 0
    diagonal = current == cp
    reach_a = jnp.where(listed_a, jnp.where(diagonal, 0, block_len), -4 * block_len)
    reach_b = jnp.where(listed_b, block_len, -4 * block_len)
    q_pos = lax.broadcasted_iota(jnp.int32, (block_len, 2 * block_len), 0)
    k_pos = lax.broadcasted_iota(jnp.int32, (block_len, 2 * block_len), 1)
    first = k_pos < block_len
    limit = jnp.where(first, q_pos + reach_a, q_pos + (block_len + reach_b))
    allowed = k_pos <= limit
    scaling = 1.0 / math.sqrt(DH)
    nt = (((1,), (1,)), ((), ()))
    for h in range(head_count):
        cols = slice(h * DH, (h + 1) * DH)
        keys = k_ref[pl.ds(start, 2 * block_len), cols]
        scores = lax.dot_general(q_ref[:, cols], keys, nt, preferred_element_type=jnp.float32)
        scores = jnp.where(allowed, scores * scaling, NEG_FILL)
        highest = jnp.max(scores, axis=1, keepdims=True)
        weights = jnp.where(allowed, jnp.exp(scores - highest), 0.0)
        total = jnp.sum(weights, axis=1, keepdims=True)
        blended = jnp.dot(
            weights.astype(jnp.bfloat16),
            v_ref[pl.ds(start, 2 * block_len), cols],
            preferred_element_type=jnp.float32,
        )
        out_ref[0, 0, :, cols] = blended.astype(jnp.bfloat16)
        stat_ref[0, 0, :, h : h + 1] = highest
        stat_ref[0, 0, :, head_count + h : head_count + h + 1] = total


def class_partials(info, row_q, key_window, value_window, chunk, chips, cores):
    block_len = row_q.shape[0] // (chips * cores)
    width = row_q.shape[1]
    head_count = width // DH

    def out_map(cp, info_ref):
        return (jnp.where(cp % cores == info_ref[1], 0, 1), cp // cores, 0, 0)

    window = (key_window.shape[0], width)
    grid_spec = pltpu.PrefetchScalarGridSpec(
        num_scalar_prefetch=1,
        grid=(chips * cores,),
        in_specs=[
            pl.BlockSpec((block_len, width), lambda cp, info_ref: (cp, 0)),
            pl.BlockSpec(window, lambda cp, info_ref: (0, chunk)),
            pl.BlockSpec(window, lambda cp, info_ref: (0, chunk)),
        ],
        out_specs=[
            pl.BlockSpec((1, 1, block_len, width), out_map),
            pl.BlockSpec((1, 1, block_len, 2 * head_count), out_map),
        ],
    )
    sources = chips * cores
    return pl.pallas_call(
        class_kernel,
        grid_spec=grid_spec,
        out_shape=[
            jax.ShapeDtypeStruct((cores, chips, block_len, width), jnp.bfloat16),
            jax.ShapeDtypeStruct((cores, chips, block_len, 2 * head_count), jnp.float32),
        ],
        cost_estimate=pl.CostEstimate(
            flops=sources * head_count * 2 * 2 * block_len * 2 * block_len * DH,
            transcendentals=sources * head_count * 2 * block_len * block_len,
            bytes_accessed=2 * sources * block_len * width * 2 + 4 * 3 * block_len * width * 2,
        ),
    )(info, row_q, key_window, value_window)


def per_device(queries, keys, values, adjacency, counts):
    block_len, feature_width = queries.shape
    chips = lax.axis_size("z")
    cores = lax.axis_size("core")
    stripe_count = chips * cores
    core = lax.axis_index("core")
    current = lax.axis_index("z") * cores + core
    row_index = lax.axis_index("pb")
    stacked = jnp.stack([keys, values])
    lag_1 = passed_along(stacked, "pb", 1)
    lag_2 = passed_along(stacked, "pb", 2)
    key_window = jnp.concatenate([keys, lag_1[0], lag_2[0]], axis=0)
    value_window = jnp.concatenate([values, lag_1[1], lag_2[1]], axis=0)
    row_table = lax.all_gather(
        jnp.concatenate([adjacency, counts[:, None]], axis=1), ("z", "core"), axis=0, tiled=True
    )
    row_adj, row_cnt = row_table[:, :-1], row_table[:, -1]
    lag_ids = jnp.arange(LAGS, dtype=jnp.int32)
    slot_ids = jnp.arange(adjacency.shape[1], dtype=jnp.int32)
    wanted = (row_index - lag_ids) * stripe_count + current
    listed = (row_adj[:, None, :] == wanted[None, :, None]) & (
        slot_ids[None, None, :] < row_cnt[:, None, None]
    )
    present = jnp.any(listed, axis=2).astype(jnp.int32)
    info = jnp.concatenate(
        [jnp.stack([current, core]).astype(jnp.int32), present.reshape(-1)]
    )

    width = feature_width // CHUNKS
    head_count = width // DH
    swap = [(0, 1), (1, 0)]
    finished = []
    for chunk in range(CHUNKS):
        row_q = lax.all_gather(
            queries[:, chunk * width : (chunk + 1) * width], ("z", "core"), axis=0, tiled=True
        )
        partial_out, stats = class_partials(
            info, row_q, key_window, value_window, chunk, chips, cores
        )
        peer_out = lax.ppermute(partial_out[1], "core", swap)
        peer_stats = lax.ppermute(stats[1], "core", swap)
        own_max, own_tot = stats[0, ..., :head_count], stats[0, ..., head_count:]
        peer_max, peer_tot = peer_stats[..., :head_count], peer_stats[..., head_count:]
        pair_max = jnp.maximum(own_max, peer_max)
        own_f = jnp.exp(own_max - pair_max)
        peer_f = jnp.exp(peer_max - pair_max)
        pair_tot = own_f * own_tot + peer_f * peer_tot
        shape = (chips, block_len, head_count, DH)
        pair_out = (
            own_f[..., None] * partial_out[0].astype(jnp.float32).reshape(shape)
            + peer_f[..., None] * peer_out.astype(jnp.float32).reshape(shape)
        ).astype(jnp.bfloat16)
        pair_out = lax.all_to_all(pair_out, "z", split_axis=0, concat_axis=0, tiled=True)
        pair_stats = lax.all_to_all(
            jnp.concatenate([pair_max, pair_tot], axis=2), "z", split_axis=0, concat_axis=0,
            tiled=True,
        )
        pair_max, pair_tot = pair_stats[..., :head_count], pair_stats[..., head_count:]
        highest = jnp.max(pair_max, axis=0)
        factor = jnp.exp(pair_max - highest[None])
        denominator = jnp.sum(factor * pair_tot, axis=0)
        numerator = jnp.sum(factor[..., None] * pair_out.astype(jnp.float32), axis=0)
        finished.append(
            (numerator / denominator[..., None]).reshape(block_len, width).astype(jnp.bfloat16)
        )
    return jnp.concatenate(finished, axis=1)


def solution(mesh):
    pb, ka = mesh.devices.shape
    grid = jax.sharding.Mesh(mesh.devices.reshape(pb, ka // 2, 2), ("pb", "z", "core"))
    rows = P(("pb", "z", "core"), None)
    in_specs = (rows, rows, rows, rows, P(("pb", "z", "core")))
    return jax.shard_map(
        per_device, mesh=grid, in_specs=in_specs, out_specs=rows, check_vma=False
    )
```

time: 247 us -> 318 us (1.29)
  the two profiles are of different devices: /device:TPU:1 before, /device:TPU:2 now
where the time goes in v3:
time: 318 us; the launch traced here: 315 us
  waiting for transfers between devices  105 us (33%)
  other arithmetic  47.4 us (15%)
  Pallas kernels  47.4 us (15%)
  starting transfers between devices  47 us (15%)
  local copies, waits for them, and re-layouts  31 us (10%)
  blocking collectives  23.2 us (7%)
  between operations  14.1 us (4%)
    pallas_call x3, Pallas kernels, class_partials(): pl.pallas_call(class_kernel, grid_spec=grid_spec, out_shape=[jax.ShapeDty...  47.4 us
    all_gather x3, waiting for transfers between devices, per_device(): lax.all_gather(queries[:, chunk * width:(chunk + 1) * width], ('z', 'core...  44.4 us
    all_to_all x3, waiting for transfers between devices, per_device(): lax.all_to_all(pair_out, 'z', split_axis=0, concat_axis=0, tiled=True)  43.6 us
    all_gather x1, blocking collectives, per_device(): lax.all_gather(jnp.concatenate([adjacency, counts[:, None]], axis=1), ('z...  23.2 us
    convert_element_type x3, other arithmetic, per_device(): pair_out = (own_f[..., None] * partial_out[0].astype(jnp.float32).reshape...  17.7 us
    all_to_all x3, starting transfers between devices, per_device(): lax.all_to_all(jnp.concatenate([pair_max, pair_tot], axis=2), 'z', split_...  14.7 us
    all_to_all x3, starting transfers between devices, per_device(): lax.all_to_all(pair_out, 'z', split_axis=0, concat_axis=0, tiled=True)  13.1 us
    add x3, other arithmetic, per_device(): pair_tot = own_f * own_tot + peer_f * peer_tot  9.13 us
  transfers between devices with their start and end apart: 17, of which 10 were waited for; matrix products, arithmetic and copies ran while one was open for 24% of the time, Pallas kernels for 15%

profile of v3, /device:TPU:2, one launch (start us, length us, event | category | flops | bytes accessed | tf_op | source)
XLA Modules:
  0.0 314.9 jit_solution(6962603837736543012)
XLA Ops:
  6.5 1.8 fusion.12
  8.4 0.7 all-gather.7.cloned.1.call-update
  9.2 0.7 all-gather.5.cloned.1.call-update
  9.9 1.3 pad_maximum_fusion.2
  11.1 4.1 %collective-permute-start.1 = (bf16[2,128,1536]{2,1,0:T(8,128)(2,1)S(1)}, bf16[2,128,1536]{2,1,0:T(8,128)(2,1)S(1)}, u32[]{:S(2)}, u32[]{:S(2)}) collective-permute-start(bf16[2,128,1536]{2,1,0:T(8,128)(2,1)S(1)} %pad_maximum_fusion.2), channel_id=1, source_target_pairs={{0,32},{16,48},{32,64},{48,80},{64,96},{80,112},{96,128},{112,144}... | collective-permute-start | bytes 2359304 | tf_op jit(solution)/shard_map/ppermute | solution.py:21
  15.2 2.7 collective-permute-start
  18.7 23.2 %all-gather = s32[16,1,25]{2,1,0:T(1,128)S(1)} all-gather(s32[1,1,25]{2,1,0:T(1,128)S(1)} %add_bitcast_fusion), channel_id=1, replica_groups=mesh['pb'=32,'z'=8,'core'=2] {'z','core'}, dimensions={0}, use_global_device_ids=true | all-gather | bytes 1700 | tf_op jit(solution)/shard_map/all_gather | solution.py:113
  43.2 7.6 %collective-permute-done = bf16[2,128,1536]{2,1,0:T(8,128)(2,1)S(1)} collective-permute-done((bf16[2,128,1536]{2,1,0:T(8,128)(2,1)S(1)}, bf16[2,128,1536]{2,1,0:T(8,128)(2,1)S(1)}, u32[]{:S(2)}, u32[]{:S(2)}) %collective-permute-start) | collective-permute-done | bytes 786464 | tf_op jit(solution)/shard_map/ppermute | solution.py:21
  50.8 1.6 pad_maximum_fusion
  52.4 4.6 %all-gather.9.cloned.1.call-done.q_ref = bf16[2048,512]{1,0:T(8,128)(2,1)} async-done(((bf16[128,512]{1,0:T(8,128)(2,1)}), bf16[2048,512]{1,0:T(8,128)(2,1)}) %all-gather.9.cloned.1.call-update) | async-done | bytes 2097168 | tf_op jit(solution)/shard_map/all_gather | solution.py:133
  57.0 15.8 %shard_map.57 = (bf16[2,8,128,512]{3,2,1,0:T(8,128)(2,1)}, f32[2,8,128,8]{3,2,1,0:T(8,128)}) custom-call(s32[50]{0:T(128)} %pad_add_fusion.info_ref, bf16[2048,512]{1,0:T(8,128)(2,1)} %all-gather.9.cloned.1.call-done.q_ref, bf16[384,1536]{1,0:T(8,128)(2,1)} %get-tuple-element.48.k_ref, bf16[384,1536]{1,0:T(8,128)(2,1)} %get-tuple-element.49.v_ref), custom_call_target="tpu_custom_call" | custom-call | flops 1073741824 | bytes 5767168 | tf_op jit(solution)/shard_map/pallas_call | solution.py:85
  72.8 3.5 %slice_convert_fusion = (f32[1,8,128,512]{3,2,1,0:T(8,128)}, bf16[8,128,512]{2,1,0:T(8,128)(2,1)}) fusion(bf16[2,8,128,512]{3,2,1,0:T(8,128)(2,1)} %get-tuple-element.16), kind=kLoop, calls=%fused_computation.9 | loop fusion | flops 524288 | bytes 5242880 | tf_op jit(solution)/shard_map/convert_element_type | solution.py:149
  76.3 2.1 collective-permute-start.7
  78.5 2.0 reshape.107
  80.5 0.8 slice_bitcast_fusion.3
  81.4 2.2 collective-permute-start.6
  83.6 16.3 %all-gather.7.cloned.1.call-done.q_ref = bf16[2048,512]{1,0:T(8,128)(2,1)} async-done(((bf16[128,512]{1,0:T(8,128)(2,1)}), bf16[2048,512]{1,0:T(8,128)(2,1)}) %all-gather.7.cloned.1.call-update) | async-done | bytes 2097168 | tf_op jit(solution)/shard_map/all_gather | solution.py:133
  99.9 15.8 %shard_map.56 = (bf16[2,8,128,512]{3,2,1,0:T(8,128)(2,1)}, f32[2,8,128,8]{3,2,1,0:T(8,128)}) custom-call(s32[50]{0:T(128)} %pad_add_fusion.info_ref, bf16[2048,512]{1,0:T(8,128)(2,1)} %all-gather.7.cloned.1.call-done.q_ref, bf16[384,1536]{1,0:T(8,128)(2,1)} %get-tuple-element.48.k_ref, bf16[384,1536]{1,0:T(8,128)(2,1)} %get-tuple-element.49.v_ref), custom_call_target="tpu_custom_call" | custom-call | flops 1073741824 | bytes 5767168 | tf_op jit(solution)/shard_map/pallas_call | solution.py:85
  115.7 1.9 slice_bitcast_fusion.4
  117.6 2.1 collective-permute-start.4
  119.7 23.5 %all-gather.5.cloned.1.call-done.q_ref = bf16[2048,512]{1,0:T(8,128)(2,1)} async-done(((bf16[128,512]{1,0:T(8,128)(2,1)}), bf16[2048,512]{1,0:T(8,128)(2,1)}) %all-gather.5.cloned.1.call-update) | async-done | bytes 2097168 | tf_op jit(solution)/shard_map/all_gather | solution.py:133
  143.1 15.8 %shard_map.55 = (bf16[2,8,128,512]{3,2,1,0:T(8,128)(2,1)}, f32[2,8,128,8]{3,2,1,0:T(8,128)}) custom-call(s32[50]{0:T(128)} %pad_add_fusion.info_ref, bf16[2048,512]{1,0:T(8,128)(2,1)} %all-gather.5.cloned.1.call-done.q_ref, bf16[384,1536]{1,0:T(8,128)(2,1)} %get-tuple-element.48.k_ref, bf16[384,1536]{1,0:T(8,128)(2,1)} %get-tuple-element.49.v_ref), custom_call_target="tpu_custom_call" | custom-call | flops 1073741824 | bytes 5767168 | tf_op jit(solution)/shard_map/pallas_call | solution.py:85
  158.9 1.9 slice_bitcast_fusion.5
  160.8 2.1 collective-permute-start.2
  162.9 3.0 fusion
  165.9 1.2 copy.50
  167.1 1.2 copy.49
  168.4 0.6 pad_maximum_fusion.6
  169.0 4.1 %all-to-all-start.4 = ((f32[8,128,8]{1,2,0:T(8,128)}), f32[8,128,8]{1,2,0:T(8,128)S(1)}, u32[]{:S(2)}, u32[]{:S(2)}) async-start(f32[8,128,8]{1,2,0:T(8,128)} %pad_maximum_fusion.6), calls=%async_computation.4 | async-start | bytes 65536 | tf_op jit(solution)/shard_map/all_to_all | solution.py:153
  173.1 3.3 %fusion.1 = (f32[8,128,4]{2,1,0:T(8,128)}, f32[8,128,4]{2,1,0:T(8,128)}, f32[8,128,4]{2,1,0:T(8,128)}, f32[8,128,4]{2,1,0:T(8,128)}) fusion(f32[8,128,8]{2,1,0:T(8,128)} %collective-permute-done.4, f32[2,8,128,8]{3,2,1,0:T(8,128)} %get-tuple-element.13), kind=kLoop, calls=%fused_computation.18 | loop fusion | flops 24576 | bytes 131072 | tf_op jit(solution)/shard_map/add | solution.py:146
  176.4 1.2 copy.46
  177.7 1.2 copy.45
  178.9 2.9 fusion.2
  181.8 1.2 copy.42
  183.0 1.3 copy.41
  185.0 7.2 %all-to-all-start.2 = ((f32[8,128,8]{1,2,0:T(8,128)}), f32[8,128,8]{1,2,0:T(8,128)S(1)}, u32[]{:S(2)}, u32[]{:S(2)}) async-start(f32[8,128,8]{1,2,0:T(8,128)} %pad_maximum_fusion.5), calls=%async_computation.2 | async-start | bytes 65536 | tf_op jit(solution)/shard_map/all_to_all | solution.py:153
  192.8 2.7 reshape.109
  195.5 4.7 %all-to-all-done.2 = f32[8,128,8]{1,2,0:T(8,128)S(1)} async-done(((f32[8,128,8]{1,2,0:T(8,128)}), f32[8,128,8]{1,2,0:T(8,128)S(1)}, u32[]{:S(2)}, u32[]{:S(2)}) %all-to-all-start.2) | async-done | bytes 32800 | tf_op jit(solution)/shard_map/all_to_all | solution.py:153
  200.2 3.3 %all-to-all-start = ((f32[8,128,8]{1,2,0:T(8,128)}), f32[8,128,8]{1,2,0:T(8,128)S(1)}, u32[]{:S(2)}, u32[]{:S(2)}) async-start(f32[8,128,8]{1,2,0:T(8,128)} %pad_maximum_fusion.4), calls=%async_computation | async-start | bytes 65536 | tf_op jit(solution)/shard_map/all_to_all | solution.py:153
  203.6 5.8 %add_convert_fusion = bf16[8,128,4,128]{3,2,1,0:T(4,128)(2,1)} fusion(f32[8,128,4,128]{3,2,1,0:T(4,128)} %reshape.109, f32[8,128,4,128]{3,2,1,0:T(4,128)S(1)} %reshape.107, f32[8,128,4]{2,1,0:T(8,128)S(1)} %copy-done.7, f32[8,128,4]{2,1,0:T(8,128)S(1)} %copy-done.6), kind=kLoop, calls=%fused_computation.1 | loop fusion | flops 2097152 | bytes 5275648 | tf_op jit(solution)/shard_map/convert_element_type | solution.py:151
  209.3 2.2 all-to-all-done
  211.5 5.1 %all-to-all-start.5 = ((bf16[8,128,4,128]{3,2,1,0:T(4,128)(2,1)}), bf16[8,128,4,128]{3,2,1,0:T(4,128)(2,1)S(1)}, u32[]{:S(2)}, u32[]{:S(2)}) async-start(bf16[8,128,4,128]{3,2,1,0:T(4,128)(2,1)} %add_convert_fusion), calls=%async_computation.5 | async-start | bytes 2097152 | tf_op jit(solution)/shard_map/all_to_all | solution.py:152
  216.6 2.0 slice_convert_fusion.1
  218.6 1.9 collective-permute-start.5
  220.5 1.9 reshape.104
  222.4 1.0 collective-permute-done.5
  223.5 2.7 reshape.106
  226.1 5.9 %add_convert_fusion.1 = bf16[8,128,4,128]{3,2,1,0:T(4,128)(2,1)} fusion(f32[8,128,4,128]{3,2,1,0:T(4,128)} %reshape.106, f32[8,128,4,128]{3,2,1,0:T(4,128)S(1)} %reshape.104, f32[8,128,4]{2,1,0:T(8,128)} %get-tuple-element.27, f32[8,128,4]{2,1,0:T(8,128)} %get-tuple-element.26), kind=kLoop, calls=%fused_computation.3 | loop fusion | flops 2097152 | bytes 5275648 | tf_op jit(solution)/shard_map/convert_element_type | solution.py:151
  232.1 11.4 %all-to-all-done.5 = bf16[8,128,4,128]{3,2,1,0:T(4,128)(2,1)S(1)} async-done(((bf16[8,128,4,128]{3,2,1,0:T(4,128)(2,1)}), bf16[8,128,4,128]{3,2,1,0:T(4,128)(2,1)S(1)}, u32[]{:S(2)}, u32[]{:S(2)}) %all-to-all-start.5) | async-done | bytes 1048608 | tf_op jit(solution)/shard_map/all_to_all | solution.py:152
  243.5 4.2 %all-to-all-start.3 = ((bf16[8,128,4,128]{3,2,1,0:T(4,128)(2,1)}), bf16[8,128,4,128]{3,2,1,0:T(4,128)(2,1)}, u32[]{:S(2)}, u32[]{:S(2)}) async-start(bf16[8,128,4,128]{3,2,1,0:T(4,128)(2,1)} %add_convert_fusion.1), calls=%async_computation.3 | async-start | bytes 2097152 | tf_op jit(solution)/shard_map/all_to_all | solution.py:152
  247.8 2.0 slice_convert_fusion.2
  249.7 1.9 collective-permute-start.3
  251.6 1.9 reshape.101
  253.6 1.0 copy.51
  254.8 2.7 reshape.103
  257.5 6.0 %add_convert_fusion.2 = bf16[8,128,4,128]{3,2,1,0:T(4,128)(2,1)} fusion(f32[8,128,4,128]{3,2,1,0:T(4,128)} %reshape.103, f32[8,128,4,128]{3,2,1,0:T(4,128)S(1)} %reshape.101, f32[8,128,4]{2,1,0:T(8,128)} %get-tuple-element.21, f32[8,128,4]{2,1,0:T(8,128)} %get-tuple-element.20), kind=kLoop, calls=%fused_computation.5 | loop fusion | flops 2097152 | bytes 5275648 | tf_op jit(solution)/shard_map/convert_element_type | solution.py:151
  263.4 11.5 %all-to-all-done.3 = bf16[8,128,4,128]{3,2,1,0:T(4,128)(2,1)} async-done(((bf16[8,128,4,128]{3,2,1,0:T(4,128)(2,1)}), bf16[8,128,4,128]{3,2,1,0:T(4,128)(2,1)}, u32[]{:S(2)}, u32[]{:S(2)}) %all-to-all-start.3) | async-done | bytes 1048608 | tf_op jit(solution)/shard_map/all_to_all | solution.py:152
  274.9 3.7 %all-to-all-start.1 = ((bf16[8,128,4,128]{3,2,1,0:T(4,128)(2,1)}), bf16[8,128,4,128]{3,2,1,0:T(4,128)(2,1)S(1)}, u32[]{:S(2)}, u32[]{:S(2)}) async-start(bf16[8,128,4,128]{3,2,1,0:T(4,128)(2,1)} %add_convert_fusion.2), calls=%async_computation.1 | async-start | bytes 2097152 | tf_op jit(solution)/shard_map/all_to_all | solution.py:152
  278.7 1.0 copy.47
  280.3 1.4 multiply_reduce_fusion
  281.9 2.9 multiply_reduce_fusion.1
  285.1 20.8 %all-to-all-done.1 = bf16[8,128,4,128]{3,2,1,0:T(4,128)(2,1)S(1)} async-done(((bf16[8,128,4,128]{3,2,1,0:T(4,128)(2,1)}), bf16[8,128,4,128]{3,2,1,0:T(4,128)(2,1)S(1)}, u32[]{:S(2)}, u32[]{:S(2)}) %all-to-all-start.1) | async-done | bytes 1048608 | tf_op jit(solution)/shard_map/all_to_all | solution.py:152
  305.9 1.4 multiply_reduce_fusion.2
  307.6 0.8 pad_maximum_fusion.3
  (62 shorter events, 4.2 us)
Async XLA Ops:
  6.5 12.1 %copy-start.10 = (s32[1,24]{1,0:T(1,128)S(1)}, s32[1,24]{1,0:T(1,128)}, u32[]{:S(2)}) copy-start(s32[1,24]{1,0:T(1,128)} %param.8) | copy-start | bytes 292
  6.5 50.5 %all-gather.9.cloned.1.call-start = ((), (), s32[]{:S(2)}) async-start(), calls=%async_computation.8 | async-start | bytes 2228224 | tf_op jit(solution)/shard_map/all_gather | solution.py:133
  8.4 91.6 %all-gather.7.cloned.1.call-start = ((), (), s32[]{:S(2)}) async-start(), calls=%async_computation.7 | async-start | bytes 2228224 | tf_op jit(solution)/shard_map/all_gather | solution.py:133
  9.1 134.0 %all-gather.5.cloned.1.call-start = ((), (), s32[]{:S(2)}) async-start(), calls=%async_computation.6 | async-start | bytes 2228224 | tf_op jit(solution)/shard_map/all_gather | solution.py:133
  9.8 40.9 %copy-start.8 = (bf16[128,1536]{1,0:T(8,128)(2,1)S(1)}, bf16[128,1536]{1,0:T(8,128)(2,1)}, u32[]{:S(2)}) copy-start(bf16[128,1536]{1,0:T(8,128)(2,1)} %param.7) | copy-start | bytes 1179652
  9.9 40.9 %copy-start.9 = (bf16[128,1536]{1,0:T(8,128)(2,1)S(1)}, bf16[128,1536]{1,0:T(8,128)(2,1)}, u32[]{:S(2)}) copy-start(bf16[128,1536]{1,0:T(8,128)(2,1)} %param.6) | copy-start | bytes 1179652
  11.1 32.0 %collective-permute-start.1 = (bf16[2,128,1536]{2,1,0:T(8,128)(2,1)S(1)}, bf16[2,128,1536]{2,1,0:T(8,128)(2,1)S(1)}, u32[]{:S(2)}, u32[]{:S(2)}) collective-permute-start(bf16[2,128,1536]{2,1,0:T(8,128)(2,1)S(1)} %pad_maximum_fusion.2), channel_id=1, source_target_pairs={{0,32},{16,48},{32,64},{48,80},{64,96},{80,112},{96,128},{112,144}... | collective-permute-start | bytes 2359304 | tf_op jit(solution)/shard_map/ppermute | solution.py:21
  15.2 35.5 %collective-permute-start = (bf16[2,128,1536]{2,1,0:T(8,128)(2,1)S(1)}, bf16[2,128,1536]{2,1,0:T(8,128)(2,1)S(1)}, u32[]{:S(2)}, u32[]{:S(2)}) collective-permute-start(bf16[2,128,1536]{2,1,0:T(8,128)(2,1)S(1)} %pad_maximum_fusion.2), channel_id=1, source_target_pairs={{0,16},{16,32},{32,48},{48,64},{64,80},{80,96},{96,112},{112,128},... | collective-permute-start | bytes 2359304 | tf_op jit(solution)/shard_map/ppermute | solution.py:21
  76.3 116.5 %collective-permute-start.7 = (bf16[8,128,512]{2,1,0:T(8,128)(2,1)}, bf16[8,128,512]{2,1,0:T(8,128)(2,1)}, u32[]{:S(2)}, u32[]{:S(2)}) collective-permute-start(bf16[8,128,512]{2,1,0:T(8,128)(2,1)} %get-tuple-element.40), channel_id=1, source_target_pairs={{0,1},{1,0},{2,3},{3,2},{4,5},{5,4},{6,7},{7,6},{8,9},{9,8},{10,11... | collective-permute-start | bytes 3145736 | tf_op jit(solution)/shard_map/ppermute | solution.py:139
  78.5 2.0 copy-start.1
  81.4 81.6 %collective-permute-start.6 = (f32[8,128,8]{2,1,0:T(8,128)}, f32[8,128,8]{2,1,0:T(8,128)}, u32[]{:S(2)}, u32[]{:S(2)}) collective-permute-start(f32[8,128,8]{2,1,0:T(8,128)} %slice_bitcast_fusion.3), channel_id=1, source_target_pairs={{0,1},{1,0},{2,3},{3,2},{4,5},{5,4},{6,7},{7,6},{8,9},{9,8},{10,11... | collective-permute-start | bytes 98312 | tf_op jit(solution)/shard_map/ppermute | solution.py:140
  117.6 55.6 %collective-permute-start.4 = (f32[8,128,8]{2,1,0:T(8,128)}, f32[8,128,8]{2,1,0:T(8,128)}, u32[]{:S(2)}, u32[]{:S(2)}) collective-permute-start(f32[8,128,8]{2,1,0:T(8,128)} %slice_bitcast_fusion.4), channel_id=1, source_target_pairs={{0,1},{1,0},{2,3},{3,2},{4,5},{5,4},{6,7},{7,6},{8,9},{9,8},{10,11... | collective-permute-start | bytes 98312 | tf_op jit(solution)/shard_map/ppermute | solution.py:140
  160.8 18.1 %collective-permute-start.2 = (f32[8,128,8]{2,1,0:T(8,128)}, f32[8,128,8]{2,1,0:T(8,128)}, u32[]{:S(2)}, u32[]{:S(2)}) collective-permute-start(f32[8,128,8]{2,1,0:T(8,128)} %slice_bitcast_fusion.5), channel_id=1, source_target_pairs={{0,1},{1,0},{2,3},{3,2},{4,5},{5,4},{6,7},{7,6},{8,9},{9,8},{10,11... | collective-permute-start | bytes 98312 | tf_op jit(solution)/shard_map/ppermute | solution.py:140
  169.0 16.0 %all-to-all-start.4 = ((f32[8,128,8]{1,2,0:T(8,128)}), f32[8,128,8]{1,2,0:T(8,128)S(1)}, u32[]{:S(2)}, u32[]{:S(2)}) async-start(f32[8,128,8]{1,2,0:T(8,128)} %pad_maximum_fusion.6), calls=%async_computation.4 | async-start | bytes 65536 | tf_op jit(solution)/shard_map/all_to_all | solution.py:153
  173.1 5.8 %copy-start = (f32[2,8,128,8]{3,2,1,0:T(8,128)S(1)}, f32[2,8,128,8]{3,2,1,0:T(8,128)}, u32[]{:S(2)}) copy-start(f32[2,8,128,8]{3,2,1,0:T(8,128)} %get-tuple-element.11) | copy-start | bytes 196612
  183.0 20.5 %copy-start.6 = (f32[8,128,4]{2,1,0:T(8,128)S(1)}, f32[8,128,4]{2,1,0:T(8,128)}, u32[]{:S(2)}) copy-start(f32[8,128,4]{2,1,0:T(8,128)} %get-tuple-element.32) | copy-start | bytes 49156
  183.0 20.5 %copy-start.7 = (f32[8,128,4]{2,1,0:T(8,128)S(1)}, f32[8,128,4]{2,1,0:T(8,128)}, u32[]{:S(2)}) copy-start(f32[8,128,4]{2,1,0:T(8,128)} %get-tuple-element.33) | copy-start | bytes 49156
  185.0 15.2 %all-to-all-start.2 = ((f32[8,128,8]{1,2,0:T(8,128)}), f32[8,128,8]{1,2,0:T(8,128)S(1)}, u32[]{:S(2)}, u32[]{:S(2)}) async-start(f32[8,128,8]{1,2,0:T(8,128)} %pad_maximum_fusion.5), calls=%async_computation.2 | async-start | bytes 65536 | tf_op jit(solution)/shard_map/all_to_all | solution.py:153
  200.2 11.3 %all-to-all-start = ((f32[8,128,8]{1,2,0:T(8,128)}), f32[8,128,8]{1,2,0:T(8,128)S(1)}, u32[]{:S(2)}, u32[]{:S(2)}) async-start(f32[8,128,8]{1,2,0:T(8,128)} %pad_maximum_fusion.4), calls=%async_computation | async-start | bytes 65536 | tf_op jit(solution)/shard_map/all_to_all | solution.py:153
  209.3 7.3 %copy-start.5 = (bf16[2,8,128,512]{3,2,1,0:T(8,128)(2,1)S(1)}, bf16[2,8,128,512]{3,2,1,0:T(8,128)(2,1)}, u32[]{:S(2)}) copy-start(bf16[2,8,128,512]{3,2,1,0:T(8,128)(2,1)} %get-tuple-element.14) | copy-start | bytes 6291460
  211.5 32.0 %all-to-all-start.5 = ((bf16[8,128,4,128]{3,2,1,0:T(4,128)(2,1)}), bf16[8,128,4,128]{3,2,1,0:T(4,128)(2,1)S(1)}, u32[]{:S(2)}, u32[]{:S(2)}) async-start(bf16[8,128,4,128]{3,2,1,0:T(4,128)(2,1)} %add_convert_fusion), calls=%async_computation.5 | async-start | bytes 2097152 | tf_op jit(solution)/shard_map/all_to_all | solution.py:152
  218.6 4.9 %collective-permute-start.5 = (bf16[8,128,512]{2,1,0:T(8,128)(2,1)}, bf16[8,128,512]{2,1,0:T(8,128)(2,1)}, u32[]{:S(2)}, u32[]{:S(2)}) collective-permute-start(bf16[8,128,512]{2,1,0:T(8,128)(2,1)} %get-tuple-element.38), channel_id=1, source_target_pairs={{0,1},{1,0},{2,3},{3,2},{4,5},{5,4},{6,7},{7,6},{8,9},{9,8},{10,11... | collective-permute-start | bytes 3145736 | tf_op jit(solution)/shard_map/ppermute | solution.py:139
  232.1 15.7 %copy-start.4 = (bf16[2,8,128,512]{3,2,1,0:T(8,128)(2,1)S(1)}, bf16[2,8,128,512]{3,2,1,0:T(8,128)(2,1)}, u32[]{:S(2)}) copy-start(bf16[2,8,128,512]{3,2,1,0:T(8,128)(2,1)} %get-tuple-element.12) | copy-start | bytes 6291460
  243.5 31.4 %all-to-all-start.3 = ((bf16[8,128,4,128]{3,2,1,0:T(4,128)(2,1)}), bf16[8,128,4,128]{3,2,1,0:T(4,128)(2,1)}, u32[]{:S(2)}, u32[]{:S(2)}) async-start(bf16[8,128,4,128]{3,2,1,0:T(4,128)(2,1)} %add_convert_fusion.1), calls=%async_computation.3 | async-start | bytes 2097152 | tf_op jit(solution)/shard_map/all_to_all | solution.py:152
  249.7 5.1 %collective-permute-start.3 = (bf16[8,128,512]{2,1,0:T(8,128)(2,1)}, bf16[8,128,512]{2,1,0:T(8,128)(2,1)}, u32[]{:S(2)}, u32[]{:S(2)}) collective-permute-start(bf16[8,128,512]{2,1,0:T(8,128)(2,1)} %get-tuple-element.36), channel_id=1, source_target_pairs={{0,1},{1,0},{2,3},{3,2},{4,5},{5,4},{6,7},{7,6},{8,9},{9,8},{10,11... | collective-permute-start | bytes 3145736 | tf_op jit(solution)/shard_map/ppermute | solution.py:139
  263.4 16.8 %copy-start.2 = (f32[8,128,4]{2,1,0:T(8,128)S(1)}, f32[8,128,4]{2,1,0:T(8,128)}, u32[]{:S(2)}) copy-start(f32[8,128,4]{2,1,0:T(8,128)} %copy.51) | copy-start | bytes 49156
  274.9 31.0 %all-to-all-start.1 = ((bf16[8,128,4,128]{3,2,1,0:T(4,128)(2,1)}), bf16[8,128,4,128]{3,2,1,0:T(4,128)(2,1)S(1)}, u32[]{:S(2)}, u32[]{:S(2)}) async-start(bf16[8,128,4,128]{3,2,1,0:T(4,128)(2,1)} %add_convert_fusion.2), calls=%async_computation.1 | async-start | bytes 2097152 | tf_op jit(solution)/shard_map/all_to_all | solution.py:152
  280.3 1.7 copy-start.3
Sparse Core Ops, SparseCore 0:
  9.4 47.5 all-gather.8
  59.1 40.7 all-gather.6
  102.0 41.0 all-gather.4

commit v4 on v2

v4 whole, which is shorter than its diff:
```python
import math

import jax
import jax.numpy as jnp
from jax import lax
from jax.experimental import pallas as pl
from jax.experimental.pallas import tpu as pltpu
from jax.sharding import PartitionSpec as P

DH = 128


NEG_FILL = -1e30
LAGS = 3
AXES = ("pb", "z", "core")


def pair_kernel(info_ref, q_ref, k_ref, v_ref, out_ref, stat_ref):
    t = pl.program_id(0)
    chip = info_ref[0]
    core = info_ref[1]
    block_len = out_ref.shape[0]
    head_count = out_ref.shape[1] // DH
    column = 2 * t + core
    q_pos = lax.broadcasted_iota(jnp.int32, (block_len, 2 * block_len), 0)
    k_pos = lax.broadcasted_iota(jnp.int32, (block_len, 2 * block_len), 1)
    first = k_pos < block_len
    starts = []
    masks = []
    for j in range(2):
        key_class = 2 * chip + (core + j) % 2
        lag_a = jnp.where(key_class <= column, 0, 1)
        base = 2 + (t * 2 + j) * LAGS + lag_a
        listed_a = info_ref[base] != 0
        listed_b = info_ref[base + 1] != 0
        diagonal = key_class == column
        reach_a = jnp.where(listed_a, jnp.where(diagonal, 0, block_len), -4 * block_len)
        reach_b = jnp.where(listed_b, block_len, -4 * block_len)
        limit = jnp.where(first, q_pos + reach_a, q_pos + (block_len + reach_b))
        masks.append(k_pos <= limit)
        starts.append(pl.multiple_of(lag_a * block_len, block_len))
    scaling = 1.0 / math.sqrt(DH)
    nt = (((1,), (1,)), ((), ()))
    for h in range(head_count):
        cols = slice(h * DH, (h + 1) * DH)
        q = q_ref[:, cols]
        scores = []
        for j in range(2):
            keys = k_ref[j, pl.ds(starts[j], 2 * block_len), cols]
            s = lax.dot_general(q, keys, nt, preferred_element_type=jnp.float32)
            scores.append(jnp.where(masks[j], s * scaling, NEG_FILL))
        highest = jnp.maximum(
            jnp.max(scores[0], axis=1, keepdims=True), jnp.max(scores[1], axis=1, keepdims=True)
        )
        total = None
        blended = None
        for j in range(2):
            w = jnp.where(masks[j], jnp.exp(scores[j] - highest), 0.0)
            part_total = jnp.sum(w, axis=1, keepdims=True)
            part = jnp.dot(
                w.astype(jnp.bfloat16),
                v_ref[j, pl.ds(starts[j], 2 * block_len), cols],
                preferred_element_type=jnp.float32,
            )
            total = part_total if total is None else total + part_total
            blended = part if blended is None else blended + part
        out_ref[:, cols] = blended.astype(jnp.bfloat16)
        stat_ref[0, :, h : h + 1] = highest
        stat_ref[0, :, head_count + h : head_count + h + 1] = total


def pair_partials(info, row_q, key_window, value_window, feature_width):
    block_len = key_window.shape[1] // LAGS
    sources = row_q.shape[0] // block_len
    head_count = feature_width // DH
    grid_spec = pltpu.PrefetchScalarGridSpec(
        num_scalar_prefetch=1,
        grid=(sources,),
        in_specs=[
            pl.BlockSpec((block_len, row_q.shape[1]), lambda t, info_ref: (t, 0)),
            pl.BlockSpec(key_window.shape, lambda t, info_ref: (0, 0, 0)),
            pl.BlockSpec(value_window.shape, lambda t, info_ref: (0, 0, 0)),
        ],
        out_specs=[
            pl.BlockSpec((block_len, feature_width), lambda t, info_ref: (t, 0)),
            pl.BlockSpec((1, block_len, 2 * head_count), lambda t, info_ref: (t, 0, 0)),
        ],
    )
    return pl.pallas_call(
        pair_kernel,
        grid_spec=grid_spec,
        out_shape=[
            jax.ShapeDtypeStruct((sources * block_len, feature_width), jnp.bfloat16),
            jax.ShapeDtypeStruct((sources, block_len, 2 * head_count), jnp.float32),
        ],
        cost_estimate=pl.CostEstimate(
            flops=sources * head_count * 2 * 2 * 2 * block_len * 2 * block_len * DH,
            transcendentals=sources * head_count * 2 * 2 * block_len * block_len,
            bytes_accessed=2 * sources * block_len * feature_width * 2
            + 2 * 2 * LAGS * block_len * feature_width * 2,
        ),
    )(info, row_q, key_window, value_window)


def per_device(queries, keys, values, adjacency, counts):
    block_len, feature_width = queries.shape
    head_count = feature_width // DH
    rows = lax.axis_size("pb")
    chips = lax.axis_size("z")
    cores = lax.axis_size("core")
    stripe_count = chips * cores
    chip = lax.axis_index("z")
    core = lax.axis_index("core")
    row_index = lax.axis_index("pb")

    stacked = jnp.stack([keys, values])

    def fetched(lag, flip):
        route = []
        for dst in range(rows * stripe_count):
            src_row = dst // stripe_count - lag
            if src_row >= 0:
                route.append((src_row * stripe_count + ((dst % stripe_count) ^ flip), dst))
        return lax.ppermute(stacked, AXES, route)

    own = [stacked, fetched(1, 0), fetched(2, 0)]
    partner = [fetched(0, 1), fetched(1, 1), fetched(2, 1)]
    key_window = jnp.stack(
        [jnp.concatenate([x[0] for x in own]), jnp.concatenate([x[0] for x in partner])]
    )
    value_window = jnp.stack(
        [jnp.concatenate([x[1] for x in own]), jnp.concatenate([x[1] for x in partner])]
    )

    lag_ids = jnp.arange(LAGS, dtype=jnp.int32)
    class_ids = jnp.arange(stripe_count, dtype=jnp.int32)
    slot_ids = jnp.arange(adjacency.shape[1], dtype=jnp.int32)
    wanted = (row_index - lag_ids[None, :]) * stripe_count + class_ids[:, None]
    listed = (adjacency[0][None, None, :] == wanted[:, :, None]) & (
        slot_ids[None, None, :] < counts[0]
    )
    marks = jnp.any(listed, axis=2).reshape(1, -1).astype(jnp.bfloat16)
    spare = jnp.zeros((block_len, DH), jnp.bfloat16)
    spare = lax.dynamic_update_slice(spare, marks, (0, 0))
    row_q = lax.all_gather(
        jnp.concatenate([queries, spare], axis=1), "z", axis=0, tiled=True
    )
    marks_all = row_q.reshape(chips, block_len, -1)[:, 0, feature_width : feature_width + stripe_count * LAGS]
    marks_all = marks_all.reshape(chips, stripe_count, LAGS).astype(jnp.int32)
    mine = [
        lax.dynamic_index_in_dim(marks_all, 2 * chip + (core + j) % 2, axis=1, keepdims=False)
        for j in range(2)
    ]
    info = jnp.concatenate(
        [jnp.stack([chip, core]).astype(jnp.int32), jnp.stack(mine, axis=1).reshape(-1)]
    )

    pair_out, pair_stats = pair_partials(info, row_q, key_window, value_window, feature_width)
    pair_out = lax.all_to_all(
        pair_out.reshape(chips, block_len, head_count, DH), "z", split_axis=0, concat_axis=0,
        tiled=True,
    )
    pair_stats = lax.all_to_all(pair_stats, "z", split_axis=0, concat_axis=0, tiled=True)
    pair_max, pair_tot = pair_stats[..., :head_count], pair_stats[..., head_count:]
    highest = jnp.max(pair_max, axis=0)
    factor = jnp.exp(pair_max - highest[None])
    denominator = jnp.sum(factor * pair_tot, axis=0)
    numerator = jnp.sum(factor[..., None] * pair_out.astype(jnp.float32), axis=0)
    return (
        (numerator / denominator[..., None]).reshape(block_len, feature_width).astype(jnp.bfloat16)
    )


def solution(mesh):
    pb, ka = mesh.devices.shape
    grid = jax.sharding.Mesh(mesh.devices.reshape(pb, ka // 2, 2), AXES)
    rows = P(AXES, None)
    in_specs = (rows, rows, rows, rows, P(AXES))
    return jax.shard_map(
        per_device, mesh=grid, in_specs=in_specs, out_specs=rows, check_vma=False
    )
```

time: 247 us -> 243 us (0.984)
  the two profiles are of different devices: /device:TPU:1 before, /device:TPU:32 now
where the time goes in v4:
time: 243 us; the launch traced here: 242 us
  waiting for transfers between devices  133 us (55%)
  starting transfers between devices  33.2 us (14%)
  Pallas kernels  32.1 us (13%)
  local copies, waits for them, and re-layouts  20 us (8%)
  between operations  14.3 us (6%)
  other arithmetic  9.11 us (4%)
    all_to_all x1, waiting for transfers between devices, per_device(): lax.all_to_all(pair_out.reshape(chips, block_len, head_count, DH), 'z', s...  73.4 us
    ppermute x5, waiting for transfers between devices, fetched(): return lax.ppermute(stacked, AXES, route)  59.6 us
    pallas_call x1, Pallas kernels, pair_partials(): pl.pallas_call(pair_kernel, grid_spec=grid_spec, out_shape=[jax.ShapeDtyp...  32.1 us
    ppermute x5, starting transfers between devices, fetched(): return lax.ppermute(stacked, AXES, route)  15.7 us
    reshape x2, local copies, waits for them, and re-layouts, per_device(): pair_out.reshape(chips, block_len, head_count, DH)  13.5 us
    all_to_all x1, starting transfers between devices, per_device(): lax.all_to_all(pair_stats, 'z', split_axis=0, concat_axis=0, tiled=True)  10.3 us
    all_to_all x1, starting transfers between devices, per_device(): lax.all_to_all(pair_out.reshape(chips, block_len, head_count, DH), 'z', s...  7.2 us
  transfers between devices with their start and end apart: 8, of which 4 were waited for; matrix products, arithmetic and copies ran while one was open for 9% of the time, Pallas kernels for 0%

profile of v4, /device:TPU:32, one launch (start us, length us, event | category | flops | bytes accessed | tf_op | source)
XLA Modules:
  0.0 241.8 jit_solution(7352454437637280496)
XLA Ops:
  6.5 0.0 all-gather.2.cloned.1.call-start
  7.2 0.1 iota_add_fusion
  7.3 0.9 and_reduce_fusion
  8.2 0.1 copy.19
  8.3 0.1 convert_element_type.27
  8.4 1.8 pad_maximum_fusion.3
  10.2 0.0 all-gather.2.cloned.1.call-update
  10.2 1.2 pad_maximum_fusion.2
  11.4 4.4 %collective-permute-start.4 = (bf16[2,128,1536]{2,1,0:T(8,128)(2,1)S(1)}, bf16[2,128,1536]{2,1,0:T(8,128)(2,1)}, u32[]{:S(2)}, u32[]{:S(2)}) collective-permute-start(bf16[2,128,1536]{2,1,0:T(8,128)(2,1)S(1)} %pad_maximum_fusion.2), channel_id=1, source_target_pairs={{1,32},{0,33},{3,34},{2,35},{5,36},{4,37},{7,38},{6,39},{9,40},{8,... | collective-permute-start | bytes 2359304 | tf_op jit(solution)/shard_map/ppermute | solution.py:124
  15.8 2.5 %collective-permute-start.1 = (bf16[2,128,1536]{2,1,0:T(8,128)(2,1)S(1)}, bf16[2,128,1536]{2,1,0:T(8,128)(2,1)S(1)}, u32[]{:S(2)}, u32[]{:S(2)}) collective-permute-start(bf16[2,128,1536]{2,1,0:T(8,128)(2,1)S(1)} %pad_maximum_fusion.2), channel_id=1, source_target_pairs={{0,32},{1,33},{2,34},{3,35},{4,36},{5,37},{6,38},{7,39},{8,40},{9,... | collective-permute-start | bytes 2359304 | tf_op jit(solution)/shard_map/ppermute | solution.py:124
  18.3 3.4 %collective-permute-start.3 = (bf16[2,128,1536]{2,1,0:T(8,128)(2,1)S(1)}, bf16[2,128,1536]{2,1,0:T(8,128)(2,1)S(1)}, u32[]{:S(2)}, u32[]{:S(2)}) collective-permute-start(bf16[2,128,1536]{2,1,0:T(8,128)(2,1)S(1)} %pad_maximum_fusion.2), channel_id=1, source_target_pairs={{1,16},{0,17},{3,18},{2,19},{5,20},{4,21},{7,22},{6,23},{9,24},{8,... | collective-permute-start | bytes 2359304 | tf_op jit(solution)/shard_map/ppermute | solution.py:124
  21.7 2.0 collective-permute-start.2
  23.7 3.4 %collective-permute-start = (bf16[2,128,1536]{2,1,0:T(8,128)(2,1)S(1)}, bf16[2,128,1536]{2,1,0:T(8,128)(2,1)}, u32[]{:S(2)}, u32[]{:S(2)}) collective-permute-start(bf16[2,128,1536]{2,1,0:T(8,128)(2,1)S(1)} %pad_maximum_fusion.2), channel_id=1, source_target_pairs={{0,16},{1,17},{2,18},{3,19},{4,20},{5,21},{6,22},{7,23},{8,24},{9,... | collective-permute-start | bytes 2359304 | tf_op jit(solution)/shard_map/ppermute | solution.py:124
  27.2 0.0 copy-start
  27.2 0.0 copy-start.1
  27.2 9.7 %collective-permute-done.4 = bf16[2,128,1536]{2,1,0:T(8,128)(2,1)} collective-permute-done((bf16[2,128,1536]{2,1,0:T(8,128)(2,1)S(1)}, bf16[2,128,1536]{2,1,0:T(8,128)(2,1)}, u32[]{:S(2)}, u32[]{:S(2)}) %collective-permute-start.4) | collective-permute-done | bytes 786464 | tf_op jit(solution)/shard_map/ppermute | solution.py:124
  36.9 1.2 slice_bitcast_fusion
  38.1 15.6 %collective-permute-done.1 = bf16[2,128,1536]{2,1,0:T(8,128)(2,1)S(1)} collective-permute-done((bf16[2,128,1536]{2,1,0:T(8,128)(2,1)S(1)}, bf16[2,128,1536]{2,1,0:T(8,128)(2,1)S(1)}, u32[]{:S(2)}, u32[]{:S(2)}) %collective-permute-start.1) | collective-permute-done | bytes 786464 | tf_op jit(solution)/shard_map/ppermute | solution.py:124
  53.7 0.1 slice_bitcast_fusion.3
  53.7 34.3 %collective-permute-done = bf16[2,128,1536]{2,1,0:T(8,128)(2,1)} collective-permute-done((bf16[2,128,1536]{2,1,0:T(8,128)(2,1)S(1)}, bf16[2,128,1536]{2,1,0:T(8,128)(2,1)}, u32[]{:S(2)}, u32[]{:S(2)}) %collective-permute-start) | collective-permute-done | bytes 786464 | tf_op jit(solution)/shard_map/ppermute | solution.py:124
  88.0 1.2 slice_bitcast_fusion.4
  89.2 0.0 copy-done
  89.2 0.0 copy-done.1
  89.2 0.2 maximum_bitcast_fusion
  89.4 0.0 collective-permute-done.3
  89.4 0.1 slice_bitcast_fusion.1
  89.5 0.0 collective-permute-done.2
  89.5 0.1 slice_bitcast_fusion.2
  89.5 0.2 maximum_bitcast_fusion.1
  89.7 1.7 pad_maximum_fusion.k_ref
  91.4 1.6 pad_maximum_fusion.1.v_ref
  93.0 0.0 all-gather.2.cloned.1.call-done.q_ref
  93.0 0.7 slice.52
  93.7 0.1 copy.31
  93.9 0.1 copy.21
  94.0 0.1 reshape.67
  94.0 0.7 pad_add_fusion.1.info_ref
  94.7 32.1 %shard_map.55 = (bf16[1024,1536]{1,0:T(8,128)(2,1)}, f32[8,128,24]{2,1,0:T(8,128)}) custom-call(s32[50]{0:T(128)} %pad_add_fusion.1.info_ref, bf16[1024,1664]{1,0:T(8,128)(2,1)} %all-gather.2.cloned.1.call-done.q_ref, bf16[2,384,1536]{2,1,0:T(8,128)(2,1)} %pad_maximum_fusion.k_ref, bf16[2,384,1536]{2,1,0:T(8,128)(2,1)} %pad_maximum_fusion.1.v_ref), custom_call_target="tpu_custom_call" | custom-call | flops 3221225472 | bytes 11010048 | tf_op jit(solution)/shard_map/pallas_call | solution.py:89
  126.9 1.9 copy.22
  128.7 10.3 %all-to-all-start = ((f32[8,128,24]{1,2,0:T(8,128)}), f32[8,128,24]{1,2,0:T(8,128)S(1)}, u32[]{:S(2)}, u32[]{:S(2)}) async-start(f32[8,128,24]{1,2,0:T(8,128)} %copy.22), calls=%async_computation | async-start | bytes 196608 | tf_op jit(solution)/shard_map/all_to_all | solution.py:163
  139.0 6.9 %reshape.70 = bf16[8,128,12,128]{3,2,1,0:T(8,128)(2,1)} reshape(bf16[1024,1536]{1,0:T(8,128)(2,1)} %get-tuple-element.8) | data formatting | bytes 6291456 | tf_op jit(solution)/shard_map/reshape | solution.py:160
  145.9 6.6 %copy.24 = bf16[8,128,12,128]{1,3,2,0:T(8,128)(2,1)} copy(bf16[8,128,12,128]{3,2,1,0:T(8,128)(2,1)} %reshape.70) | data formatting | bytes 6291456 | tf_op jit(solution)/shard_map/reshape | solution.py:160
  152.5 0.0 all-to-all-done
  152.5 7.2 %all-to-all-start.1 = ((bf16[8,128,12,128]{1,3,2,0:T(8,128)(2,1)}), bf16[8,128,12,128]{1,3,2,0:T(8,128)(2,1)S(1)}, u32[]{:S(2)}, u32[]{:S(2)}) async-start(bf16[8,128,12,128]{1,3,2,0:T(8,128)(2,1)} %copy.24), calls=%async_computation.1 | async-start | bytes 6291456 | tf_op jit(solution)/shard_map/all_to_all | solution.py:159
  159.7 73.4 %all-to-all-done.1 = bf16[8,128,12,128]{1,3,2,0:T(8,128)(2,1)S(1)} async-done(((bf16[8,128,12,128]{1,3,2,0:T(8,128)(2,1)}), bf16[8,128,12,128]{1,3,2,0:T(8,128)(2,1)S(1)}, u32[]{:S(2)}, u32[]{:S(2)}) %all-to-all-start.1) | async-done | bytes 3145760 | tf_op jit(solution)/shard_map/all_to_all | solution.py:159
  233.2 0.8 multiply_reduce_fusion
  234.0 0.1 divide_convert_fusion
  234.1 0.9 copy.27
  (9 shorter events, 0.1 us)
Async XLA Ops:
  6.5 86.4 %all-gather.2.cloned.1.call-start = ((), (), s32[]{:S(2)}) async-start(), calls=%async_computation.2 | async-start | bytes 3833856 | tf_op jit(solution)/shard_map/all_gather | solution.py:145
  11.4 25.5 %collective-permute-start.4 = (bf16[2,128,1536]{2,1,0:T(8,128)(2,1)S(1)}, bf16[2,128,1536]{2,1,0:T(8,128)(2,1)}, u32[]{:S(2)}, u32[]{:S(2)}) collective-permute-start(bf16[2,128,1536]{2,1,0:T(8,128)(2,1)S(1)} %pad_maximum_fusion.2), channel_id=1, source_target_pairs={{1,32},{0,33},{3,34},{2,35},{5,36},{4,37},{7,38},{6,39},{9,40},{8,... | collective-permute-start | bytes 2359304 | tf_op jit(solution)/shard_map/ppermute | solution.py:124
  15.8 37.9 %collective-permute-start.1 = (bf16[2,128,1536]{2,1,0:T(8,128)(2,1)S(1)}, bf16[2,128,1536]{2,1,0:T(8,128)(2,1)S(1)}, u32[]{:S(2)}, u32[]{:S(2)}) collective-permute-start(bf16[2,128,1536]{2,1,0:T(8,128)(2,1)S(1)} %pad_maximum_fusion.2), channel_id=1, source_target_pairs={{0,32},{1,33},{2,34},{3,35},{4,36},{5,37},{6,38},{7,39},{8,40},{9,... | collective-permute-start | bytes 2359304 | tf_op jit(solution)/shard_map/ppermute | solution.py:124
  18.3 71.1 %collective-permute-start.3 = (bf16[2,128,1536]{2,1,0:T(8,128)(2,1)S(1)}, bf16[2,128,1536]{2,1,0:T(8,128)(2,1)S(1)}, u32[]{:S(2)}, u32[]{:S(2)}) collective-permute-start(bf16[2,128,1536]{2,1,0:T(8,128)(2,1)S(1)} %pad_maximum_fusion.2), channel_id=1, source_target_pairs={{1,16},{0,17},{3,18},{2,19},{5,20},{4,21},{7,22},{6,23},{9,24},{8,... | collective-permute-start | bytes 2359304 | tf_op jit(solution)/shard_map/ppermute | solution.py:124
  21.7 67.8 %collective-permute-start.2 = (bf16[2,128,1536]{2,1,0:T(8,128)(2,1)S(1)}, bf16[2,128,1536]{2,1,0:T(8,128)(2,1)S(1)}, u32[]{:S(2)}, u32[]{:S(2)}) collective-permute-start(bf16[2,128,1536]{2,1,0:T(8,128)(2,1)S(1)} %pad_maximum_fusion.2), channel_id=1, source_target_pairs={{1,0},{0,1},{3,2},{2,3},{5,4},{4,5},{7,6},{6,7},{9,8},{8,9},{11,10... | collective-permute-start | bytes 2359304 | tf_op jit(solution)/shard_map/ppermute | solution.py:124
  23.7 64.3 %collective-permute-start = (bf16[2,128,1536]{2,1,0:T(8,128)(2,1)S(1)}, bf16[2,128,1536]{2,1,0:T(8,128)(2,1)}, u32[]{:S(2)}, u32[]{:S(2)}) collective-permute-start(bf16[2,128,1536]{2,1,0:T(8,128)(2,1)S(1)} %pad_maximum_fusion.2), channel_id=1, source_target_pairs={{0,16},{1,17},{2,18},{3,19},{4,20},{5,21},{6,22},{7,23},{8,24},{9,... | collective-permute-start | bytes 2359304 | tf_op jit(solution)/shard_map/ppermute | solution.py:124
  27.2 62.0 %copy-start = (bf16[128,1536]{1,0:T(8,128)(2,1)S(1)}, bf16[128,1536]{1,0:T(8,128)(2,1)}, u32[]{:S(2)}) copy-start(bf16[128,1536]{1,0:T(8,128)(2,1)} %param.7) | copy-start | bytes 1179652
  27.2 62.0 %copy-start.1 = (bf16[128,1536]{1,0:T(8,128)(2,1)S(1)}, bf16[128,1536]{1,0:T(8,128)(2,1)}, u32[]{:S(2)}) copy-start(bf16[128,1536]{1,0:T(8,128)(2,1)} %param.6) | copy-start | bytes 1179652
  128.7 23.8 %all-to-all-start = ((f32[8,128,24]{1,2,0:T(8,128)}), f32[8,128,24]{1,2,0:T(8,128)S(1)}, u32[]{:S(2)}, u32[]{:S(2)}) async-start(f32[8,128,24]{1,2,0:T(8,128)} %copy.22), calls=%async_computation | async-start | bytes 196608 | tf_op jit(solution)/shard_map/all_to_all | solution.py:163
  152.5 80.7 %all-to-all-start.1 = ((bf16[8,128,12,128]{1,3,2,0:T(8,128)(2,1)}), bf16[8,128,12,128]{1,3,2,0:T(8,128)(2,1)S(1)}, u32[]{:S(2)}, u32[]{:S(2)}) async-start(bf16[8,128,12,128]{1,3,2,0:T(8,128)(2,1)} %copy.24), calls=%async_computation.1 | async-start | bytes 6291456 | tf_op jit(solution)/shard_map/all_to_all | solution.py:159
Sparse Core Ops, SparseCore 0:
  10.3 55.0 all-gather.1

commit v5 on v4

--- a/solution.py
+++ b/solution.py
@@ -15,18 +15,26 @@
 AXES = ("pb", "z", "core")
 
 
+def passed_along(block, axis, distance):
+    devices = range(lax.axis_size(axis))
+    route = [(i - distance, i) for i in devices if i - distance in devices]
+    return lax.ppermute(block, axis, route)
+
+
 def pair_kernel(info_ref, q_ref, k_ref, v_ref, out_ref, stat_ref):
     t = pl.program_id(0)
     chip = info_ref[0]
     core = info_ref[1]
     block_len = out_ref.shape[0]
-    head_count = out_ref.shape[1] // DH
+    feature_width = k_ref.shape[2]
+    head_count = feature_width // DH
     column = 2 * t + core
     q_pos = lax.broadcasted_iota(jnp.int32, (block_len, 2 * block_len), 0)
     k_pos = lax.broadcasted_iota(jnp.int32, (block_len, 2 * block_len), 1)
     first = k_pos < block_len
     starts = []
     masks = []
+    stat_ref[...] = jnp.zeros_like(stat_ref)
     for j in range(2):
         key_class = 2 * chip + (core + j) % 2
         lag_a = jnp.where(key_class <= column, 0, 1)
@@ -52,6 +60,7 @@
         highest = jnp.maximum(
             jnp.max(scores[0], axis=1, keepdims=True), jnp.max(scores[1], axis=1, keepdims=True)
         )
+        highest = (highest + jnp.abs(highest) * (2.0**-7)).astype(jnp.bfloat16).astype(jnp.float32)
         total = None
         blended = None
         for j in range(2):
@@ -65,13 +74,15 @@
             total = part_total if total is None else total + part_total
             blended = part if blended is None else blended + part
         out_ref[:, cols] = blended.astype(jnp.bfloat16)
-        stat_ref[0, :, h : h + 1] = highest
-        stat_ref[0, :, head_count + h : head_count + h + 1] = total
+        stat_ref[:, h : h + 1] = highest
+        stat_ref[:, head_count + h : head_count + h + 1] = total
+    out_ref[:, feature_width:] = stat_ref[...].astype(jnp.bfloat16)
 
 
-def pair_partials(info, row_q, key_window, value_window, feature_width):
+def pair_partials(info, row_q, key_window, value_window):
     block_len = key_window.shape[1] // LAGS
     sources = row_q.shape[0] // block_len
+    feature_width = key_window.shape[2]
     head_count = feature_width // DH
     grid_spec = pltpu.PrefetchScalarGridSpec(
         num_scalar_prefetch=1,
@@ -81,22 +92,17 @@
             pl.BlockSpec(key_window.shape, lambda t, info_ref: (0, 0, 0)),
             pl.BlockSpec(value_window.shape, lambda t, info_ref: (0, 0, 0)),
         ],
-        out_specs=[
-            pl.BlockSpec((block_len, feature_width), lambda t, info_ref: (t, 0)),
-            pl.BlockSpec((1, block_len, 2 * head_count), lambda t, info_ref: (t, 0, 0)),
-        ],
+        out_specs=pl.BlockSpec((block_len, row_q.shape[1]), lambda t, info_ref: (t, 0)),
+        scratch_shapes=[pltpu.VMEM((block_len, row_q.shape[1] - feature_width), jnp.float32)],
     )
     return pl.pallas_call(
         pair_kernel,
         grid_spec=grid_spec,
-        out_shape=[
-            jax.ShapeDtypeStruct((sources * block_len, feature_width), jnp.bfloat16),
-            jax.ShapeDtypeStruct((sources, block_len, 2 * head_count), jnp.float32),
-        ],
+        out_shape=jax.ShapeDtypeStruct(row_q.shape, jnp.bfloat16),
         cost_estimate=pl.CostEstimate(
             flops=sources * head_count * 2 * 2 * 2 * block_len * 2 * block_len * DH,
             transcendentals=sources * head_count * 2 * 2 * block_len * block_len,
-            bytes_accessed=2 * sources * block_len * feature_width * 2
+            bytes_accessed=2 * sources * block_len * row_q.shape[1] * 2
             + 2 * 2 * LAGS * block_len * feature_width * 2,
         ),
     )(info, row_q, key_window, value_window)
@@ -115,16 +121,13 @@
 
     stacked = jnp.stack([keys, values])
 
-    def fetched(lag, flip):
-        route = []
-        for dst in range(rows * stripe_count):
-            src_row = dst // stripe_count - lag
-            if src_row >= 0:
-                route.append((src_row * stripe_count + ((dst % stripe_count) ^ flip), dst))
-        return lax.ppermute(stacked, AXES, route)
-
-    own = [stacked, fetched(1, 0), fetched(2, 0)]
-    partner = [fetched(0, 1), fetched(1, 1), fetched(2, 1)]
+    swap = [(0, 1), (1, 0)]
+    lag_1 = passed_along(stacked, "pb", 1)
+    lag_2 = passed_along(stacked, "pb", 2)
+    partner_0 = lax.ppermute(stacked, "core", swap)
+    partner_12 = lax.ppermute(jnp.stack([lag_1, lag_2]), "core", swap)
+    own = [stacked, lag_1, lag_2]
+    partner = [partner_0, partner_12[0], partner_12[1]]
     key_window = jnp.stack(
         [jnp.concatenate([x[0] for x in own]), jnp.concatenate([x[0] for x in partner])]
     )
@@ -155,17 +158,17 @@
         [jnp.stack([chip, core]).astype(jnp.int32), jnp.stack(mine, axis=1).reshape(-1)]
     )
 
-    pair_out, pair_stats = pair_partials(info, row_q, key_window, value_window, feature_width)
+    pair_out = pair_partials(info, row_q, key_window, value_window)
     pair_out = lax.all_to_all(
-        pair_out.reshape(chips, block_len, head_count, DH), "z", split_axis=0, concat_axis=0,
-        tiled=True,
+        pair_out.reshape(chips, block_len, -1), "z", split_axis=0, concat_axis=0, tiled=True
     )
-    pair_stats = lax.all_to_all(pair_stats, "z", split_axis=0, concat_axis=0, tiled=True)
+    pair_stats = pair_out[..., feature_width : feature_width + 2 * head_count].astype(jnp.float32)
     pair_max, pair_tot = pair_stats[..., :head_count], pair_stats[..., head_count:]
     highest = jnp.max(pair_max, axis=0)
     factor = jnp.exp(pair_max - highest[None])
     denominator = jnp.sum(factor * pair_tot, axis=0)
-    numerator = jnp.sum(factor[..., None] * pair_out.astype(jnp.float32), axis=0)
+    partial_out = pair_out[..., :feature_width].reshape(chips, block_len, head_count, DH)
+    numerator = jnp.sum(factor[..., None] * partial_out.astype(jnp.float32), axis=0)
     return (
         (numerator / denominator[..., None]).reshape(block_len, feature_width).astype(jnp.bfloat16)
     )

time: 243 us -> 200 us (0.82)
  waiting for transfers between devices: 133 us -> 38.5 us
  blocking collectives: 0 us -> 87.1 us
  starting transfers between devices: 33.2 us -> 11.4 us
  local copies, waits for them, and re-layouts: 20 us -> 6.92 us
    all_to_all x0 -> x1, blocking collectives: none -> 87.1 us  [per_device(): lax.all_to_all(pair_out.reshape(chips, block_len, -1), 'z', split_axis=0,...]
    all_to_all x2 -> x0, waiting for transfers between devices: 73.4 us -> none  [the longest x1 73.4 us: per_device(): lax.all_to_all(pair_out.reshape(chips, block_len, head_count, DH), 'z', s...]
    ppermute x5 -> x4, waiting for transfers between devices: 59.6 us -> 35.9 us  [the longest x2 32.9 us: passed_along(): return lax.ppermute(block, axis, route)]
    all_to_all x2 -> x0, starting transfers between devices: 17.5 us -> none  [the longest x1 10.3 us: per_device(): lax.all_to_all(pair_stats, 'z', split_axis=0, concat_axis=0, tiled=True)]
    reshape x2 -> x1, local copies, waits for them, and re-layouts: 13.5 us -> 4.48 us  [per_device(): pair_out.reshape(chips, block_len, -1)]
    ppermute x5 -> x4, starting transfers between devices: 15.7 us -> 11.4 us  [the longest x2 7.43 us: passed_along(): return lax.ppermute(block, axis, route)]
    all_gather x1, waiting for transfers between devices: 0.01 us -> 2.64 us  [per_device(): lax.all_gather(jnp.concatenate([queries, spare], axis=1), 'z', axis=0, ti...]
  transfers between devices with their start and end apart: 8 -> 5, of which waited for: 4 -> 4; matrix products, arithmetic and copies ran while one was open for 9% -> 3% of each run, Pallas kernels for 0% -> 0%
where the time goes in v5:
time: 200 us
  blocking collectives  87.1 us (44%)
  waiting for transfers between devices  38.5 us (19%)
  Pallas kernels  32.4 us (16%)
  between operations  14.3 us (7%)
  starting transfers between devices  11.4 us (6%)
  other arithmetic  9.03 us (5%)
  local copies, waits for them, and re-layouts  6.92 us (3%)
    all_to_all x1, blocking collectives, per_device(): lax.all_to_all(pair_out.reshape(chips, block_len, -1), 'z', split_axis=0,...  87.1 us
    ppermute x2, waiting for transfers between devices, passed_along(): return lax.ppermute(block, axis, route)  32.9 us
    pallas_call x1, Pallas kernels, pair_partials(): pl.pallas_call(pair_kernel, grid_spec=grid_spec, out_shape=jax.ShapeDtype...  32.4 us
    ppermute x2, starting transfers between devices, passed_along(): return lax.ppermute(block, axis, route)  7.43 us
    reshape x1, local copies, waits for them, and re-layouts, per_device(): pair_out.reshape(chips, block_len, -1)  4.48 us
  transfers between devices with their start and end apart: 5, of which 4 were waited for; matrix products, arithmetic and copies ran while one was open for 3% of the time, Pallas kernels for 0%

profile of v5, /device:TPU:32, one launch (start us, length us, event | category | flops | bytes accessed | tf_op | source)
XLA Modules:
  0.0 199.6 jit_solution(2798988214379620365)
XLA Ops:
  6.5 0.0 all-gather.2.cloned.1.call-start
  7.2 0.1 iota_add_fusion
  7.3 0.9 and_reduce_fusion
  8.2 0.1 copy.10
  8.3 0.1 convert_element_type.28
  8.4 1.8 pad_maximum_fusion.4
  10.2 0.0 all-gather.2.cloned.1.call-update
  10.2 1.2 pad_maximum_fusion.3
  11.4 4.9 %collective-permute-start.1 = (bf16[2,128,1536]{2,1,0:T(8,128)(2,1)S(1)}, bf16[2,128,1536]{2,1,0:T(8,128)(2,1)S(1)}, u32[]{:S(2)}, u32[]{:S(2)}) collective-permute-start(bf16[2,128,1536]{2,1,0:T(8,128)(2,1)S(1)} %pad_maximum_fusion.3), channel_id=1, source_target_pairs={{0,32},{16,48},{32,64},{48,80},{64,96},{80,112},{96,128},{112,144}... | collective-permute-start | bytes 2359304 | tf_op jit(solution)/shard_map/ppermute | solution.py:21
  16.3 2.5 %collective-permute-start = (bf16[2,128,1536]{2,1,0:T(8,128)(2,1)S(1)}, bf16[2,128,1536]{2,1,0:T(8,128)(2,1)S(1)}, u32[]{:S(2)}, u32[]{:S(2)}) collective-permute-start(bf16[2,128,1536]{2,1,0:T(8,128)(2,1)S(1)} %pad_maximum_fusion.3), channel_id=1, source_target_pairs={{0,16},{16,32},{32,48},{48,64},{64,80},{80,96},{96,112},{112,128},... | collective-permute-start | bytes 2359304 | tf_op jit(solution)/shard_map/ppermute | solution.py:21
  18.8 1.9 collective-permute-start.2
  20.8 15.8 %collective-permute-done.1 = bf16[2,128,1536]{2,1,0:T(8,128)(2,1)S(1)} collective-permute-done((bf16[2,128,1536]{2,1,0:T(8,128)(2,1)S(1)}, bf16[2,128,1536]{2,1,0:T(8,128)(2,1)S(1)}, u32[]{:S(2)}, u32[]{:S(2)}) %collective-permute-start.1) | collective-permute-done | bytes 786464 | tf_op jit(solution)/shard_map/ppermute | solution.py:21
  36.5 17.1 %collective-permute-done = bf16[2,128,1536]{2,1,0:T(8,128)(2,1)S(1)} collective-permute-done((bf16[2,128,1536]{2,1,0:T(8,128)(2,1)S(1)}, bf16[2,128,1536]{2,1,0:T(8,128)(2,1)S(1)}, u32[]{:S(2)}, u32[]{:S(2)}) %collective-permute-start) | collective-permute-done | bytes 786464 | tf_op jit(solution)/shard_map/ppermute | solution.py:21
  53.7 0.1 pad_maximum_fusion.2
  53.8 0.0 copy-start
  53.8 0.0 copy-start.1
  53.8 2.1 %collective-permute-start.3 = (bf16[2,2,128,1536]{3,2,1,0:T(8,128)(2,1)S(1)}, bf16[2,2,128,1536]{3,2,1,0:T(8,128)(2,1)S(1)}, u32[]{:S(2)}, u32[]{:S(2)}) collective-permute-start(bf16[2,2,128,1536]{3,2,1,0:T(8,128)(2,1)S(1)} %pad_maximum_fusion.2), channel_id=1, source_target_pairs={{0,1},{1,0},{2,3},{3,2},{4,5},{5,4},{6,7},{7,6},{8,9},{9,8},{10,11... | collective-permute-start | bytes 4718600 | tf_op jit(solution)/shard_map/ppermute | solution.py:128
  55.9 0.1 slice_bitcast_fusion.3
  55.9 0.1 slice_bitcast_fusion.4
  56.0 0.0 copy-done
  56.0 0.0 copy-done.1
  56.0 0.2 maximum_bitcast_fusion
  56.2 0.0 collective-permute-done.2
  56.2 0.1 slice_bitcast_fusion.2
  56.3 3.0 %collective-permute-done.3 = bf16[2,2,128,1536]{3,2,1,0:T(8,128)(2,1)S(1)} collective-permute-done((bf16[2,2,128,1536]{3,2,1,0:T(8,128)(2,1)S(1)}, bf16[2,2,128,1536]{3,2,1,0:T(8,128)(2,1)S(1)}, u32[]{:S(2)}, u32[]{:S(2)}) %collective-permute-start.3) | collective-permute-done | bytes 1572896 | tf_op jit(solution)/shard_map/ppermute | solution.py:128
  59.3 0.1 slice_bitcast_fusion.1
  59.4 0.2 maximum_bitcast_fusion.1
  59.5 1.7 pad_maximum_fusion.k_ref
  61.2 1.6 pad_maximum_fusion.1.v_ref
  62.8 2.6 %all-gather.2.cloned.1.call-done.q_ref = bf16[1024,1664]{1,0:T(8,128)(2,1)} async-done(((bf16[128,1664]{1,0:T(8,128)(2,1)}), bf16[1024,1664]{1,0:T(8,128)(2,1)}) %all-gather.2.cloned.1.call-update) | async-done | bytes 3407888 | tf_op jit(solution)/shard_map/all_gather | solution.py:148
  65.4 0.7 slice.70
  66.2 0.1 copy.15
  66.3 0.1 copy.12
  66.4 0.1 reshape.77
  66.5 0.6 pad_add_fusion.1.info_ref
  67.1 32.4 %shard_map.55 = bf16[1024,1664]{1,0:T(8,128)(2,1)} custom-call(s32[50]{0:T(128)} %pad_add_fusion.1.info_ref, bf16[1024,1664]{1,0:T(8,128)(2,1)} %all-gather.2.cloned.1.call-done.q_ref, bf16[2,384,1536]{2,1,0:T(8,128)(2,1)} %pad_maximum_fusion.k_ref, bf16[2,384,1536]{2,1,0:T(8,128)(2,1)} %pad_maximum_fusion.1.v_ref), custom_call_target="tpu_custom_call" | custom-call | flops 3221225472 | bytes 11534336 | tf_op jit(solution)/shard_map/pallas_call | solution.py:98
  99.5 4.5 %copy.13 = bf16[8,128,1664]{1,2,0:T(8,128)(2,1)S(1)} copy(bf16[8,128,1664]{2,1,0:T(8,128)(2,1)} %bitcast.49) | data formatting | bytes 6815744 | tf_op jit(solution)/shard_map/reshape | solution.py:163
  104.0 87.1 %all_to_all.5 = bf16[8,128,1664]{1,2,0:T(8,128)(2,1)S(1)} all-to-all(bf16[8,128,1664]{1,2,0:T(8,128)(2,1)S(1)} %copy.13), channel_id=1, replica_groups=mesh['pb'=32,'z'=8,'core'=2] {'z'}, dimensions={0} | all-to-all | bytes 6815744 | tf_op jit(solution)/shard_map/all_to_all | solution.py:162
  191.1 0.7 fusion
  191.8 0.1 fusion.1
  191.8 0.9 copy.14
  (10 shorter events, 0.1 us)
Async XLA Ops:
  6.5 58.9 %all-gather.2.cloned.1.call-start = ((), (), s32[]{:S(2)}) async-start(), calls=%async_computation.1 | async-start | bytes 3833856 | tf_op jit(solution)/shard_map/all_gather | solution.py:148
  11.4 25.2 %collective-permute-start.1 = (bf16[2,128,1536]{2,1,0:T(8,128)(2,1)S(1)}, bf16[2,128,1536]{2,1,0:T(8,128)(2,1)S(1)}, u32[]{:S(2)}, u32[]{:S(2)}) collective-permute-start(bf16[2,128,1536]{2,1,0:T(8,128)(2,1)S(1)} %pad_maximum_fusion.3), channel_id=1, source_target_pairs={{0,32},{16,48},{32,64},{48,80},{64,96},{80,112},{96,128},{112,144}... | collective-permute-start | bytes 2359304 | tf_op jit(solution)/shard_map/ppermute | solution.py:21
  16.3 37.3 %collective-permute-start = (bf16[2,128,1536]{2,1,0:T(8,128)(2,1)S(1)}, bf16[2,128,1536]{2,1,0:T(8,128)(2,1)S(1)}, u32[]{:S(2)}, u32[]{:S(2)}) collective-permute-start(bf16[2,128,1536]{2,1,0:T(8,128)(2,1)S(1)} %pad_maximum_fusion.3), channel_id=1, source_target_pairs={{0,16},{16,32},{32,48},{48,64},{64,80},{80,96},{96,112},{112,128},... | collective-permute-start | bytes 2359304 | tf_op jit(solution)/shard_map/ppermute | solution.py:21
  18.8 37.4 %collective-permute-start.2 = (bf16[2,128,1536]{2,1,0:T(8,128)(2,1)S(1)}, bf16[2,128,1536]{2,1,0:T(8,128)(2,1)S(1)}, u32[]{:S(2)}, u32[]{:S(2)}) collective-permute-start(bf16[2,128,1536]{2,1,0:T(8,128)(2,1)S(1)} %pad_maximum_fusion.3), channel_id=1, source_target_pairs={{0,1},{1,0},{2,3},{3,2},{4,5},{5,4},{6,7},{7,6},{8,9},{9,8},{10,11... | collective-permute-start | bytes 2359304 | tf_op jit(solution)/shard_map/ppermute | solution.py:127
  53.8 2.2 %copy-start = (bf16[128,1536]{1,0:T(8,128)(2,1)S(1)}, bf16[128,1536]{1,0:T(8,128)(2,1)}, u32[]{:S(2)}) copy-start(bf16[128,1536]{1,0:T(8,128)(2,1)} %param.7) | copy-start | bytes 1179652
  53.8 2.2 %copy-start.1 = (bf16[128,1536]{1,0:T(8,128)(2,1)S(1)}, bf16[128,1536]{1,0:T(8,128)(2,1)}, u32[]{:S(2)}) copy-start(bf16[128,1536]{1,0:T(8,128)(2,1)} %param.6) | copy-start | bytes 1179652
  53.8 5.4 %collective-permute-start.3 = (bf16[2,2,128,1536]{3,2,1,0:T(8,128)(2,1)S(1)}, bf16[2,2,128,1536]{3,2,1,0:T(8,128)(2,1)S(1)}, u32[]{:S(2)}, u32[]{:S(2)}) collective-permute-start(bf16[2,2,128,1536]{3,2,1,0:T(8,128)(2,1)S(1)} %pad_maximum_fusion.2), channel_id=1, source_target_pairs={{0,1},{1,0},{2,3},{3,2},{4,5},{5,4},{6,7},{7,6},{8,9},{9,8},{10,11... | collective-permute-start | bytes 4718600 | tf_op jit(solution)/shard_map/ppermute | solution.py:128
Sparse Core Ops, SparseCore 0:
  10.3 55.0 all-gather.1

commit v6 on v5

--- a/solution.py
+++ b/solution.py
@@ -13,6 +13,7 @@
 NEG_FILL = -1e30
 LAGS = 3
 AXES = ("pb", "z", "core")
+HEADER = 4
 
 
 def passed_along(block, axis, distance):
@@ -22,10 +23,11 @@
 
 
 def pair_kernel(info_ref, q_ref, k_ref, v_ref, out_ref, stat_ref):
-    t = pl.program_id(0)
     chip = info_ref[0]
     core = info_ref[1]
-    block_len = out_ref.shape[0]
+    chips = info_ref[2]
+    t = (chip + info_ref[3] + pl.program_id(0)) % chips
+    block_len = out_ref.shape[1]
     feature_width = k_ref.shape[2]
     head_count = feature_width // DH
     column = 2 * t + core
@@ -38,7 +40,7 @@
     for j in range(2):
         key_class = 2 * chip + (core + j) % 2
         lag_a = jnp.where(key_class <= column, 0, 1)
-        base = 2 + (t * 2 + j) * LAGS + lag_a
+        base = HEADER + (t * 2 + j) * LAGS + lag_a
         listed_a = info_ref[base] != 0
         listed_b = info_ref[base + 1] != 0
         diagonal = key_class == column
@@ -73,36 +75,42 @@
             )
             total = part_total if total is None else total + part_total
             blended = part if blended is None else blended + part
-        out_ref[:, cols] = blended.astype(jnp.bfloat16)
+        out_ref[0, :, cols] = blended.astype(jnp.bfloat16)
+        upper = total.astype(jnp.bfloat16).astype(jnp.float32)
         stat_ref[:, h : h + 1] = highest
-        stat_ref[:, head_count + h : head_count + h + 1] = total
-    out_ref[:, feature_width:] = stat_ref[...].astype(jnp.bfloat16)
-
-
-def pair_partials(info, row_q, key_window, value_window):
+        stat_ref[:, head_count + h : head_count + h + 1] = upper
+        stat_ref[:, 2 * head_count + h : 2 * head_count + h + 1] = total - upper
+    out_ref[0, :, feature_width:] = stat_ref[...].astype(jnp.bfloat16)
+
+
+def pair_partials(info, row_q, key_window, value_window, steps):
     block_len = key_window.shape[1] // LAGS
-    sources = row_q.shape[0] // block_len
+    chips = row_q.shape[0] // block_len
     feature_width = key_window.shape[2]
     head_count = feature_width // DH
+
+    def q_map(i, info_ref):
+        return ((info_ref[0] + info_ref[3] + i) % chips, 0)
+
     grid_spec = pltpu.PrefetchScalarGridSpec(
         num_scalar_prefetch=1,
-        grid=(sources,),
+        grid=(steps,),
         in_specs=[
-            pl.BlockSpec((block_len, row_q.shape[1]), lambda t, info_ref: (t, 0)),
-            pl.BlockSpec(key_window.shape, lambda t, info_ref: (0, 0, 0)),
-            pl.BlockSpec(value_window.shape, lambda t, info_ref: (0, 0, 0)),
+            pl.BlockSpec((block_len, row_q.shape[1]), q_map),
+            pl.BlockSpec(key_window.shape, lambda i, info_ref: (0, 0, 0)),
+            pl.BlockSpec(value_window.shape, lambda i, info_ref: (0, 0, 0)),
         ],
-        out_specs=pl.BlockSpec((block_len, row_q.shape[1]), lambda t, info_ref: (t, 0)),
+        out_specs=pl.BlockSpec((1, block_len, row_q.shape[1]), lambda i, info_ref: (i, 0, 0)),
         scratch_shapes=[pltpu.VMEM((block_len, row_q.shape[1] - feature_width), jnp.float32)],
     )
     return pl.pallas_call(
         pair_kernel,
         grid_spec=grid_spec,
-        out_shape=jax.ShapeDtypeStruct(row_q.shape, jnp.bfloat16),
+        out_shape=jax.ShapeDtypeStruct((steps, block_len, row_q.shape[1]), jnp.bfloat16),
         cost_estimate=pl.CostEstimate(
-            flops=sources * head_count * 2 * 2 * 2 * block_len * 2 * block_len * DH,
-            transcendentals=sources * head_count * 2 * 2 * block_len * block_len,
-            bytes_accessed=2 * sources * block_len * row_q.shape[1] * 2
+            flops=steps * head_count * 2 * 2 * 2 * block_len * 2 * block_len * DH,
+            transcendentals=steps * head_count * 2 * 2 * block_len * block_len,
+            bytes_accessed=2 * steps * block_len * row_q.shape[1] * 2
             + 2 * 2 * LAGS * block_len * feature_width * 2,
         ),
     )(info, row_q, key_window, value_window)
@@ -154,16 +162,26 @@
         lax.dynamic_index_in_dim(marks_all, 2 * chip + (core + j) % 2, axis=1, keepdims=False)
         for j in range(2)
     ]
-    info = jnp.concatenate(
-        [jnp.stack([chip, core]).astype(jnp.int32), jnp.stack(mine, axis=1).reshape(-1)]
-    )
-
-    pair_out = pair_partials(info, row_q, key_window, value_window)
-    pair_out = lax.all_to_all(
-        pair_out.reshape(chips, block_len, -1), "z", split_axis=0, concat_axis=0, tiled=True
-    )
-    pair_stats = pair_out[..., feature_width : feature_width + 2 * head_count].astype(jnp.float32)
-    pair_max, pair_tot = pair_stats[..., :head_count], pair_stats[..., head_count:]
+    mine = jnp.stack(mine, axis=1).reshape(-1)
+    header = jnp.stack([chip, core, jnp.int32(chips)]).astype(jnp.int32)
+
+    half = chips // 2
+    first_offset = chips // 4
+    received = []
+    for offset in (first_offset, first_offset + half):
+        info = jnp.concatenate([header, jnp.full((1,), offset % chips, jnp.int32), mine])
+        pair_out = pair_partials(info, row_q, key_window, value_window, half)
+        for i in range(half):
+            shift = (offset + i) % chips
+            if shift == 0:
+                received.append(pair_out[i])
+            else:
+                route = [(src, (src + shift) % chips) for src in range(chips)]
+                received.append(lax.ppermute(pair_out[i], "z", route))
+    pair_out = jnp.stack(received)
+    pair_stats = pair_out[..., feature_width : feature_width + 3 * head_count].astype(jnp.float32)
+    pair_max = pair_stats[..., :head_count]
+    pair_tot = pair_stats[..., head_count : 2 * head_count] + pair_stats[..., 2 * head_count :]
     highest = jnp.max(pair_max, axis=0)
     factor = jnp.exp(pair_max - highest[None])
     denominator = jnp.sum(factor * pair_tot, axis=0)

time: 200 us -> 220 us (1.10)
  blocking collectives: 87.1 us -> 0 us
  waiting for transfers between devices: 38.5 us -> 86.2 us
  starting transfers between devices: 11.4 us -> 43.5 us
  local copies, waits for them, and re-layouts: 6.92 us -> 23.6 us
  other arithmetic: 9.03 us -> 14.5 us
  Pallas kernels: 32.4 us -> 36.5 us
    all_to_all x1 -> x0, blocking collectives: 87.1 us -> none  [per_device(): lax.all_to_all(pair_out.reshape(chips, block_len, -1), 'z', split_axis=0,...]
    ppermute x0 -> x7, waiting for transfers between devices: none -> 47.6 us  [per_device(): received.append(lax.ppermute(pair_out[i], 'z', route))]
    ppermute x0 -> x7, starting transfers between devices: none -> 32.1 us  [per_device(): received.append(lax.ppermute(pair_out[i], 'z', route))]
    mul x0 -> x2, local copies, waits for them, and re-layouts: none -> 9.63 us  [per_device(): factor[..., None] * partial_out.astype(jnp.float32)]
    unnamed x5 -> x17, local copies, waits for them, and re-layouts: 0.11 us -> 5.85 us
    reshape x2 -> x1, local copies, waits for them, and re-layouts: 4.58 us -> 0.09 us  [per_device(): mine = jnp.stack(mine, axis=1).reshape(-1)]
    reduce_sum x1, other arithmetic: 0.67 us -> 4.76 us  [per_device(): jnp.sum(factor[..., None] * partial_out.astype(jnp.float32), axis=0)]
    pallas_call x1 -> x2, Pallas kernels: 32.4 us -> 36.5 us  [pair_partials(): pl.pallas_call(pair_kernel, grid_spec=grid_spec, out_shape=jax.ShapeDtype...]
  transfers between devices with their start and end apart: 5 -> 12, of which waited for: 4 -> 8; matrix products, arithmetic and copies ran while one was open for 3% -> 5% of each run, Pallas kernels for 0% -> 8%
where the time goes in v6:
time: 220 us; the launch traced here: 219 us
  waiting for transfers between devices  86.2 us (39%)
  starting transfers between devices  43.5 us (20%)
  Pallas kernels  36.5 us (17%)
  local copies, waits for them, and re-layouts  23.6 us (11%)
  other arithmetic  14.5 us (7%)
  between operations  14.4 us (7%)
    ppermute x7, waiting for transfers between devices, per_device(): received.append(lax.ppermute(pair_out[i], 'z', route))  47.6 us
    pallas_call x2, Pallas kernels, pair_partials(): pl.pallas_call(pair_kernel, grid_spec=grid_spec, out_shape=jax.ShapeDtype...  36.5 us
    ppermute x2, waiting for transfers between devices, passed_along(): return lax.ppermute(block, axis, route)  32.9 us
    ppermute x7, starting transfers between devices, per_device(): received.append(lax.ppermute(pair_out[i], 'z', route))  32.1 us
    mul x2, local copies, waits for them, and re-layouts, per_device(): factor[..., None] * partial_out.astype(jnp.float32)  9.63 us
    ppermute x2, starting transfers between devices, passed_along(): return lax.ppermute(block, axis, route)  7.43 us
    unnamed x17, local copies, waits for them, and re-layouts  5.85 us
    reduce_sum x1, other arithmetic, per_device(): jnp.sum(factor[..., None] * partial_out.astype(jnp.float32), axis=0)  4.76 us
  transfers between devices with their start and end apart: 12, of which 8 were waited for; matrix products, arithmetic and copies ran while one was open for 5% of the time, Pallas kernels for 8%

profile of v6, /device:TPU:32, one launch (start us, length us, event | category | flops | bytes accessed | tf_op | source)
XLA Modules:
  0.0 218.6 jit_solution(817968459122706624)
XLA Ops:
  6.5 0.1 iota_add_fusion
  7.3 0.9 and_reduce_fusion
  8.1 0.1 copy.17
  8.3 0.1 convert_element_type.28
  8.4 1.9 pad_maximum_fusion.4
  10.2 0.0 all-gather.2.cloned.1.call-update
  10.3 1.2 pad_maximum_fusion.3
  11.4 4.9 %collective-permute-start.1 = (bf16[2,128,1536]{2,1,0:T(8,128)(2,1)S(1)}, bf16[2,128,1536]{2,1,0:T(8,128)(2,1)S(1)}, u32[]{:S(2)}, u32[]{:S(2)}) collective-permute-start(bf16[2,128,1536]{2,1,0:T(8,128)(2,1)S(1)} %pad_maximum_fusion.3), channel_id=1, source_target_pairs={{0,32},{16,48},{32,64},{48,80},{64,96},{80,112},{96,128},{112,144}... | collective-permute-start | bytes 2359304 | tf_op jit(solution)/shard_map/ppermute | solution.py:22
  16.4 2.5 %collective-permute-start = (bf16[2,128,1536]{2,1,0:T(8,128)(2,1)S(1)}, bf16[2,128,1536]{2,1,0:T(8,128)(2,1)S(1)}, u32[]{:S(2)}, u32[]{:S(2)}) collective-permute-start(bf16[2,128,1536]{2,1,0:T(8,128)(2,1)S(1)} %pad_maximum_fusion.3), channel_id=1, source_target_pairs={{0,16},{16,32},{32,48},{48,64},{64,80},{80,96},{96,112},{112,128},... | collective-permute-start | bytes 2359304 | tf_op jit(solution)/shard_map/ppermute | solution.py:22
  18.9 1.9 collective-permute-start.2
  20.9 15.8 %collective-permute-done.1 = bf16[2,128,1536]{2,1,0:T(8,128)(2,1)S(1)} collective-permute-done((bf16[2,128,1536]{2,1,0:T(8,128)(2,1)S(1)}, bf16[2,128,1536]{2,1,0:T(8,128)(2,1)S(1)}, u32[]{:S(2)}, u32[]{:S(2)}) %collective-permute-start.1) | collective-permute-done | bytes 786464 | tf_op jit(solution)/shard_map/ppermute | solution.py:22
  36.6 17.1 %collective-permute-done = bf16[2,128,1536]{2,1,0:T(8,128)(2,1)S(1)} collective-permute-done((bf16[2,128,1536]{2,1,0:T(8,128)(2,1)S(1)}, bf16[2,128,1536]{2,1,0:T(8,128)(2,1)S(1)}, u32[]{:S(2)}, u32[]{:S(2)}) %collective-permute-start) | collective-permute-done | bytes 786464 | tf_op jit(solution)/shard_map/ppermute | solution.py:22
  53.7 0.1 pad_maximum_fusion.2
  53.9 0.0 copy-start.2
  53.9 0.0 copy-start.3
  53.9 2.1 collective-permute-start.3
  56.0 0.1 slice_bitcast_fusion.10
  56.0 0.1 slice_bitcast_fusion.11
  56.1 0.2 maximum_bitcast_fusion
  56.3 0.0 collective-permute-done.2
  56.3 0.1 slice_bitcast_fusion.9
  56.3 3.0 %collective-permute-done.3 = bf16[2,2,128,1536]{3,2,1,0:T(8,128)(2,1)S(1)} collective-permute-done((bf16[2,2,128,1536]{3,2,1,0:T(8,128)(2,1)S(1)}, bf16[2,2,128,1536]{3,2,1,0:T(8,128)(2,1)S(1)}, u32[]{:S(2)}, u32[]{:S(2)}) %collective-permute-start.3) | collective-permute-done | bytes 1572896 | tf_op jit(solution)/shard_map/ppermute | solution.py:136
  59.3 0.1 slice_bitcast_fusion.8
  59.4 0.2 maximum_bitcast_fusion.1
  59.6 1.6 pad_maximum_fusion.k_ref
  61.2 1.6 pad_maximum_fusion.1.v_ref
  62.9 2.7 %all-gather.2.cloned.1.call-done.q_ref = bf16[1024,1664]{1,0:T(8,128)(2,1)} async-done(((bf16[128,1664]{1,0:T(8,128)(2,1)}), bf16[1024,1664]{1,0:T(8,128)(2,1)}) %all-gather.2.cloned.1.call-update) | async-done | bytes 3407888 | tf_op jit(solution)/shard_map/all_gather | solution.py:156
  65.5 0.7 slice.106
  66.2 0.1 copy.24
  66.4 0.1 copy.19
  66.5 0.1 reshape.74
  66.6 0.7 concatenate.29.info_ref
  67.3 0.6 concatenate.24.info_ref
  67.9 18.2 %shard_map.55 = bf16[4,128,1664]{2,1,0:T(8,128)(2,1)} custom-call(s32[52]{0:T(128)} %concatenate.24.info_ref, bf16[1024,1664]{1,0:T(8,128)(2,1)} %all-gather.2.cloned.1.call-done.q_ref, bf16[2,384,1536]{2,1,0:T(8,128)(2,1)} %pad_maximum_fusion.k_ref, bf16[2,384,1536]{2,1,0:T(8,128)(2,1)} %pad_maximum_fusion.1.v_ref), custom_call_target="tpu_custom_call" | custom-call | flops 1610612736 | bytes 8126464 | tf_op jit(solution)/shard_map/pallas_call | solution.py:106
  86.1 2.5 %slice_bitcast_fusion.3 = (bf16[128,1664]{1,0:T(8,128)(2,1)}, bf16[128,1664]{1,0:T(8,128)(2,1)}, bf16[128,1664]{1,0:T(8,128)(2,1)}, bf16[128,1664]{1,0:T(8,128)(2,1)S(1)}) fusion(bf16[4,128,1664]{2,1,0:T(8,128)(2,1)} %shard_map.55), kind=kLoop, calls=%fused_computation.19 | loop fusion | bytes 3407872 | tf_op jit(solution)/shard_map/squeeze | solution.py:180
  88.6 3.4 %collective-permute-start.4 = (bf16[128,1664]{1,0:T(8,128)(2,1)S(1)}, bf16[128,1664]{1,0:T(8,128)(2,1)S(1)}, u32[]{:S(2)}, u32[]{:S(2)}) collective-permute-start(bf16[128,1664]{1,0:T(8,128)(2,1)S(1)} %get-tuple-element.14), channel_id=1, source_target_pairs={{0,4},{2,6},{4,8},{6,10},{8,12},{10,14},{12,0},{14,2},{1,5},{3,7},... | collective-permute-start | bytes 1277960 | tf_op jit(solution)/shard_map/ppermute | solution.py:180
  92.0 8.2 %collective-permute-start.5 = (bf16[128,1664]{1,0:T(8,128)(2,1)}, bf16[128,1664]{1,0:T(8,128)(2,1)}, u32[]{:S(2)}, u32[]{:S(2)}) collective-permute-start(bf16[128,1664]{1,0:T(8,128)(2,1)} %get-tuple-element.13), channel_id=1, source_target_pairs={{0,6},{2,8},{4,10},{6,12},{8,14},{10,0},{12,2},{14,4},{1,7},{3,9},... | collective-permute-start | bytes 1277960 | tf_op jit(solution)/shard_map/ppermute | solution.py:180
  100.2 3.7 %collective-permute-start.6 = (bf16[128,1664]{1,0:T(8,128)(2,1)}, bf16[128,1664]{1,0:T(8,128)(2,1)}, u32[]{:S(2)}, u32[]{:S(2)}) collective-permute-start(bf16[128,1664]{1,0:T(8,128)(2,1)} %get-tuple-element.12), channel_id=1, source_target_pairs={{0,8},{2,10},{4,12},{6,14},{8,0},{10,2},{12,4},{14,6},{1,9},{3,11}... | collective-permute-start | bytes 1277960 | tf_op jit(solution)/shard_map/ppermute | solution.py:180
  104.0 6.0 %collective-permute-start.7 = (bf16[128,1664]{1,0:T(8,128)(2,1)}, bf16[128,1664]{1,0:T(8,128)(2,1)}, u32[]{:S(2)}, u32[]{:S(2)}) collective-permute-start(bf16[128,1664]{1,0:T(8,128)(2,1)} %get-tuple-element.11), channel_id=1, source_target_pairs={{0,10},{2,12},{4,14},{6,0},{8,2},{10,4},{12,6},{14,8},{1,11},{3,13... | collective-permute-start | bytes 1277960 | tf_op jit(solution)/shard_map/ppermute | solution.py:180
  110.0 18.2 %shard_map.56 = bf16[4,128,1664]{2,1,0:T(8,128)(2,1)} custom-call(s32[52]{0:T(128)} %concatenate.29.info_ref, bf16[1024,1664]{1,0:T(8,128)(2,1)} %all-gather.2.cloned.1.call-done.q_ref, bf16[2,384,1536]{2,1,0:T(8,128)(2,1)} %pad_maximum_fusion.k_ref, bf16[2,384,1536]{2,1,0:T(8,128)(2,1)} %pad_maximum_fusion.1.v_ref), custom_call_target="tpu_custom_call" | custom-call | flops 1610612736 | bytes 8126464 | tf_op jit(solution)/shard_map/pallas_call | solution.py:106
  128.2 1.2 slice_bitcast_fusion.1
  129.4 3.7 %collective-permute-start.8 = (bf16[128,1664]{1,0:T(8,128)(2,1)S(1)}, bf16[128,1664]{1,0:T(8,128)(2,1)S(1)}, u32[]{:S(2)}, u32[]{:S(2)}) collective-permute-start(bf16[128,1664]{1,0:T(8,128)(2,1)S(1)} %get-tuple-element.10), channel_id=1, source_target_pairs={{0,12},{2,14},{4,0},{6,2},{8,4},{10,6},{12,8},{14,10},{1,13},{3,15... | collective-permute-start | bytes 1277960 | tf_op jit(solution)/shard_map/ppermute | solution.py:180
  133.1 0.8 copy-done.4
  133.9 2.0 collective-permute-start.9
  136.0 1.0 bitcast_dynamic-update-slice_fusion.6
  137.0 17.7 %collective-permute-done.5 = bf16[128,1664]{1,0:T(8,128)(2,1)} collective-permute-done((bf16[128,1664]{1,0:T(8,128)(2,1)}, bf16[128,1664]{1,0:T(8,128)(2,1)}, u32[]{:S(2)}, u32[]{:S(2)}) %collective-permute-start.5) | collective-permute-done | bytes 426016 | tf_op jit(solution)/shard_map/ppermute | solution.py:180
  154.7 1.0 bitcast_dynamic-update-slice_fusion.5
  155.8 1.0 bitcast_dynamic-update-slice_fusion.4
  156.8 1.0 bitcast_dynamic-update-slice_fusion.3
  157.9 13.5 %collective-permute-done.8 = bf16[128,1664]{1,0:T(8,128)(2,1)S(1)} collective-permute-done((bf16[128,1664]{1,0:T(8,128)(2,1)S(1)}, bf16[128,1664]{1,0:T(8,128)(2,1)S(1)}, u32[]{:S(2)}, u32[]{:S(2)}) %collective-permute-start.8) | collective-permute-done | bytes 426016 | tf_op jit(solution)/shard_map/ppermute | solution.py:180
  171.4 6.8 %collective-permute-done.9 = bf16[128,1664]{1,0:T(8,128)(2,1)S(1)} collective-permute-done((bf16[128,1664]{1,0:T(8,128)(2,1)S(1)}, bf16[128,1664]{1,0:T(8,128)(2,1)S(1)}, u32[]{:S(2)}, u32[]{:S(2)}) %collective-permute-start.9) | collective-permute-done | bytes 426016 | tf_op jit(solution)/shard_map/ppermute | solution.py:180
  178.3 0.1 slice_bitcast_fusion
  178.4 5.0 %collective-permute-start.10 = (bf16[128,1664]{1,0:T(8,128)(2,1)S(1)}, bf16[128,1664]{1,0:T(8,128)(2,1)S(1)}, u32[]{:S(2)}, u32[]{:S(2)}) collective-permute-start(bf16[128,1664]{1,0:T(8,128)(2,1)S(1)} %get-tuple-element.7), channel_id=1, source_target_pairs={{0,2},{2,4},{4,6},{6,8},{8,10},{10,12},{12,14},{14,0},{1,3},{3,5},... | collective-permute-start | bytes 1277960 | tf_op jit(solution)/shard_map/ppermute | solution.py:180
  183.4 9.6 %collective-permute-done.10 = bf16[128,1664]{1,0:T(8,128)(2,1)S(1)} collective-permute-done((bf16[128,1664]{1,0:T(8,128)(2,1)S(1)}, bf16[128,1664]{1,0:T(8,128)(2,1)S(1)}, u32[]{:S(2)}, u32[]{:S(2)}) %collective-permute-start.10) | collective-permute-done | bytes 426016 | tf_op jit(solution)/shard_map/ppermute | solution.py:180
  193.1 1.1 fusion.1
  194.2 1.2 copy.20
  195.4 3.0 %mul.28 = f32[8,128,12,128]{1,3,2,0:T(8,128)} broadcast(f32[8,128,12]{1,2,0:T(8,128)S(1)} %copy.20), dimensions={0,1,2} | broadcast | bytes 6340608 | tf_op jit(solution)/shard_map/mul | solution.py:189
  198.4 6.6 %copy.21 = f32[8,128,1536]{2,1,0:T(8,128)} copy(f32[8,128,1536]{1,2,0:T(8,128)} %bitcast.70) | data formatting | bytes 12582912 | tf_op jit(solution)/shard_map/mul | solution.py:189
  205.0 4.8 %multiply_reduce_fusion = f32[128,1536]{1,0:T(8,128)} fusion(f32[8,128,1536]{2,1,0:T(8,128)} %copy.21, bf16[8,128,1664]{2,1,0:T(8,128)(2,1)S(1)} %bitcast_dynamic-update-slice_fusion), kind=kLoop, calls=%fused_computation | loop fusion | flops 4521984 | bytes 10223616 | tf_op jit(solution)/shard_map/reduce_sum | solution.py:189
  209.8 0.1 copy.22
  209.8 0.1 div.11
  209.9 0.3 copy.23
  210.2 0.7 copy-done.1
  210.9 0.9 divide_convert_fusion
  (22 shorter events, 0.3 us)
Async XLA Ops:
  6.5 59.0 %all-gather.2.cloned.1.call-start = ((), (), s32[]{:S(2)}) async-start(), calls=%async_computation | async-start | bytes 3833856 | tf_op jit(solution)/shard_map/all_gather | solution.py:156
  11.4 25.2 %collective-permute-start.1 = (bf16[2,128,1536]{2,1,0:T(8,128)(2,1)S(1)}, bf16[2,128,1536]{2,1,0:T(8,128)(2,1)S(1)}, u32[]{:S(2)}, u32[]{:S(2)}) collective-permute-start(bf16[2,128,1536]{2,1,0:T(8,128)(2,1)S(1)} %pad_maximum_fusion.3), channel_id=1, source_target_pairs={{0,32},{16,48},{32,64},{48,80},{64,96},{80,112},{96,128},{112,144}... | collective-permute-start | bytes 2359304 | tf_op jit(solution)/shard_map/ppermute | solution.py:22
  16.4 37.3 %collective-permute-start = (bf16[2,128,1536]{2,1,0:T(8,128)(2,1)S(1)}, bf16[2,128,1536]{2,1,0:T(8,128)(2,1)S(1)}, u32[]{:S(2)}, u32[]{:S(2)}) collective-permute-start(bf16[2,128,1536]{2,1,0:T(8,128)(2,1)S(1)} %pad_maximum_fusion.3), channel_id=1, source_target_pairs={{0,16},{16,32},{32,48},{48,64},{64,80},{80,96},{96,112},{112,128},... | collective-permute-start | bytes 2359304 | tf_op jit(solution)/shard_map/ppermute | solution.py:22
  18.9 37.4 %collective-permute-start.2 = (bf16[2,128,1536]{2,1,0:T(8,128)(2,1)S(1)}, bf16[2,128,1536]{2,1,0:T(8,128)(2,1)S(1)}, u32[]{:S(2)}, u32[]{:S(2)}) collective-permute-start(bf16[2,128,1536]{2,1,0:T(8,128)(2,1)S(1)} %pad_maximum_fusion.3), channel_id=1, source_target_pairs={{0,1},{1,0},{2,3},{3,2},{4,5},{5,4},{6,7},{7,6},{8,9},{9,8},{10,11... | collective-permute-start | bytes 2359304 | tf_op jit(solution)/shard_map/ppermute | solution.py:135
  53.9 2.2 %copy-start.2 = (bf16[128,1536]{1,0:T(8,128)(2,1)S(1)}, bf16[128,1536]{1,0:T(8,128)(2,1)}, u32[]{:S(2)}) copy-start(bf16[128,1536]{1,0:T(8,128)(2,1)} %param.7) | copy-start | bytes 1179652
  53.9 2.2 %copy-start.3 = (bf16[128,1536]{1,0:T(8,128)(2,1)S(1)}, bf16[128,1536]{1,0:T(8,128)(2,1)}, u32[]{:S(2)}) copy-start(bf16[128,1536]{1,0:T(8,128)(2,1)} %param.6) | copy-start | bytes 1179652
  53.9 5.4 %collective-permute-start.3 = (bf16[2,2,128,1536]{3,2,1,0:T(8,128)(2,1)S(1)}, bf16[2,2,128,1536]{3,2,1,0:T(8,128)(2,1)S(1)}, u32[]{:S(2)}, u32[]{:S(2)}) collective-permute-start(bf16[2,2,128,1536]{3,2,1,0:T(8,128)(2,1)S(1)} %pad_maximum_fusion.2), channel_id=1, source_target_pairs={{0,1},{1,0},{2,3},{3,2},{4,5},{5,4},{6,7},{7,6},{8,9},{9,8},{10,11... | collective-permute-start | bytes 4718600 | tf_op jit(solution)/shard_map/ppermute | solution.py:136
  88.6 44.5 %collective-permute-start.4 = (bf16[128,1664]{1,0:T(8,128)(2,1)S(1)}, bf16[128,1664]{1,0:T(8,128)(2,1)S(1)}, u32[]{:S(2)}, u32[]{:S(2)}) collective-permute-start(bf16[128,1664]{1,0:T(8,128)(2,1)S(1)} %get-tuple-element.14), channel_id=1, source_target_pairs={{0,4},{2,6},{4,8},{6,10},{8,12},{10,14},{12,0},{14,2},{1,5},{3,7},... | collective-permute-start | bytes 1277960 | tf_op jit(solution)/shard_map/ppermute | solution.py:180
  92.0 62.7 %collective-permute-start.5 = (bf16[128,1664]{1,0:T(8,128)(2,1)}, bf16[128,1664]{1,0:T(8,128)(2,1)}, u32[]{:S(2)}, u32[]{:S(2)}) collective-permute-start(bf16[128,1664]{1,0:T(8,128)(2,1)} %get-tuple-element.13), channel_id=1, source_target_pairs={{0,6},{2,8},{4,10},{6,12},{8,14},{10,0},{12,2},{14,4},{1,7},{3,9},... | collective-permute-start | bytes 1277960 | tf_op jit(solution)/shard_map/ppermute | solution.py:180
  100.2 55.5 %collective-permute-start.6 = (bf16[128,1664]{1,0:T(8,128)(2,1)}, bf16[128,1664]{1,0:T(8,128)(2,1)}, u32[]{:S(2)}, u32[]{:S(2)}) collective-permute-start(bf16[128,1664]{1,0:T(8,128)(2,1)} %get-tuple-element.12), channel_id=1, source_target_pairs={{0,8},{2,10},{4,12},{6,14},{8,0},{10,2},{12,4},{14,6},{1,9},{3,11}... | collective-permute-start | bytes 1277960 | tf_op jit(solution)/shard_map/ppermute | solution.py:180
  104.0 52.8 %collective-permute-start.7 = (bf16[128,1664]{1,0:T(8,128)(2,1)}, bf16[128,1664]{1,0:T(8,128)(2,1)}, u32[]{:S(2)}, u32[]{:S(2)}) collective-permute-start(bf16[128,1664]{1,0:T(8,128)(2,1)} %get-tuple-element.11), channel_id=1, source_target_pairs={{0,10},{2,12},{4,14},{6,0},{8,2},{10,4},{12,6},{14,8},{1,11},{3,13... | collective-permute-start | bytes 1277960 | tf_op jit(solution)/shard_map/ppermute | solution.py:180
  129.4 42.0 %collective-permute-start.8 = (bf16[128,1664]{1,0:T(8,128)(2,1)S(1)}, bf16[128,1664]{1,0:T(8,128)(2,1)S(1)}, u32[]{:S(2)}, u32[]{:S(2)}) collective-permute-start(bf16[128,1664]{1,0:T(8,128)(2,1)S(1)} %get-tuple-element.10), channel_id=1, source_target_pairs={{0,12},{2,14},{4,0},{6,2},{8,4},{10,6},{12,8},{14,10},{1,13},{3,15... | collective-permute-start | bytes 1277960 | tf_op jit(solution)/shard_map/ppermute | solution.py:180
  133.1 0.8 copy-start.4
  133.9 44.4 %copy-start = (bf16[4,128,1664]{2,1,0:T(8,128)(2,1)S(1)}, bf16[4,128,1664]{2,1,0:T(8,128)(2,1)}, u32[]{:S(2)}) copy-start(bf16[4,128,1664]{2,1,0:T(8,128)(2,1)} %shard_map.56) | copy-start | bytes 5111812
  133.9 44.4 %collective-permute-start.9 = (bf16[128,1664]{1,0:T(8,128)(2,1)S(1)}, bf16[128,1664]{1,0:T(8,128)(2,1)S(1)}, u32[]{:S(2)}, u32[]{:S(2)}) collective-permute-start(bf16[128,1664]{1,0:T(8,128)(2,1)S(1)} %get-tuple-element.9), channel_id=1, source_target_pairs={{0,14},{2,0},{4,2},{6,4},{8,6},{10,8},{12,10},{14,12},{1,15},{3,1}... | collective-permute-start | bytes 1277960 | tf_op jit(solution)/shard_map/ppermute | solution.py:180
  178.4 14.5 %collective-permute-start.10 = (bf16[128,1664]{1,0:T(8,128)(2,1)S(1)}, bf16[128,1664]{1,0:T(8,128)(2,1)S(1)}, u32[]{:S(2)}, u32[]{:S(2)}) collective-permute-start(bf16[128,1664]{1,0:T(8,128)(2,1)S(1)} %get-tuple-element.7), channel_id=1, source_target_pairs={{0,2},{2,4},{4,6},{6,8},{8,10},{10,12},{12,14},{14,0},{1,3},{3,5},... | collective-permute-start | bytes 1277960 | tf_op jit(solution)/shard_map/ppermute | solution.py:180
  209.8 1.1 copy-start.1
Sparse Core Ops, SparseCore 0:
  10.4 55.0 all-gather.1

commit v7 on v5

--- a/solution.py
+++ b/solution.py
@@ -19,6 +19,22 @@
     devices = range(lax.axis_size(axis))
     route = [(i - distance, i) for i in devices if i - distance in devices]
     return lax.ppermute(block, axis, route)
+
+
+def split_parts(value, count):
+    parts = []
+    for _ in range(count - 1):
+        upper = value.astype(jnp.bfloat16).astype(jnp.float32)
+        parts.append(upper)
+        value = value - upper
+    return parts + [value]
+
+
+def joined(parts, head_count):
+    total = parts[..., :head_count]
+    for part in range(1, parts.shape[-1] // head_count):
+        total = total + parts[..., part * head_count : (part + 1) * head_count]
+    return total
 
 
 def pair_kernel(info_ref, q_ref, k_ref, v_ref, out_ref, stat_ref):
@@ -60,7 +76,6 @@
         highest = jnp.maximum(
             jnp.max(scores[0], axis=1, keepdims=True), jnp.max(scores[1], axis=1, keepdims=True)
         )
-        highest = (highest + jnp.abs(highest) * (2.0**-7)).astype(jnp.bfloat16).astype(jnp.float32)
         total = None
         blended = None
         for j in range(2):
@@ -74,8 +89,8 @@
             total = part_total if total is None else total + part_total
             blended = part if blended is None else blended + part
         out_ref[:, cols] = blended.astype(jnp.bfloat16)
-        stat_ref[:, h : h + 1] = highest
-        stat_ref[:, head_count + h : head_count + h + 1] = total
+        for part, value in enumerate(split_parts(highest, 3) + split_parts(total, 2)):
+            stat_ref[:, part * head_count + h : part * head_count + h + 1] = value
     out_ref[:, feature_width:] = stat_ref[...].astype(jnp.bfloat16)
 
 
@@ -162,8 +177,9 @@
     pair_out = lax.all_to_all(
         pair_out.reshape(chips, block_len, -1), "z", split_axis=0, concat_axis=0, tiled=True
     )
-    pair_stats = pair_out[..., feature_width : feature_width + 2 * head_count].astype(jnp.float32)
-    pair_max, pair_tot = pair_stats[..., :head_count], pair_stats[..., head_count:]
+    pair_stats = pair_out[..., feature_width : feature_width + 5 * head_count].astype(jnp.float32)
+    pair_max = joined(pair_stats[..., : 3 * head_count], head_count)
+    pair_tot = joined(pair_stats[..., 3 * head_count :], head_count)
     highest = jnp.max(pair_max, axis=0)
     factor = jnp.exp(pair_max - highest[None])
     denominator = jnp.sum(factor * pair_tot, axis=0)

time: 200 us -> 200 us (level)
  no operation moved by 1% of the time
where the time goes in v7:
time: 200 us
  blocking collectives  87.1 us (44%)
  waiting for transfers between devices  38.5 us (19%)
  Pallas kernels  32.3 us (16%)
  between operations  14.3 us (7%)
  starting transfers between devices  11.4 us (6%)
  other arithmetic  9.06 us (5%)
  local copies, waits for them, and re-layouts  6.92 us (3%)
    all_to_all x1, blocking collectives, per_device(): lax.all_to_all(pair_out.reshape(chips, block_len, -1), 'z', split_axis=0,...  87.1 us
    ppermute x2, waiting for transfers between devices, passed_along(): return lax.ppermute(block, axis, route)  32.9 us
    pallas_call x1, Pallas kernels, pair_partials(): pl.pallas_call(pair_kernel, grid_spec=grid_spec, out_shape=jax.ShapeDtype...  32.3 us
    ppermute x2, starting transfers between devices, passed_along(): return lax.ppermute(block, axis, route)  7.43 us
    reshape x1, local copies, waits for them, and re-layouts, per_device(): pair_out.reshape(chips, block_len, -1)  4.48 us
  transfers between devices with their start and end apart: 5, of which 4 were waited for; matrix products, arithmetic and copies ran while one was open for 3% of the time, Pallas kernels for 0%

profile of v7, /device:TPU:32, one launch (start us, length us, event | category | flops | bytes accessed | tf_op | source)
XLA Modules:
  0.0 199.5 jit_solution(4114240816803331953)
XLA Ops:
  6.5 0.0 all-gather.2.cloned.1.call-start
  7.2 0.1 iota_add_fusion
  7.3 0.9 and_reduce_fusion
  8.2 0.1 copy.10
  8.3 0.1 convert_element_type.28
  8.4 1.8 pad_maximum_fusion.4
  10.2 0.0 all-gather.2.cloned.1.call-update
  10.2 1.2 pad_maximum_fusion.3
  11.4 4.9 %collective-permute-start.1 = (bf16[2,128,1536]{2,1,0:T(8,128)(2,1)S(1)}, bf16[2,128,1536]{2,1,0:T(8,128)(2,1)S(1)}, u32[]{:S(2)}, u32[]{:S(2)}) collective-permute-start(bf16[2,128,1536]{2,1,0:T(8,128)(2,1)S(1)} %pad_maximum_fusion.3), channel_id=1, source_target_pairs={{0,32},{16,48},{32,64},{48,80},{64,96},{80,112},{96,128},{112,144}... | collective-permute-start | bytes 2359304 | tf_op jit(solution)/shard_map/ppermute | solution.py:21
  16.3 2.5 %collective-permute-start = (bf16[2,128,1536]{2,1,0:T(8,128)(2,1)S(1)}, bf16[2,128,1536]{2,1,0:T(8,128)(2,1)S(1)}, u32[]{:S(2)}, u32[]{:S(2)}) collective-permute-start(bf16[2,128,1536]{2,1,0:T(8,128)(2,1)S(1)} %pad_maximum_fusion.3), channel_id=1, source_target_pairs={{0,16},{16,32},{32,48},{48,64},{64,80},{80,96},{96,112},{112,128},... | collective-permute-start | bytes 2359304 | tf_op jit(solution)/shard_map/ppermute | solution.py:21
  18.8 1.9 collective-permute-start.2
  20.8 15.8 %collective-permute-done.1 = bf16[2,128,1536]{2,1,0:T(8,128)(2,1)S(1)} collective-permute-done((bf16[2,128,1536]{2,1,0:T(8,128)(2,1)S(1)}, bf16[2,128,1536]{2,1,0:T(8,128)(2,1)S(1)}, u32[]{:S(2)}, u32[]{:S(2)}) %collective-permute-start.1) | collective-permute-done | bytes 786464 | tf_op jit(solution)/shard_map/ppermute | solution.py:21
  36.5 17.1 %collective-permute-done = bf16[2,128,1536]{2,1,0:T(8,128)(2,1)S(1)} collective-permute-done((bf16[2,128,1536]{2,1,0:T(8,128)(2,1)S(1)}, bf16[2,128,1536]{2,1,0:T(8,128)(2,1)S(1)}, u32[]{:S(2)}, u32[]{:S(2)}) %collective-permute-start) | collective-permute-done | bytes 786464 | tf_op jit(solution)/shard_map/ppermute | solution.py:21
  53.7 0.1 pad_maximum_fusion.2
  53.8 0.0 copy-start
  53.8 0.0 copy-start.1
  53.8 2.1 %collective-permute-start.3 = (bf16[2,2,128,1536]{3,2,1,0:T(8,128)(2,1)S(1)}, bf16[2,2,128,1536]{3,2,1,0:T(8,128)(2,1)S(1)}, u32[]{:S(2)}, u32[]{:S(2)}) collective-permute-start(bf16[2,2,128,1536]{3,2,1,0:T(8,128)(2,1)S(1)} %pad_maximum_fusion.2), channel_id=1, source_target_pairs={{0,1},{1,0},{2,3},{3,2},{4,5},{5,4},{6,7},{7,6},{8,9},{9,8},{10,11... | collective-permute-start | bytes 4718600 | tf_op jit(solution)/shard_map/ppermute | solution.py:143
  55.9 0.1 slice_bitcast_fusion.3
  55.9 0.1 slice_bitcast_fusion.4
  56.0 0.0 copy-done
  56.0 0.0 copy-done.1
  56.0 0.2 maximum_bitcast_fusion
  56.2 0.0 collective-permute-done.2
  56.2 0.1 slice_bitcast_fusion.2
  56.3 3.0 %collective-permute-done.3 = bf16[2,2,128,1536]{3,2,1,0:T(8,128)(2,1)S(1)} collective-permute-done((bf16[2,2,128,1536]{3,2,1,0:T(8,128)(2,1)S(1)}, bf16[2,2,128,1536]{3,2,1,0:T(8,128)(2,1)S(1)}, u32[]{:S(2)}, u32[]{:S(2)}) %collective-permute-start.3) | collective-permute-done | bytes 1572896 | tf_op jit(solution)/shard_map/ppermute | solution.py:143
  59.3 0.1 slice_bitcast_fusion.1
  59.4 0.2 maximum_bitcast_fusion.1
  59.5 1.7 pad_maximum_fusion.k_ref
  61.2 1.6 pad_maximum_fusion.1.v_ref
  62.8 2.6 %all-gather.2.cloned.1.call-done.q_ref = bf16[1024,1664]{1,0:T(8,128)(2,1)} async-done(((bf16[128,1664]{1,0:T(8,128)(2,1)}), bf16[1024,1664]{1,0:T(8,128)(2,1)}) %all-gather.2.cloned.1.call-update) | async-done | bytes 3407888 | tf_op jit(solution)/shard_map/all_gather | solution.py:163
  65.4 0.7 slice.89
  66.2 0.1 copy.15
  66.3 0.1 copy.12
  66.4 0.1 reshape.77
  66.5 0.6 pad_add_fusion.1.info_ref
  67.1 32.3 %shard_map.55 = bf16[1024,1664]{1,0:T(8,128)(2,1)} custom-call(s32[50]{0:T(128)} %pad_add_fusion.1.info_ref, bf16[1024,1664]{1,0:T(8,128)(2,1)} %all-gather.2.cloned.1.call-done.q_ref, bf16[2,384,1536]{2,1,0:T(8,128)(2,1)} %pad_maximum_fusion.k_ref, bf16[2,384,1536]{2,1,0:T(8,128)(2,1)} %pad_maximum_fusion.1.v_ref), custom_call_target="tpu_custom_call" | custom-call | flops 3221225472 | bytes 11534336 | tf_op jit(solution)/shard_map/pallas_call | solution.py:113
  99.3 4.5 %copy.13 = bf16[8,128,1664]{1,2,0:T(8,128)(2,1)S(1)} copy(bf16[8,128,1664]{2,1,0:T(8,128)(2,1)} %bitcast.49) | data formatting | bytes 6815744 | tf_op jit(solution)/shard_map/reshape | solution.py:178
  103.8 87.1 %all_to_all.5 = bf16[8,128,1664]{1,2,0:T(8,128)(2,1)S(1)} all-to-all(bf16[8,128,1664]{1,2,0:T(8,128)(2,1)S(1)} %copy.13), channel_id=1, replica_groups=mesh['pb'=32,'z'=8,'core'=2] {'z'}, dimensions={0} | all-to-all | bytes 6815744 | tf_op jit(solution)/shard_map/all_to_all | solution.py:177
  191.0 0.7 fusion
  191.7 0.1 fusion.1
  191.7 0.9 copy.14
  (10 shorter events, 0.1 us)
Async XLA Ops:
  6.5 58.9 %all-gather.2.cloned.1.call-start = ((), (), s32[]{:S(2)}) async-start(), calls=%async_computation.1 | async-start | bytes 3833856 | tf_op jit(solution)/shard_map/all_gather | solution.py:163
  11.4 25.2 %collective-permute-start.1 = (bf16[2,128,1536]{2,1,0:T(8,128)(2,1)S(1)}, bf16[2,128,1536]{2,1,0:T(8,128)(2,1)S(1)}, u32[]{:S(2)}, u32[]{:S(2)}) collective-permute-start(bf16[2,128,1536]{2,1,0:T(8,128)(2,1)S(1)} %pad_maximum_fusion.3), channel_id=1, source_target_pairs={{0,32},{16,48},{32,64},{48,80},{64,96},{80,112},{96,128},{112,144}... | collective-permute-start | bytes 2359304 | tf_op jit(solution)/shard_map/ppermute | solution.py:21
  16.3 37.3 %collective-permute-start = (bf16[2,128,1536]{2,1,0:T(8,128)(2,1)S(1)}, bf16[2,128,1536]{2,1,0:T(8,128)(2,1)S(1)}, u32[]{:S(2)}, u32[]{:S(2)}) collective-permute-start(bf16[2,128,1536]{2,1,0:T(8,128)(2,1)S(1)} %pad_maximum_fusion.3), channel_id=1, source_target_pairs={{0,16},{16,32},{32,48},{48,64},{64,80},{80,96},{96,112},{112,128},... | collective-permute-start | bytes 2359304 | tf_op jit(solution)/shard_map/ppermute | solution.py:21
  18.8 37.4 %collective-permute-start.2 = (bf16[2,128,1536]{2,1,0:T(8,128)(2,1)S(1)}, bf16[2,128,1536]{2,1,0:T(8,128)(2,1)S(1)}, u32[]{:S(2)}, u32[]{:S(2)}) collective-permute-start(bf16[2,128,1536]{2,1,0:T(8,128)(2,1)S(1)} %pad_maximum_fusion.3), channel_id=1, source_target_pairs={{0,1},{1,0},{2,3},{3,2},{4,5},{5,4},{6,7},{7,6},{8,9},{9,8},{10,11... | collective-permute-start | bytes 2359304 | tf_op jit(solution)/shard_map/ppermute | solution.py:142
  53.8 2.2 %copy-start = (bf16[128,1536]{1,0:T(8,128)(2,1)S(1)}, bf16[128,1536]{1,0:T(8,128)(2,1)}, u32[]{:S(2)}) copy-start(bf16[128,1536]{1,0:T(8,128)(2,1)} %param.7) | copy-start | bytes 1179652
  53.8 2.2 %copy-start.1 = (bf16[128,1536]{1,0:T(8,128)(2,1)S(1)}, bf16[128,1536]{1,0:T(8,128)(2,1)}, u32[]{:S(2)}) copy-start(bf16[128,1536]{1,0:T(8,128)(2,1)} %param.6) | copy-start | bytes 1179652
  53.8 5.4 %collective-permute-start.3 = (bf16[2,2,128,1536]{3,2,1,0:T(8,128)(2,1)S(1)}, bf16[2,2,128,1536]{3,2,1,0:T(8,128)(2,1)S(1)}, u32[]{:S(2)}, u32[]{:S(2)}) collective-permute-start(bf16[2,2,128,1536]{3,2,1,0:T(8,128)(2,1)S(1)} %pad_maximum_fusion.2), channel_id=1, source_target_pairs={{0,1},{1,0},{2,3},{3,2},{4,5},{5,4},{6,7},{7,6},{8,9},{9,8},{10,11... | collective-permute-start | bytes 4718600 | tf_op jit(solution)/shard_map/ppermute | solution.py:143
Sparse Core Ops, SparseCore 0:
  10.3 55.0 all-gather.1

commit v8 on v7

--- a/solution.py
+++ b/solution.py
@@ -96,14 +96,14 @@
 
 def pair_partials(info, row_q, key_window, value_window):
     block_len = key_window.shape[1] // LAGS
-    sources = row_q.shape[0] // block_len
+    sources = row_q.shape[0] // block_len // 2
     feature_width = key_window.shape[2]
     head_count = feature_width // DH
     grid_spec = pltpu.PrefetchScalarGridSpec(
         num_scalar_prefetch=1,
         grid=(sources,),
         in_specs=[
-            pl.BlockSpec((block_len, row_q.shape[1]), lambda t, info_ref: (t, 0)),
+            pl.BlockSpec((block_len, row_q.shape[1]), lambda t, info_ref: (2 * t + info_ref[1], 0)),
             pl.BlockSpec(key_window.shape, lambda t, info_ref: (0, 0, 0)),
             pl.BlockSpec(value_window.shape, lambda t, info_ref: (0, 0, 0)),
         ],
@@ -113,7 +113,7 @@
     return pl.pallas_call(
         pair_kernel,
         grid_spec=grid_spec,
-        out_shape=jax.ShapeDtypeStruct(row_q.shape, jnp.bfloat16),
+        out_shape=jax.ShapeDtypeStruct((sources * block_len, row_q.shape[1]), jnp.bfloat16),
         cost_estimate=pl.CostEstimate(
             flops=sources * head_count * 2 * 2 * 2 * block_len * 2 * block_len * DH,
             transcendentals=sources * head_count * 2 * 2 * block_len * block_len,
@@ -161,10 +161,11 @@
     spare = jnp.zeros((block_len, DH), jnp.bfloat16)
     spare = lax.dynamic_update_slice(spare, marks, (0, 0))
     row_q = lax.all_gather(
-        jnp.concatenate([queries, spare], axis=1), "z", axis=0, tiled=True
-    )
-    marks_all = row_q.reshape(chips, block_len, -1)[:, 0, feature_width : feature_width + stripe_count * LAGS]
-    marks_all = marks_all.reshape(chips, stripe_count, LAGS).astype(jnp.int32)
+        jnp.concatenate([queries, spare], axis=1), ("z", "core"), axis=0, tiled=True
+    )
+    marks_all = row_q.reshape(stripe_count, block_len, -1)[:, 0, feature_width : feature_width + stripe_count * LAGS]
+    marks_all = marks_all.reshape(chips, cores, stripe_count, LAGS).astype(jnp.int32)
+    marks_all = lax.dynamic_index_in_dim(marks_all, core, axis=1, keepdims=False)
     mine = [
         lax.dynamic_index_in_dim(marks_all, 2 * chip + (core + j) % 2, axis=1, keepdims=False)
         for j in range(2)

time: 200 us -> 201 us (level)
  no operation moved by 1% of the time
where the time goes in v8:
time: 201 us; the launch traced here: 200 us
  blocking collectives  86.4 us (43%)
  waiting for transfers between devices  39.6 us (20%)
  Pallas kernels  32.3 us (16%)
  between operations  14.3 us (7%)
  starting transfers between devices  11.4 us (6%)
  other arithmetic  9.1 us (5%)
  local copies, waits for them, and re-layouts  7.13 us (4%)
    all_to_all x1, blocking collectives, per_device(): lax.all_to_all(pair_out.reshape(chips, block_len, -1), 'z', split_axis=0,...  86.4 us
    ppermute x2, waiting for transfers between devices, passed_along(): return lax.ppermute(block, axis, route)  32.9 us
    pallas_call x1, Pallas kernels, pair_partials(): pl.pallas_call(pair_kernel, grid_spec=grid_spec, out_shape=jax.ShapeDtype...  32.3 us
    ppermute x2, starting transfers between devices, passed_along(): return lax.ppermute(block, axis, route)  7.43 us
    reshape x1, local copies, waits for them, and re-layouts, per_device(): pair_out.reshape(chips, block_len, -1)  4.48 us
  transfers between devices with their start and end apart: 5, of which 4 were waited for; matrix products, arithmetic and copies ran while one was open for 3% of the time, Pallas kernels for 0%

profile of v8, /device:TPU:32, one launch (start us, length us, event | category | flops | bytes accessed | tf_op | source)
XLA Modules:
  0.0 200.2 jit_solution(12387856511411437883)
XLA Ops:
  6.5 0.0 all-gather.2.cloned.1.call-start
  7.2 0.1 iota_add_fusion
  7.3 0.9 and_reduce_fusion
  8.2 0.1 copy.13
  8.3 0.1 convert_element_type.28
  8.4 1.8 pad_maximum_fusion.4
  10.2 0.0 all-gather.2.cloned.1.call-update
  10.2 1.2 pad_maximum_fusion.3
  11.4 4.9 %collective-permute-start.1 = (bf16[2,128,1536]{2,1,0:T(8,128)(2,1)S(1)}, bf16[2,128,1536]{2,1,0:T(8,128)(2,1)S(1)}, u32[]{:S(2)}, u32[]{:S(2)}) collective-permute-start(bf16[2,128,1536]{2,1,0:T(8,128)(2,1)S(1)} %pad_maximum_fusion.3), channel_id=1, source_target_pairs={{0,32},{16,48},{32,64},{48,80},{64,96},{80,112},{96,128},{112,144}... | collective-permute-start | bytes 2359304 | tf_op jit(solution)/shard_map/ppermute | solution.py:21
  16.3 2.5 %collective-permute-start = (bf16[2,128,1536]{2,1,0:T(8,128)(2,1)S(1)}, bf16[2,128,1536]{2,1,0:T(8,128)(2,1)S(1)}, u32[]{:S(2)}, u32[]{:S(2)}) collective-permute-start(bf16[2,128,1536]{2,1,0:T(8,128)(2,1)S(1)} %pad_maximum_fusion.3), channel_id=1, source_target_pairs={{0,16},{16,32},{32,48},{48,64},{64,80},{80,96},{96,112},{112,128},... | collective-permute-start | bytes 2359304 | tf_op jit(solution)/shard_map/ppermute | solution.py:21
  18.8 1.9 collective-permute-start.2
  20.8 15.8 %collective-permute-done.1 = bf16[2,128,1536]{2,1,0:T(8,128)(2,1)S(1)} collective-permute-done((bf16[2,128,1536]{2,1,0:T(8,128)(2,1)S(1)}, bf16[2,128,1536]{2,1,0:T(8,128)(2,1)S(1)}, u32[]{:S(2)}, u32[]{:S(2)}) %collective-permute-start.1) | collective-permute-done | bytes 786464 | tf_op jit(solution)/shard_map/ppermute | solution.py:21
  36.6 17.1 %collective-permute-done = bf16[2,128,1536]{2,1,0:T(8,128)(2,1)S(1)} collective-permute-done((bf16[2,128,1536]{2,1,0:T(8,128)(2,1)S(1)}, bf16[2,128,1536]{2,1,0:T(8,128)(2,1)S(1)}, u32[]{:S(2)}, u32[]{:S(2)}) %collective-permute-start) | collective-permute-done | bytes 786464 | tf_op jit(solution)/shard_map/ppermute | solution.py:21
  53.7 0.1 pad_maximum_fusion.2
  53.8 0.0 copy-start
  53.8 0.0 copy-start.1
  53.8 2.1 %collective-permute-start.3 = (bf16[2,2,128,1536]{3,2,1,0:T(8,128)(2,1)S(1)}, bf16[2,2,128,1536]{3,2,1,0:T(8,128)(2,1)S(1)}, u32[]{:S(2)}, u32[]{:S(2)}) collective-permute-start(bf16[2,2,128,1536]{3,2,1,0:T(8,128)(2,1)S(1)} %pad_maximum_fusion.2), channel_id=1, source_target_pairs={{0,1},{1,0},{2,3},{3,2},{4,5},{5,4},{6,7},{7,6},{8,9},{9,8},{10,11... | collective-permute-start | bytes 4718600 | tf_op jit(solution)/shard_map/ppermute | solution.py:143
  55.9 0.1 slice_bitcast_fusion.3
  56.0 0.1 slice_bitcast_fusion.4
  56.0 0.0 copy-done
  56.0 0.0 copy-done.1
  56.0 0.2 maximum_bitcast_fusion
  56.2 0.0 collective-permute-done.2
  56.2 0.1 slice_bitcast_fusion.2
  56.3 3.3 %collective-permute-done.3 = bf16[2,2,128,1536]{3,2,1,0:T(8,128)(2,1)S(1)} collective-permute-done((bf16[2,2,128,1536]{3,2,1,0:T(8,128)(2,1)S(1)}, bf16[2,2,128,1536]{3,2,1,0:T(8,128)(2,1)S(1)}, u32[]{:S(2)}, u32[]{:S(2)}) %collective-permute-start.3) | collective-permute-done | bytes 1572896 | tf_op jit(solution)/shard_map/ppermute | solution.py:143
  59.6 0.1 slice_bitcast_fusion.1
  59.7 0.2 maximum_bitcast_fusion.1
  59.9 1.6 pad_maximum_fusion.k_ref
  61.5 1.6 pad_maximum_fusion.1.v_ref
  63.1 3.4 %all-gather.2.cloned.1.call-done.q_ref = bf16[2048,1664]{1,0:T(8,128)(2,1)} async-done(((bf16[128,1664]{1,0:T(8,128)(2,1)}), bf16[2048,1664]{1,0:T(8,128)(2,1)}) %all-gather.2.cloned.1.call-update) | async-done | bytes 6815760 | tf_op jit(solution)/shard_map/all_gather | solution.py:163
  66.5 0.8 slice.89
  67.3 0.1 reshape.81
  67.4 0.1 copy.15
  67.5 0.1 copy.16
  67.6 0.1 copy.17
  67.7 0.1 reshape.79
  67.8 0.6 pad_add_fusion.1.info_ref
  68.4 32.3 %shard_map.55 = bf16[1024,1664]{1,0:T(8,128)(2,1)} custom-call(s32[50]{0:T(128)} %pad_add_fusion.1.info_ref, bf16[2048,1664]{1,0:T(8,128)(2,1)} %all-gather.2.cloned.1.call-done.q_ref, bf16[2,384,1536]{2,1,0:T(8,128)(2,1)} %pad_maximum_fusion.k_ref, bf16[2,384,1536]{2,1,0:T(8,128)(2,1)} %pad_maximum_fusion.1.v_ref), custom_call_target="tpu_custom_call" | custom-call | flops 3221225472 | bytes 11534336 | tf_op jit(solution)/shard_map/pallas_call | solution.py:113
  100.7 4.5 %copy.18 = bf16[8,128,1664]{1,2,0:T(8,128)(2,1)S(1)} copy(bf16[8,128,1664]{2,1,0:T(8,128)(2,1)} %bitcast.51) | data formatting | bytes 6815744 | tf_op jit(solution)/shard_map/reshape | solution.py:179
  105.2 86.4 %all_to_all.5 = bf16[8,128,1664]{1,2,0:T(8,128)(2,1)S(1)} all-to-all(bf16[8,128,1664]{1,2,0:T(8,128)(2,1)S(1)} %copy.18), channel_id=1, replica_groups=mesh['pb'=32,'z'=8,'core'=2] {'z'}, dimensions={0} | all-to-all | bytes 6815744 | tf_op jit(solution)/shard_map/all_to_all | solution.py:178
  191.6 0.7 fusion
  192.3 0.1 fusion.1
  192.4 0.9 copy.19
  (9 shorter events, 0.1 us)
Async XLA Ops:
  6.5 60.0 %all-gather.2.cloned.1.call-start = ((), (), s32[]{:S(2)}) async-start(), calls=%async_computation.1 | async-start | bytes 7241728 | tf_op jit(solution)/shard_map/all_gather | solution.py:163
  11.4 25.2 %collective-permute-start.1 = (bf16[2,128,1536]{2,1,0:T(8,128)(2,1)S(1)}, bf16[2,128,1536]{2,1,0:T(8,128)(2,1)S(1)}, u32[]{:S(2)}, u32[]{:S(2)}) collective-permute-start(bf16[2,128,1536]{2,1,0:T(8,128)(2,1)S(1)} %pad_maximum_fusion.3), channel_id=1, source_target_pairs={{0,32},{16,48},{32,64},{48,80},{64,96},{80,112},{96,128},{112,144}... | collective-permute-start | bytes 2359304 | tf_op jit(solution)/shard_map/ppermute | solution.py:21
  16.3 37.3 %collective-permute-start = (bf16[2,128,1536]{2,1,0:T(8,128)(2,1)S(1)}, bf16[2,128,1536]{2,1,0:T(8,128)(2,1)S(1)}, u32[]{:S(2)}, u32[]{:S(2)}) collective-permute-start(bf16[2,128,1536]{2,1,0:T(8,128)(2,1)S(1)} %pad_maximum_fusion.3), channel_id=1, source_target_pairs={{0,16},{16,32},{32,48},{48,64},{64,80},{80,96},{96,112},{112,128},... | collective-permute-start | bytes 2359304 | tf_op jit(solution)/shard_map/ppermute | solution.py:21
  18.8 37.4 %collective-permute-start.2 = (bf16[2,128,1536]{2,1,0:T(8,128)(2,1)S(1)}, bf16[2,128,1536]{2,1,0:T(8,128)(2,1)S(1)}, u32[]{:S(2)}, u32[]{:S(2)}) collective-permute-start(bf16[2,128,1536]{2,1,0:T(8,128)(2,1)S(1)} %pad_maximum_fusion.3), channel_id=1, source_target_pairs={{0,1},{1,0},{2,3},{3,2},{4,5},{5,4},{6,7},{7,6},{8,9},{9,8},{10,11... | collective-permute-start | bytes 2359304 | tf_op jit(solution)/shard_map/ppermute | solution.py:142
  53.8 2.2 %copy-start = (bf16[128,1536]{1,0:T(8,128)(2,1)S(1)}, bf16[128,1536]{1,0:T(8,128)(2,1)}, u32[]{:S(2)}) copy-start(bf16[128,1536]{1,0:T(8,128)(2,1)} %param.7) | copy-start | bytes 1179652
  53.8 2.2 %copy-start.1 = (bf16[128,1536]{1,0:T(8,128)(2,1)S(1)}, bf16[128,1536]{1,0:T(8,128)(2,1)}, u32[]{:S(2)}) copy-start(bf16[128,1536]{1,0:T(8,128)(2,1)} %param.6) | copy-start | bytes 1179652
  53.8 5.7 %collective-permute-start.3 = (bf16[2,2,128,1536]{3,2,1,0:T(8,128)(2,1)S(1)}, bf16[2,2,128,1536]{3,2,1,0:T(8,128)(2,1)S(1)}, u32[]{:S(2)}, u32[]{:S(2)}) collective-permute-start(bf16[2,2,128,1536]{3,2,1,0:T(8,128)(2,1)S(1)} %pad_maximum_fusion.2), channel_id=1, source_target_pairs={{0,1},{1,0},{2,3},{3,2},{4,5},{5,4},{6,7},{7,6},{8,9},{9,8},{10,11... | collective-permute-start | bytes 4718600 | tf_op jit(solution)/shard_map/ppermute | solution.py:143
Sparse Core Ops, SparseCore 0:
  10.3 56.1 all-gather.1

commit v9 on v7

--- a/solution.py
+++ b/solution.py
@@ -174,20 +174,56 @@
     )
 
     pair_out = pair_partials(info, row_q, key_window, value_window)
-    pair_out = lax.all_to_all(
-        pair_out.reshape(chips, block_len, -1), "z", split_axis=0, concat_axis=0, tiled=True
-    )
-    pair_stats = pair_out[..., feature_width : feature_width + 5 * head_count].astype(jnp.float32)
-    pair_max = joined(pair_stats[..., : 3 * head_count], head_count)
-    pair_tot = joined(pair_stats[..., 3 * head_count :], head_count)
-    highest = jnp.max(pair_max, axis=0)
-    factor = jnp.exp(pair_max - highest[None])
-    denominator = jnp.sum(factor * pair_tot, axis=0)
-    partial_out = pair_out[..., :feature_width].reshape(chips, block_len, head_count, DH)
-    numerator = jnp.sum(factor[..., None] * partial_out.astype(jnp.float32), axis=0)
-    return (
-        (numerator / denominator[..., None]).reshape(block_len, feature_width).astype(jnp.bfloat16)
-    )
+    pair_out = pair_out.reshape(chips, block_len, -1)
+
+    def decode(block):
+        stats = block[:, feature_width : feature_width + 5 * head_count].astype(jnp.float32)
+        values = block[:, :feature_width].astype(jnp.float32).reshape(block_len, head_count, DH)
+        return values, joined(stats[:, : 3 * head_count], head_count), joined(
+            stats[:, 3 * head_count :], head_count
+        )
+
+    def merged(blocks):
+        decoded = [decode(b) for b in blocks]
+        top = decoded[0][1]
+        for _, m, _ in decoded[1:]:
+            top = jnp.maximum(top, m)
+        values = None
+        total = None
+        for v, m, l in decoded:
+            f = jnp.exp(m - top)
+            values = f[..., None] * v if values is None else values + f[..., None] * v
+            total = f * l if total is None else total + f * l
+        return values, top, total
+
+    def encoded(values, top, total):
+        parts = split_parts(top, 3) + split_parts(total, 2)
+        spare = jnp.zeros((block_len, DH - 5 * head_count), jnp.float32)
+        stats = jnp.concatenate(parts + [spare], axis=1)
+        return jnp.concatenate(
+            [values.reshape(block_len, feature_width), stats], axis=1
+        ).astype(jnp.bfloat16)
+
+    def block_for(offset):
+        return lax.dynamic_index_in_dim(pair_out, (chip + offset) % chips, axis=0, keepdims=False)
+
+    rightward = [(z, (z + 1) % chips) for z in range(chips)]
+    leftward = [(z, (z - 1) % chips) for z in range(chips)]
+    reach_r = chips // 2
+    reach_l = chips - 1 - reach_r
+    acc_r = block_for(reach_r)
+    acc_l = block_for(-reach_l)
+    for step in range(1, reach_r):
+        acc_r = encoded(*merged([lax.ppermute(acc_r, "z", rightward), block_for(reach_r - step)]))
+        if step < reach_l:
+            acc_l = encoded(
+                *merged([lax.ppermute(acc_l, "z", leftward), block_for(step - reach_l)])
+            )
+    final = [block_for(0), lax.ppermute(acc_r, "z", rightward)]
+    if reach_l > 0:
+        final.append(lax.ppermute(acc_l, "z", leftward))
+    values, top, total = merged(final)
+    return (values / total[..., None]).reshape(block_len, feature_width).astype(jnp.bfloat16)
 
 
 def solution(mesh):

time: 200 us -> 187 us (0.935)
  the two profiles are of different devices: /device:TPU:32 before, /device:TPU:50 now
where the time goes in v9:
time: 187 us; the launch traced here: 186 us
  waiting for transfers between devices  73 us (39%)
  starting transfers between devices  39.9 us (21%)
  Pallas kernels  32.2 us (17%)
  other arithmetic  15.9 us (9%)
  between operations  14.7 us (8%)
  local copies, waits for them, and re-layouts  10.6 us (6%)
    ppermute x2, waiting for transfers between devices, passed_along(): return lax.ppermute(block, axis, route)  44.8 us
    pallas_call x1, Pallas kernels, pair_partials(): pl.pallas_call(pair_kernel, grid_spec=grid_spec, out_shape=jax.ShapeDtype...  32.2 us
    ppermute x2, starting transfers between devices, per_device(): lax.ppermute(acc_l, 'z', leftward)  13.7 us
    ppermute x3, waiting for transfers between devices, per_device(): lax.ppermute(acc_r, 'z', rightward)  12.6 us
    ppermute x1, waiting for transfers between devices, per_device(): final = [block_for(0), lax.ppermute(acc_r, 'z', rightward)]  9.27 us
    ppermute x3, starting transfers between devices, per_device(): lax.ppermute(acc_r, 'z', rightward)  8.11 us
    ppermute x2, starting transfers between devices, passed_along(): return lax.ppermute(block, axis, route)  6.53 us
    ppermute x1, starting transfers between devices, per_device(): final.append(lax.ppermute(acc_l, 'z', leftward))  5.6 us
  transfers between devices with their start and end apart: 12, of which 9 were waited for; matrix products, arithmetic and copies ran while one was open for 9% of the time, Pallas kernels for 0%

profile of v9, /device:TPU:50, one launch (start us, length us, event | category | flops | bytes accessed | tf_op | source)
XLA Modules:
  0.0 186.3 jit_solution(14282277258597654532)
XLA Ops:
  7.3 0.9 and_reduce_fusion
  8.1 0.1 copy.17
  8.3 0.1 convert_element_type.194
  8.4 1.8 pad_maximum_fusion.4
  10.2 1.2 pad_maximum_fusion.3
  11.4 3.4 %collective-permute-start = (bf16[2,128,1536]{2,1,0:T(8,128)(2,1)S(1)}, bf16[2,128,1536]{2,1,0:T(8,128)(2,1)S(1)}, u32[]{:S(2)}, u32[]{:S(2)}) collective-permute-start(bf16[2,128,1536]{2,1,0:T(8,128)(2,1)S(1)} %pad_maximum_fusion.3), channel_id=1, source_target_pairs={{0,16},{16,32},{32,48},{48,64},{64,80},{80,96},{96,112},{112,128},... | collective-permute-start | bytes 2359304 | tf_op jit(solution)/shard_map/ppermute | solution.py:21
  14.8 3.1 %collective-permute-start.1 = (bf16[2,128,1536]{2,1,0:T(8,128)(2,1)S(1)}, bf16[2,128,1536]{2,1,0:T(8,128)(2,1)S(1)}, u32[]{:S(2)}, u32[]{:S(2)}) collective-permute-start(bf16[2,128,1536]{2,1,0:T(8,128)(2,1)S(1)} %pad_maximum_fusion.3), channel_id=1, source_target_pairs={{0,32},{16,48},{32,64},{48,80},{64,96},{80,112},{96,128},{112,144}... | collective-permute-start | bytes 2359304 | tf_op jit(solution)/shard_map/ppermute | solution.py:21
  17.9 1.9 %collective-permute-start.2 = (bf16[2,128,1536]{2,1,0:T(8,128)(2,1)S(1)}, bf16[2,128,1536]{2,1,0:T(8,128)(2,1)S(1)}, u32[]{:S(2)}, u32[]{:S(2)}) collective-permute-start(bf16[2,128,1536]{2,1,0:T(8,128)(2,1)S(1)} %pad_maximum_fusion.3), channel_id=1, source_target_pairs={{0,1},{1,0},{2,3},{3,2},{4,5},{5,4},{6,7},{7,6},{8,9},{9,8},{10,11... | collective-permute-start | bytes 2359304 | tf_op jit(solution)/shard_map/ppermute | solution.py:142
  20.0 13.7 %collective-permute-done = bf16[2,128,1536]{2,1,0:T(8,128)(2,1)S(1)} collective-permute-done((bf16[2,128,1536]{2,1,0:T(8,128)(2,1)S(1)}, bf16[2,128,1536]{2,1,0:T(8,128)(2,1)S(1)}, u32[]{:S(2)}, u32[]{:S(2)}) %collective-permute-start) | collective-permute-done | bytes 786464 | tf_op jit(solution)/shard_map/ppermute | solution.py:21
  33.7 31.2 %collective-permute-done.1 = bf16[2,128,1536]{2,1,0:T(8,128)(2,1)S(1)} collective-permute-done((bf16[2,128,1536]{2,1,0:T(8,128)(2,1)S(1)}, bf16[2,128,1536]{2,1,0:T(8,128)(2,1)S(1)}, u32[]{:S(2)}, u32[]{:S(2)}) %collective-permute-start.1) | collective-permute-done | bytes 786464 | tf_op jit(solution)/shard_map/ppermute | solution.py:21
  64.9 0.1 pad_maximum_fusion.2
  65.0 2.1 %collective-permute-start.3 = (bf16[2,2,128,1536]{3,2,1,0:T(8,128)(2,1)S(1)}, bf16[2,2,128,1536]{3,2,1,0:T(8,128)(2,1)S(1)}, u32[]{:S(2)}, u32[]{:S(2)}) collective-permute-start(bf16[2,2,128,1536]{3,2,1,0:T(8,128)(2,1)S(1)} %pad_maximum_fusion.2), channel_id=1, source_target_pairs={{0,1},{1,0},{2,3},{3,2},{4,5},{5,4},{6,7},{7,6},{8,9},{9,8},{10,11... | collective-permute-start | bytes 4718600 | tf_op jit(solution)/shard_map/ppermute | solution.py:143
  67.2 0.2 maximum_bitcast_fusion
  67.5 3.0 %collective-permute-done.3 = bf16[2,2,128,1536]{3,2,1,0:T(8,128)(2,1)S(1)} collective-permute-done((bf16[2,2,128,1536]{3,2,1,0:T(8,128)(2,1)S(1)}, bf16[2,2,128,1536]{3,2,1,0:T(8,128)(2,1)S(1)}, u32[]{:S(2)}, u32[]{:S(2)}) %collective-permute-start.3) | collective-permute-done | bytes 1572896 | tf_op jit(solution)/shard_map/ppermute | solution.py:143
  70.5 0.1 slice_bitcast_fusion.1
  70.6 0.2 maximum_bitcast_fusion.1
  70.7 1.6 pad_maximum_fusion.1.v_ref
  72.3 1.7 pad_maximum_fusion.k_ref
  74.0 0.7 slice.509
  74.7 0.1 copy.29
  74.9 0.1 copy.19
  75.0 0.1 reshape.114
  75.1 0.7 pad_add_fusion.1.info_ref
  75.8 32.2 %shard_map.55 = bf16[1024,1664]{1,0:T(8,128)(2,1)} custom-call(s32[50]{0:T(128)} %pad_add_fusion.1.info_ref, bf16[1024,1664]{1,0:T(8,128)(2,1)} %all-gather.2.cloned.1.call-done.q_ref, bf16[2,384,1536]{2,1,0:T(8,128)(2,1)} %pad_maximum_fusion.k_ref, bf16[2,384,1536]{2,1,0:T(8,128)(2,1)} %pad_maximum_fusion.1.v_ref), custom_call_target="tpu_custom_call" | custom-call | flops 3221225472 | bytes 11534336 | tf_op jit(solution)/shard_map/pallas_call | solution.py:113
  108.0 2.2 %constant_dynamic-slice_fusion.7 = (bf16[1,128,1664]{2,1,0:T(8,128)(2,1)S(1)}, bf16[1,128,1664]{2,1,0:T(8,128)(2,1)S(1)}, bf16[1,128,1664]{2,1,0:T(8,128)(2,1)S(...) fusion(bf16[8,128,1664]{2,1,0:T(8,128)(2,1)} %bitcast.119, ...), kind=kLoop, calls=%fused_computation.162 | loop fusion | bytes 6815776 | tf_op jit(solution)/shard_map/jit(dynamic_index_in_dim)/dynamic_slice | solution.py:208
  110.2 1.0 copy.21
  111.2 4.3 %collective-permute-start.4 = (bf16[128,1664]{0,1:T(8,128)(2,1)}, bf16[128,1664]{0,1:T(8,128)(2,1)}, u32[]{:S(2)}, u32[]{:S(2)}) collective-permute-start(bf16[128,1664]{0,1:T(8,128)(2,1)} %bitcast.137), channel_id=1, source_target_pairs={{0,2},{2,4},{4,6},{6,8},{8,10},{10,12},{12,14},{14,0},{1,3},{3,5},... | collective-permute-start | bytes 1277960 | tf_op jit(solution)/shard_map/ppermute | solution.py:217
  115.4 0.3 copy.22
  115.7 0.6 slice_convert_fusion.10
  116.3 0.3 copy.23
  116.6 0.3 copy.24
  116.9 0.3 copy.25
  117.2 8.6 %collective-permute-start.8 = (bf16[128,1664]{0,1:T(8,128)(2,1)S(1)}, bf16[128,1664]{0,1:T(8,128)(2,1)}, u32[]{:S(2)}, u32[]{:S(2)}) collective-permute-start(bf16[128,1664]{0,1:T(8,128)(2,1)S(1)} %bitcast.136), channel_id=1, source_target_pairs={{0,14},{2,0},{4,2},{6,4},{8,6},{10,8},{12,10},{14,12},{1,15},{3,1}... | collective-permute-start | bytes 1277960 | tf_op jit(solution)/shard_map/ppermute | solution.py:220
  125.8 0.3 copy.26
  126.1 0.3 copy.27
  126.4 0.3 copy.20
  126.6 0.6 slice_convert_fusion.3
  127.3 5.3 %collective-permute-done.4 = bf16[128,1664]{0,1:T(8,128)(2,1)} collective-permute-done((bf16[128,1664]{0,1:T(8,128)(2,1)}, bf16[128,1664]{0,1:T(8,128)(2,1)}, u32[]{:S(2)}, u32[]{:S(2)}) %collective-permute-start.4) | collective-permute-done | bytes 426016 | tf_op jit(solution)/shard_map/ppermute | solution.py:217
  132.5 0.7 slice_convert_fusion.11
  133.3 0.8 fusion.31
  134.1 1.2 fusion.12
  135.3 0.6 concatenate.44
  135.9 1.9 %collective-permute-start.5 = (bf16[128,1664]{0,1:T(8,128)(2,1)S(1)}, bf16[128,1664]{0,1:T(8,128)(2,1)S(1)}, u32[]{:S(2)}, u32[]{:S(2)}) collective-permute-start(bf16[128,1664]{0,1:T(8,128)(2,1)S(1)} %concatenate.44), channel_id=1, source_target_pairs={{0,2},{2,4},{4,6},{6,8},{8,10},{10,12},{12,14},{14,0},{1,3},{3,5},... | collective-permute-start | bytes 1277960 | tf_op jit(solution)/shard_map/ppermute | solution.py:217
  137.8 0.7 slice_convert_fusion.4
  138.5 0.8 fusion.22
  139.4 1.2 fusion.6
  140.5 0.6 concatenate.47
  141.2 5.1 %collective-permute-start.9 = (bf16[128,1664]{0,1:T(8,128)(2,1)S(1)}, bf16[128,1664]{0,1:T(8,128)(2,1)S(1)}, u32[]{:S(2)}, u32[]{:S(2)}) collective-permute-start(bf16[128,1664]{0,1:T(8,128)(2,1)S(1)} %concatenate.47), channel_id=1, source_target_pairs={{0,14},{2,0},{4,2},{6,4},{8,6},{10,8},{12,10},{14,12},{1,15},{3,1}... | collective-permute-start | bytes 1277960 | tf_op jit(solution)/shard_map/ppermute | solution.py:220
  146.3 4.0 %collective-permute-done.5 = bf16[128,1664]{0,1:T(8,128)(2,1)S(1)} collective-permute-done((bf16[128,1664]{0,1:T(8,128)(2,1)S(1)}, bf16[128,1664]{0,1:T(8,128)(2,1)S(1)}, u32[]{:S(2)}, u32[]{:S(2)}) %collective-permute-start.5) | collective-permute-done | bytes 426016 | tf_op jit(solution)/shard_map/ppermute | solution.py:217
  150.3 0.2 fusion.10
  150.5 0.6 concatenate.45
  151.1 1.9 %collective-permute-start.6 = (bf16[128,1664]{0,1:T(8,128)(2,1)S(1)}, bf16[128,1664]{0,1:T(8,128)(2,1)S(1)}, u32[]{:S(2)}, u32[]{:S(2)}) collective-permute-start(bf16[128,1664]{0,1:T(8,128)(2,1)S(1)} %concatenate.45), channel_id=1, source_target_pairs={{0,2},{2,4},{4,6},{6,8},{8,10},{10,12},{12,14},{14,0},{1,3},{3,5},... | collective-permute-start | bytes 1277960 | tf_op jit(solution)/shard_map/ppermute | solution.py:217
  153.1 1.8 collective-permute-done.9
  154.8 0.2 fusion.4
  155.0 0.6 concatenate.48
  155.7 5.6 %collective-permute-start.10 = (bf16[128,1664]{0,1:T(8,128)(2,1)S(1)}, bf16[128,1664]{0,1:T(8,128)(2,1)S(1)}, u32[]{:S(2)}, u32[]{:S(2)}) collective-permute-start(bf16[128,1664]{0,1:T(8,128)(2,1)S(1)} %concatenate.48), channel_id=1, source_target_pairs={{0,14},{2,0},{4,2},{6,4},{8,6},{10,8},{12,10},{14,12},{1,15},{3,1}... | collective-permute-start | bytes 1277960 | tf_op jit(solution)/shard_map/ppermute | solution.py:224
  161.3 3.4 %collective-permute-done.6 = bf16[128,1664]{0,1:T(8,128)(2,1)S(1)} collective-permute-done((bf16[128,1664]{0,1:T(8,128)(2,1)S(1)}, bf16[128,1664]{0,1:T(8,128)(2,1)S(1)}, u32[]{:S(2)}, u32[]{:S(2)}) %collective-permute-start.6) | collective-permute-done | bytes 426016 | tf_op jit(solution)/shard_map/ppermute | solution.py:217
  164.7 0.2 fusion.8
  164.9 0.6 concatenate.46
  165.5 1.9 %collective-permute-start.7 = (bf16[128,1664]{0,1:T(8,128)(2,1)S(1)}, bf16[128,1664]{0,1:T(8,128)(2,1)S(1)}, u32[]{:S(2)}, u32[]{:S(2)}) collective-permute-start(bf16[128,1664]{0,1:T(8,128)(2,1)S(1)} %concatenate.46), channel_id=1, source_target_pairs={{0,2},{2,4},{4,6},{6,8},{8,10},{10,12},{12,14},{14,0},{1,3},{3,5},... | collective-permute-start | bytes 1277960 | tf_op jit(solution)/shard_map/ppermute | solution.py:222
  167.5 1.5 collective-permute-done.10
  168.9 9.3 %collective-permute-done.7 = bf16[128,1664]{0,1:T(8,128)(2,1)S(1)} collective-permute-done((bf16[128,1664]{0,1:T(8,128)(2,1)S(1)}, bf16[128,1664]{0,1:T(8,128)(2,1)S(1)}, u32[]{:S(2)}, u32[]{:S(2)}) %collective-permute-start.7) | collective-permute-done | bytes 426016 | tf_op jit(solution)/shard_map/ppermute | solution.py:222
  178.2 0.3 fusion
  178.5 0.9 copy.28
  (49 shorter events, 0.5 us)
Async XLA Ops:
  6.5 67.5 %all-gather.2.cloned.1.call-start = ((), (), s32[]{:S(2)}) async-start(), calls=%async_computation | async-start | bytes 3833856 | tf_op jit(solution)/shard_map/all_gather | solution.py:163
  11.4 22.3 %collective-permute-start = (bf16[2,128,1536]{2,1,0:T(8,128)(2,1)S(1)}, bf16[2,128,1536]{2,1,0:T(8,128)(2,1)S(1)}, u32[]{:S(2)}, u32[]{:S(2)}) collective-permute-start(bf16[2,128,1536]{2,1,0:T(8,128)(2,1)S(1)} %pad_maximum_fusion.3), channel_id=1, source_target_pairs={{0,16},{16,32},{32,48},{48,64},{64,80},{80,96},{96,112},{112,128},... | collective-permute-start | bytes 2359304 | tf_op jit(solution)/shard_map/ppermute | solution.py:21
  14.8 50.1 %collective-permute-start.1 = (bf16[2,128,1536]{2,1,0:T(8,128)(2,1)S(1)}, bf16[2,128,1536]{2,1,0:T(8,128)(2,1)S(1)}, u32[]{:S(2)}, u32[]{:S(2)}) collective-permute-start(bf16[2,128,1536]{2,1,0:T(8,128)(2,1)S(1)} %pad_maximum_fusion.3), channel_id=1, source_target_pairs={{0,32},{16,48},{32,64},{48,80},{64,96},{80,112},{96,128},{112,144}... | collective-permute-start | bytes 2359304 | tf_op jit(solution)/shard_map/ppermute | solution.py:21
  17.9 49.5 %collective-permute-start.2 = (bf16[2,128,1536]{2,1,0:T(8,128)(2,1)S(1)}, bf16[2,128,1536]{2,1,0:T(8,128)(2,1)S(1)}, u32[]{:S(2)}, u32[]{:S(2)}) collective-permute-start(bf16[2,128,1536]{2,1,0:T(8,128)(2,1)S(1)} %pad_maximum_fusion.3), channel_id=1, source_target_pairs={{0,1},{1,0},{2,3},{3,2},{4,5},{5,4},{6,7},{7,6},{8,9},{9,8},{10,11... | collective-permute-start | bytes 2359304 | tf_op jit(solution)/shard_map/ppermute | solution.py:142
  65.0 2.2 %copy-start = (bf16[128,1536]{1,0:T(8,128)(2,1)S(1)}, bf16[128,1536]{1,0:T(8,128)(2,1)}, u32[]{:S(2)}) copy-start(bf16[128,1536]{1,0:T(8,128)(2,1)} %param.7) | copy-start | bytes 1179652
  65.0 2.2 %copy-start.1 = (bf16[128,1536]{1,0:T(8,128)(2,1)S(1)}, bf16[128,1536]{1,0:T(8,128)(2,1)}, u32[]{:S(2)}) copy-start(bf16[128,1536]{1,0:T(8,128)(2,1)} %param.6) | copy-start | bytes 1179652
  65.0 5.4 %collective-permute-start.3 = (bf16[2,2,128,1536]{3,2,1,0:T(8,128)(2,1)S(1)}, bf16[2,2,128,1536]{3,2,1,0:T(8,128)(2,1)S(1)}, u32[]{:S(2)}, u32[]{:S(2)}) collective-permute-start(bf16[2,2,128,1536]{3,2,1,0:T(8,128)(2,1)S(1)} %pad_maximum_fusion.2), channel_id=1, source_target_pairs={{0,1},{1,0},{2,3},{3,2},{4,5},{5,4},{6,7},{7,6},{8,9},{9,8},{10,11... | collective-permute-start | bytes 4718600 | tf_op jit(solution)/shard_map/ppermute | solution.py:143
  111.2 21.4 %collective-permute-start.4 = (bf16[128,1664]{0,1:T(8,128)(2,1)}, bf16[128,1664]{0,1:T(8,128)(2,1)}, u32[]{:S(2)}, u32[]{:S(2)}) collective-permute-start(bf16[128,1664]{0,1:T(8,128)(2,1)} %bitcast.137), channel_id=1, source_target_pairs={{0,2},{2,4},{4,6},{6,8},{8,10},{10,12},{12,14},{14,0},{1,3},{3,5},... | collective-permute-start | bytes 1277960 | tf_op jit(solution)/shard_map/ppermute | solution.py:217
  117.2 20.6 %collective-permute-start.8 = (bf16[128,1664]{0,1:T(8,128)(2,1)S(1)}, bf16[128,1664]{0,1:T(8,128)(2,1)}, u32[]{:S(2)}, u32[]{:S(2)}) collective-permute-start(bf16[128,1664]{0,1:T(8,128)(2,1)S(1)} %bitcast.136), channel_id=1, source_target_pairs={{0,14},{2,0},{4,2},{6,4},{8,6},{10,8},{12,10},{14,12},{1,15},{3,1}... | collective-permute-start | bytes 1277960 | tf_op jit(solution)/shard_map/ppermute | solution.py:220
  135.9 14.4 %collective-permute-start.5 = (bf16[128,1664]{0,1:T(8,128)(2,1)S(1)}, bf16[128,1664]{0,1:T(8,128)(2,1)S(1)}, u32[]{:S(2)}, u32[]{:S(2)}) collective-permute-start(bf16[128,1664]{0,1:T(8,128)(2,1)S(1)} %concatenate.44), channel_id=1, source_target_pairs={{0,2},{2,4},{4,6},{6,8},{8,10},{10,12},{12,14},{14,0},{1,3},{3,5},... | collective-permute-start | bytes 1277960 | tf_op jit(solution)/shard_map/ppermute | solution.py:217
  141.2 13.6 %collective-permute-start.9 = (bf16[128,1664]{0,1:T(8,128)(2,1)S(1)}, bf16[128,1664]{0,1:T(8,128)(2,1)S(1)}, u32[]{:S(2)}, u32[]{:S(2)}) collective-permute-start(bf16[128,1664]{0,1:T(8,128)(2,1)S(1)} %concatenate.47), channel_id=1, source_target_pairs={{0,14},{2,0},{4,2},{6,4},{8,6},{10,8},{12,10},{14,12},{1,15},{3,1}... | collective-permute-start | bytes 1277960 | tf_op jit(solution)/shard_map/ppermute | solution.py:220
  151.1 13.5 %collective-permute-start.6 = (bf16[128,1664]{0,1:T(8,128)(2,1)S(1)}, bf16[128,1664]{0,1:T(8,128)(2,1)S(1)}, u32[]{:S(2)}, u32[]{:S(2)}) collective-permute-start(bf16[128,1664]{0,1:T(8,128)(2,1)S(1)} %concatenate.45), channel_id=1, source_target_pairs={{0,2},{2,4},{4,6},{6,8},{8,10},{10,12},{12,14},{14,0},{1,3},{3,5},... | collective-permute-start | bytes 1277960 | tf_op jit(solution)/shard_map/ppermute | solution.py:217
  155.7 13.3 %collective-permute-start.10 = (bf16[128,1664]{0,1:T(8,128)(2,1)S(1)}, bf16[128,1664]{0,1:T(8,128)(2,1)S(1)}, u32[]{:S(2)}, u32[]{:S(2)}) collective-permute-start(bf16[128,1664]{0,1:T(8,128)(2,1)S(1)} %concatenate.48), channel_id=1, source_target_pairs={{0,14},{2,0},{4,2},{6,4},{8,6},{10,8},{12,10},{14,12},{1,15},{3,1}... | collective-permute-start | bytes 1277960 | tf_op jit(solution)/shard_map/ppermute | solution.py:224
  165.5 12.7 %collective-permute-start.7 = (bf16[128,1664]{0,1:T(8,128)(2,1)S(1)}, bf16[128,1664]{0,1:T(8,128)(2,1)S(1)}, u32[]{:S(2)}, u32[]{:S(2)}) collective-permute-start(bf16[128,1664]{0,1:T(8,128)(2,1)S(1)} %concatenate.46), channel_id=1, source_target_pairs={{0,2},{2,4},{4,6},{6,8},{8,10},{10,12},{12,14},{14,0},{1,3},{3,5},... | collective-permute-start | bytes 1277960 | tf_op jit(solution)/shard_map/ppermute | solution.py:222
Sparse Core Ops, SparseCore 0:
  10.3 54.8 all-gather.1

commit v10 on v9

--- a/solution.py
+++ b/solution.py
@@ -13,6 +13,7 @@
 NEG_FILL = -1e30
 LAGS = 3
 AXES = ("pb", "z", "core")
+HEADER = 4
 
 
 def passed_along(block, axis, distance):
@@ -38,10 +39,11 @@
 
 
 def pair_kernel(info_ref, q_ref, k_ref, v_ref, out_ref, stat_ref):
-    t = pl.program_id(0)
     chip = info_ref[0]
     core = info_ref[1]
-    block_len = out_ref.shape[0]
+    chips = info_ref[2]
+    t = (chip + info_ref[info_ref[3] + pl.program_id(0)]) % chips
+    block_len = out_ref.shape[1]
     feature_width = k_ref.shape[2]
     head_count = feature_width // DH
     column = 2 * t + core
@@ -54,7 +56,7 @@
     for j in range(2):
         key_class = 2 * chip + (core + j) % 2
         lag_a = jnp.where(key_class <= column, 0, 1)
-        base = 2 + (t * 2 + j) * LAGS + lag_a
+        base = HEADER + (t * 2 + j) * LAGS + lag_a
         listed_a = info_ref[base] != 0
         listed_b = info_ref[base + 1] != 0
         diagonal = key_class == column
@@ -74,12 +76,15 @@
             s = lax.dot_general(q, keys, nt, preferred_element_type=jnp.float32)
             scores.append(jnp.where(masks[j], s * scaling, NEG_FILL))
         highest = jnp.maximum(
-            jnp.max(scores[0], axis=1, keepdims=True), jnp.max(scores[1], axis=1, keepdims=True)
+            jnp.maximum(
+                jnp.max(scores[0], axis=1, keepdims=True), jnp.max(scores[1], axis=1, keepdims=True)
+            ),
+            0.1 * NEG_FILL,
         )
         total = None
         blended = None
         for j in range(2):
-            w = jnp.where(masks[j], jnp.exp(scores[j] - highest), 0.0)
+            w = jnp.exp(scores[j] - highest)
             part_total = jnp.sum(w, axis=1, keepdims=True)
             part = jnp.dot(
                 w.astype(jnp.bfloat16),
@@ -88,36 +93,40 @@
             )
             total = part_total if total is None else total + part_total
             blended = part if blended is None else blended + part
-        out_ref[:, cols] = blended.astype(jnp.bfloat16)
+        out_ref[0, :, cols] = blended.astype(jnp.bfloat16)
         for part, value in enumerate(split_parts(highest, 3) + split_parts(total, 2)):
             stat_ref[:, part * head_count + h : part * head_count + h + 1] = value
-    out_ref[:, feature_width:] = stat_ref[...].astype(jnp.bfloat16)
-
-
-def pair_partials(info, row_q, key_window, value_window):
+    out_ref[0, :, feature_width:] = stat_ref[...].astype(jnp.bfloat16)
+
+
+def pair_partials(info, row_q, key_window, value_window, steps):
     block_len = key_window.shape[1] // LAGS
-    sources = row_q.shape[0] // block_len
+    chips = row_q.shape[0] // block_len
     feature_width = key_window.shape[2]
     head_count = feature_width // DH
+
+    def q_map(i, info_ref):
+        return ((info_ref[0] + info_ref[info_ref[3] + i]) % chips, 0)
+
     grid_spec = pltpu.PrefetchScalarGridSpec(
         num_scalar_prefetch=1,
-        grid=(sources,),
+        grid=(steps,),
         in_specs=[
-            pl.BlockSpec((block_len, row_q.shape[1]), lambda t, info_ref: (t, 0)),
-            pl.BlockSpec(key_window.shape, lambda t, info_ref: (0, 0, 0)),
-            pl.BlockSpec(value_window.shape, lambda t, info_ref: (0, 0, 0)),
+            pl.BlockSpec((block_len, row_q.shape[1]), q_map),
+            pl.BlockSpec(key_window.shape, lambda i, info_ref: (0, 0, 0)),
+            pl.BlockSpec(value_window.shape, lambda i, info_ref: (0, 0, 0)),
         ],
-        out_specs=pl.BlockSpec((block_len, row_q.shape[1]), lambda t, info_ref: (t, 0)),
+        out_specs=pl.BlockSpec((1, block_len, row_q.shape[1]), lambda i, info_ref: (i, 0, 0)),
         scratch_shapes=[pltpu.VMEM((block_len, row_q.shape[1] - feature_width), jnp.float32)],
     )
     return pl.pallas_call(
         pair_kernel,
         grid_spec=grid_spec,
-        out_shape=jax.ShapeDtypeStruct(row_q.shape, jnp.bfloat16),
+        out_shape=jax.ShapeDtypeStruct((steps, block_len, row_q.shape[1]), jnp.bfloat16),
         cost_estimate=pl.CostEstimate(
-            flops=sources * head_count * 2 * 2 * 2 * block_len * 2 * block_len * DH,
-            transcendentals=sources * head_count * 2 * 2 * block_len * block_len,
-            bytes_accessed=2 * sources * block_len * row_q.shape[1] * 2
+            flops=steps * head_count * 2 * 2 * 2 * block_len * 2 * block_len * DH,
+            transcendentals=steps * head_count * 2 * 2 * block_len * block_len,
+            bytes_accessed=2 * steps * block_len * row_q.shape[1] * 2
             + 2 * 2 * LAGS * block_len * feature_width * 2,
         ),
     )(info, row_q, key_window, value_window)
@@ -169,12 +178,25 @@
         lax.dynamic_index_in_dim(marks_all, 2 * chip + (core + j) % 2, axis=1, keepdims=False)
         for j in range(2)
     ]
-    info = jnp.concatenate(
-        [jnp.stack([chip, core]).astype(jnp.int32), jnp.stack(mine, axis=1).reshape(-1)]
-    )
-
-    pair_out = pair_partials(info, row_q, key_window, value_window)
-    pair_out = pair_out.reshape(chips, block_len, -1)
+    mine = jnp.stack(mine, axis=1).reshape(-1)
+    header = jnp.stack([chip, core, jnp.int32(chips), jnp.int32(HEADER + mine.shape[0])])
+
+    reach_r = chips // 2
+    reach_l = chips - 1 - reach_r
+    order = []
+    for step in range(reach_r + 1):
+        order.append(reach_r - step)
+        if step < reach_l:
+            order.append(step - reach_l)
+    blocks = {}
+
+    def compute(offsets, queries_in):
+        info = jnp.concatenate(
+            [header.astype(jnp.int32), mine, jnp.array(offsets, jnp.int32) % chips]
+        )
+        out = pair_partials(info, queries_in, key_window, value_window, len(offsets))
+        for i, offset in enumerate(offsets):
+            blocks[offset] = out[i]
 
     def decode(block):
         stats = block[:, feature_width : feature_width + 5 * head_count].astype(jnp.float32)
@@ -205,12 +227,11 @@
         ).astype(jnp.bfloat16)
 
     def block_for(offset):
-        return lax.dynamic_index_in_dim(pair_out, (chip + offset) % chips, axis=0, keepdims=False)
+        return blocks[offset]
 
     rightward = [(z, (z + 1) % chips) for z in range(chips)]
     leftward = [(z, (z - 1) % chips) for z in range(chips)]
-    reach_r = chips // 2
-    reach_l = chips - 1 - reach_r
+    compute(order, row_q)
     acc_r = block_for(reach_r)
     acc_l = block_for(-reach_l)
     for step in range(1, reach_r):

time: 187 us -> 208 us (1.11)
  the two profiles are of different devices: /device:TPU:50 before, /device:TPU:42 now
where the time goes in v10:
time: 208 us; the launch traced here: 207 us
  waiting for transfers between devices  75.6 us (36%)
  starting transfers between devices  40 us (19%)
  Pallas kernels  31.8 us (15%)
  other arithmetic  27.7 us (13%)
  local copies, waits for them, and re-layouts  17.2 us (8%)
  between operations  14.9 us (7%)
    ppermute x2, waiting for transfers between devices, passed_along(): return lax.ppermute(block, axis, route)  45 us
    pallas_call x1, Pallas kernels, pair_partials(): pl.pallas_call(pair_kernel, grid_spec=grid_spec, out_shape=jax.ShapeDtype...  31.8 us
    ppermute x3, waiting for transfers between devices, per_device(): lax.ppermute(acc_r, 'z', rightward)  17.2 us
    ppermute x2, starting transfers between devices, per_device(): lax.ppermute(acc_l, 'z', leftward)  13.6 us
    another operation x15, other arithmetic  10.8 us
    ppermute x1, waiting for transfers between devices, per_device(): final = [block_for(0), lax.ppermute(acc_r, 'z', rightward)]  10 us
    ppermute x3, starting transfers between devices, per_device(): lax.ppermute(acc_r, 'z', rightward)  8.27 us
    ppermute x2, starting transfers between devices, passed_along(): return lax.ppermute(block, axis, route)  6.53 us
  transfers between devices with their start and end apart: 12, of which 8 were waited for; matrix products, arithmetic and copies ran while one was open for 9% of the time, Pallas kernels for 0%

profile of v10, /device:TPU:42, one launch (start us, length us, event | category | flops | bytes accessed | tf_op | source)
XLA Modules:
  0.0 207.3 jit_solution(13496770081883055211)
XLA Ops:
  7.3 0.9 and_reduce_fusion
  8.4 1.8 pad_maximum_fusion.4
  10.2 1.2 pad_maximum_fusion.3
  11.4 3.4 %collective-permute-start = (bf16[2,128,1536]{2,1,0:T(8,128)(2,1)S(1)}, bf16[2,128,1536]{2,1,0:T(8,128)(2,1)S(1)}, u32[]{:S(2)}, u32[]{:S(2)}) collective-permute-start(bf16[2,128,1536]{2,1,0:T(8,128)(2,1)S(1)} %pad_maximum_fusion.3), channel_id=1, source_target_pairs={{0,16},{16,32},{32,48},{48,64},{64,80},{80,96},{96,112},{112,128},... | collective-permute-start | bytes 2359304 | tf_op jit(solution)/shard_map/ppermute | solution.py:22
  14.8 3.1 %collective-permute-start.1 = (bf16[2,128,1536]{2,1,0:T(8,128)(2,1)S(1)}, bf16[2,128,1536]{2,1,0:T(8,128)(2,1)S(1)}, u32[]{:S(2)}, u32[]{:S(2)}) collective-permute-start(bf16[2,128,1536]{2,1,0:T(8,128)(2,1)S(1)} %pad_maximum_fusion.3), channel_id=1, source_target_pairs={{0,32},{16,48},{32,64},{48,80},{64,96},{80,112},{96,128},{112,144}... | collective-permute-start | bytes 2359304 | tf_op jit(solution)/shard_map/ppermute | solution.py:22
  17.9 1.9 collective-permute-start.2
  19.9 13.8 %collective-permute-done = bf16[2,128,1536]{2,1,0:T(8,128)(2,1)S(1)} collective-permute-done((bf16[2,128,1536]{2,1,0:T(8,128)(2,1)S(1)}, bf16[2,128,1536]{2,1,0:T(8,128)(2,1)S(1)}, u32[]{:S(2)}, u32[]{:S(2)}) %collective-permute-start) | collective-permute-done | bytes 786464 | tf_op jit(solution)/shard_map/ppermute | solution.py:22
  33.7 31.2 %collective-permute-done.1 = bf16[2,128,1536]{2,1,0:T(8,128)(2,1)S(1)} collective-permute-done((bf16[2,128,1536]{2,1,0:T(8,128)(2,1)S(1)}, bf16[2,128,1536]{2,1,0:T(8,128)(2,1)S(1)}, u32[]{:S(2)}, u32[]{:S(2)}) %collective-permute-start.1) | collective-permute-done | bytes 786464 | tf_op jit(solution)/shard_map/ppermute | solution.py:22
  65.0 2.1 collective-permute-start.3
  67.5 3.0 %collective-permute-done.3 = bf16[2,2,128,1536]{3,2,1,0:T(8,128)(2,1)S(1)} collective-permute-done((bf16[2,2,128,1536]{3,2,1,0:T(8,128)(2,1)S(1)}, bf16[2,2,128,1536]{3,2,1,0:T(8,128)(2,1)S(1)}, u32[]{:S(2)}, u32[]{:S(2)}) %collective-permute-start.3) | collective-permute-done | bytes 1572896 | tf_op jit(solution)/shard_map/ppermute | solution.py:152
  70.7 1.6 pad_maximum_fusion.1.v_ref
  72.3 1.7 pad_maximum_fusion.k_ref
  74.0 0.7 slice.541
  75.1 0.6 concatenate.39.info_ref
  75.6 31.8 %shard_map.64 = bf16[8,128,1664]{2,1,0:T(8,128)(2,1)} custom-call(s32[60]{0:T(128)} %concatenate.39.info_ref, bf16[1024,1664]{1,0:T(8,128)(2,1)} %all-gather.2.cloned.1.call-done.q_ref, bf16[2,384,1536]{2,1,0:T(8,128)(2,1)} %pad_maximum_fusion.k_ref, bf16[2,384,1536]{2,1,0:T(8,128)(2,1)} %pad_maximum_fusion.1.v_ref), custom_call_target="tpu_custom_call" | custom-call | flops 3221225472 | bytes 11534336 | tf_op jit(solution)/shard_map/pallas_call | solution.py:122
  107.5 2.2 %slice_bitcast_fusion.7 = (bf16[128,1664]{1,0:T(8,128)(2,1)S(1)}, bf16[128,1664]{1,0:T(8,128)(2,1)S(1)}, bf16[128,1664]{1,0:T(8,128)(2,1)S(1)}, bf16[128,1664]{1...) fusion(bf16[8,128,1664]{2,1,0:T(8,128)(2,1)} %shard_map.64), kind=kLoop, calls=%fused_computation.21 | loop fusion | bytes 6815744 | tf_op jit(solution)/shard_map/squeeze | solution.py:199
  109.7 4.4 %collective-permute-start.4 = (bf16[128,1664]{1,0:T(8,128)(2,1)S(1)}, bf16[128,1664]{1,0:T(8,128)(2,1)S(1)}, u32[]{:S(2)}, u32[]{:S(2)}) collective-permute-start(bf16[128,1664]{1,0:T(8,128)(2,1)S(1)} %get-tuple-element.51), channel_id=1, source_target_pairs={{0,2},{2,4},{4,6},{6,8},{8,10},{10,12},{12,14},{14,0},{1,3},{3,5},... | collective-permute-start | bytes 1277960 | tf_op jit(solution)/shard_map/ppermute | solution.py:238
  114.1 8.5 %collective-permute-start.8 = (bf16[128,1664]{1,0:T(8,128)(2,1)S(1)}, bf16[128,1664]{1,0:T(8,128)(2,1)S(1)}, u32[]{:S(2)}, u32[]{:S(2)}) collective-permute-start(bf16[128,1664]{1,0:T(8,128)(2,1)S(1)} %get-tuple-element.47), channel_id=1, source_target_pairs={{0,14},{2,0},{4,2},{6,4},{8,6},{10,8},{12,10},{14,12},{1,15},{3,1}... | collective-permute-start | bytes 1277960 | tf_op jit(solution)/shard_map/ppermute | solution.py:241
  122.7 8.2 %collective-permute-done.4 = bf16[128,1664]{1,0:T(8,128)(2,1)S(1)} collective-permute-done((bf16[128,1664]{1,0:T(8,128)(2,1)S(1)}, bf16[128,1664]{1,0:T(8,128)(2,1)S(1)}, u32[]{:S(2)}, u32[]{:S(2)}) %collective-permute-start.4) | collective-permute-done | bytes 426016 | tf_op jit(solution)/shard_map/ppermute | solution.py:238
  130.9 0.8 copy-done.10
  131.6 0.8 fusion.18
  132.5 0.6 max.71
  133.1 0.6 subtract_convert_fusion.9
  133.7 0.8 fusion.9
  134.6 0.6 subtract_convert_fusion.3
  135.4 0.3 copy.72
  135.8 0.3 copy.74
  136.1 0.9 subtract_convert_fusion.8
  137.0 1.3 add_convert_fusion.4
  138.4 1.7 concatenate.44
  140.1 1.9 collective-permute-start.5
  142.1 0.3 copy.84
  142.6 0.3 copy.86
  142.9 1.3 add_convert_fusion.1
  144.3 5.1 %collective-permute-start.9 = (bf16[128,1664]{1,0:T(8,128)(2,1)S(1)}, bf16[128,1664]{1,0:T(8,128)(2,1)S(1)}, u32[]{:S(2)}, u32[]{:S(2)}) collective-permute-start(bf16[128,1664]{1,0:T(8,128)(2,1)S(1)} %concatenate.47), channel_id=1, source_target_pairs={{0,14},{2,0},{4,2},{6,4},{8,6},{10,8},{12,10},{14,12},{1,15},{3,1}... | collective-permute-start | bytes 1277960 | tf_op jit(solution)/shard_map/ppermute | solution.py:241
  149.5 5.4 %collective-permute-done.5 = bf16[128,1664]{1,0:T(8,128)(2,1)} collective-permute-done((bf16[128,1664]{1,0:T(8,128)(2,1)}, bf16[128,1664]{1,0:T(8,128)(2,1)}, u32[]{:S(2)}, u32[]{:S(2)}) %collective-permute-start.5) | collective-permute-done | bytes 426016 | tf_op jit(solution)/shard_map/ppermute | solution.py:238
  154.9 0.8 slice_convert_fusion.9
  155.6 0.8 fusion.15
  156.5 0.6 max.70
  157.1 0.6 subtract_convert_fusion.7
  157.7 0.4 collective-permute-done.9
  158.3 0.7 subtract_convert_fusion.1
  159.1 0.3 copy.76
  159.8 0.9 subtract_convert_fusion.6
  160.8 1.3 add_convert_fusion.3
  162.1 0.9 concatenate.45
  163.0 2.0 collective-permute-start.6
  165.9 1.3 add_convert_fusion
  167.2 0.9 concatenate.48
  168.1 5.7 %collective-permute-start.10 = (bf16[128,1664]{1,0:T(8,128)(2,1)}, bf16[128,1664]{1,0:T(8,128)(2,1)}, u32[]{:S(2)}, u32[]{:S(2)}) collective-permute-start(bf16[128,1664]{1,0:T(8,128)(2,1)} %concatenate.48), channel_id=1, source_target_pairs={{0,14},{2,0},{4,2},{6,4},{8,6},{10,8},{12,10},{14,12},{1,15},{3,1}... | collective-permute-start | bytes 1277960 | tf_op jit(solution)/shard_map/ppermute | solution.py:245
  173.8 3.6 %collective-permute-done.6 = bf16[128,1664]{1,0:T(8,128)(2,1)} collective-permute-done((bf16[128,1664]{1,0:T(8,128)(2,1)}, bf16[128,1664]{1,0:T(8,128)(2,1)}, u32[]{:S(2)}, u32[]{:S(2)}) %collective-permute-start.6) | collective-permute-done | bytes 426016 | tf_op jit(solution)/shard_map/ppermute | solution.py:238
  177.4 0.8 slice_convert_fusion.7
  179.0 0.3 copy.82
  179.2 1.2 add_convert_fusion.2
  180.6 1.9 collective-permute-start.7
  182.6 0.8 slice_convert_fusion
  183.3 10.0 %collective-permute-done.7 = bf16[128,1664]{1,0:T(8,128)(2,1)S(1)} collective-permute-done((bf16[128,1664]{1,0:T(8,128)(2,1)S(1)}, bf16[128,1664]{1,0:T(8,128)(2,1)S(1)}, u32[]{:S(2)}, u32[]{:S(2)}) %collective-permute-start.7) | collective-permute-done | bytes 426016 | tf_op jit(solution)/shard_map/ppermute | solution.py:243
  193.4 0.8 copy-done.7
  194.1 0.3 fusion.1
  195.0 0.3 copy.94
  195.4 0.3 copy.96
  195.7 1.0 div.11
  196.7 1.4 copy.98
  198.1 2.4 %divide_convert_fusion = bf16[128,1536]{1,0:T(8,128)(2,1)} fusion(f32[128,1536]{1,0:T(8,128)S(1)} %copy.98, f32[128,1536]{1,0:T(8,128)S(1)} %copy.96, f32[128,1536]{1,0:T(8,128)S(1)} %copy.94, f32[128,1536]{1,0:T(8,128)S(1)} %copy.92, bf16[128,1664]{1,0:T(8,128)(2,1)} %collective-permute-done.10, bf16[128,1664]{1,0:T(8,128)(2,1)} %copy-done.7, ...), kind=kLoop, calls=%fused_computation.8 | loop fusion | flops 1966080 | bytes 4718592 | tf_op jit(solution)/shard_map/convert_element_type | solution.py:247
  (120 shorter events, 5.4 us)
Async XLA Ops:
  6.5 67.4 %all-gather.2.cloned.1.call-start = ((), (), s32[]{:S(2)}) async-start(), calls=%async_computation | async-start | bytes 3833856 | tf_op jit(solution)/shard_map/all_gather | solution.py:172
  11.4 22.3 %collective-permute-start = (bf16[2,128,1536]{2,1,0:T(8,128)(2,1)S(1)}, bf16[2,128,1536]{2,1,0:T(8,128)(2,1)S(1)}, u32[]{:S(2)}, u32[]{:S(2)}) collective-permute-start(bf16[2,128,1536]{2,1,0:T(8,128)(2,1)S(1)} %pad_maximum_fusion.3), channel_id=1, source_target_pairs={{0,16},{16,32},{32,48},{48,64},{64,80},{80,96},{96,112},{112,128},... | collective-permute-start | bytes 2359304 | tf_op jit(solution)/shard_map/ppermute | solution.py:22
  14.8 50.1 %collective-permute-start.1 = (bf16[2,128,1536]{2,1,0:T(8,128)(2,1)S(1)}, bf16[2,128,1536]{2,1,0:T(8,128)(2,1)S(1)}, u32[]{:S(2)}, u32[]{:S(2)}) collective-permute-start(bf16[2,128,1536]{2,1,0:T(8,128)(2,1)S(1)} %pad_maximum_fusion.3), channel_id=1, source_target_pairs={{0,32},{16,48},{32,64},{48,80},{64,96},{80,112},{96,128},{112,144}... | collective-permute-start | bytes 2359304 | tf_op jit(solution)/shard_map/ppermute | solution.py:22
  17.9 49.5 %collective-permute-start.2 = (bf16[2,128,1536]{2,1,0:T(8,128)(2,1)S(1)}, bf16[2,128,1536]{2,1,0:T(8,128)(2,1)S(1)}, u32[]{:S(2)}, u32[]{:S(2)}) collective-permute-start(bf16[2,128,1536]{2,1,0:T(8,128)(2,1)S(1)} %pad_maximum_fusion.3), channel_id=1, source_target_pairs={{0,1},{1,0},{2,3},{3,2},{4,5},{5,4},{6,7},{7,6},{8,9},{9,8},{10,11... | collective-permute-start | bytes 2359304 | tf_op jit(solution)/shard_map/ppermute | solution.py:151
  65.0 2.2 %copy-start.5 = (bf16[128,1536]{1,0:T(8,128)(2,1)S(1)}, bf16[128,1536]{1,0:T(8,128)(2,1)}, u32[]{:S(2)}) copy-start(bf16[128,1536]{1,0:T(8,128)(2,1)} %param.8) | copy-start | bytes 1179652
  65.0 2.2 %copy-start.6 = (bf16[128,1536]{1,0:T(8,128)(2,1)S(1)}, bf16[128,1536]{1,0:T(8,128)(2,1)}, u32[]{:S(2)}) copy-start(bf16[128,1536]{1,0:T(8,128)(2,1)} %param.7) | copy-start | bytes 1179652
  65.0 5.4 %collective-permute-start.3 = (bf16[2,2,128,1536]{3,2,1,0:T(8,128)(2,1)S(1)}, bf16[2,2,128,1536]{3,2,1,0:T(8,128)(2,1)S(1)}, u32[]{:S(2)}, u32[]{:S(2)}) collective-permute-start(bf16[2,2,128,1536]{3,2,1,0:T(8,128)(2,1)S(1)} %pad_maximum_fusion.2), channel_id=1, source_target_pairs={{0,1},{1,0},{2,3},{3,2},{4,5},{5,4},{6,7},{7,6},{8,9},{9,8},{10,11... | collective-permute-start | bytes 4718600 | tf_op jit(solution)/shard_map/ppermute | solution.py:152
  72.3 2.7 %copy-start.20 = (s32[8]{0:T(128)S(1)}, s32[8]{0:T(128)}, u32[]{:S(2)}) copy-start(s32[8]{0:T(128)} %constant.86) | copy-start | bytes 100
  109.7 24.9 %copy-start.1 = (bf16[128,1664]{1,0:T(8,128)(2,1)}, bf16[128,1664]{1,0:T(8,128)(2,1)S(1)}, u32[]{:S(2)}) copy-start(bf16[128,1664]{1,0:T(8,128)(2,1)S(1)} %get-tuple-element.45) | copy-start | bytes 1277956
  109.7 24.9 %copy-start.2 = (bf16[128,1664]{1,0:T(8,128)(2,1)}, bf16[128,1664]{1,0:T(8,128)(2,1)S(1)}, u32[]{:S(2)}) copy-start(bf16[128,1664]{1,0:T(8,128)(2,1)S(1)} %get-tuple-element.49) | copy-start | bytes 1277956
  109.7 24.9 %copy-start.3 = (bf16[128,1664]{1,0:T(8,128)(2,1)}, bf16[128,1664]{1,0:T(8,128)(2,1)S(1)}, u32[]{:S(2)}) copy-start(bf16[128,1664]{1,0:T(8,128)(2,1)S(1)} %get-tuple-element.46) | copy-start | bytes 1277956
  109.7 25.6 %copy-start.4 = (bf16[128,1664]{1,0:T(8,128)(2,1)}, bf16[128,1664]{1,0:T(8,128)(2,1)S(1)}, u32[]{:S(2)}) copy-start(bf16[128,1664]{1,0:T(8,128)(2,1)S(1)} %get-tuple-element.50) | copy-start | bytes 1277956
  109.7 72.8 %copy-start = (bf16[128,1664]{1,0:T(8,128)(2,1)}, bf16[128,1664]{1,0:T(8,128)(2,1)S(1)}, u32[]{:S(2)}) copy-start(bf16[128,1664]{1,0:T(8,128)(2,1)S(1)} %get-tuple-element.44) | copy-start | bytes 1277956
  109.7 21.2 %collective-permute-start.4 = (bf16[128,1664]{1,0:T(8,128)(2,1)S(1)}, bf16[128,1664]{1,0:T(8,128)(2,1)S(1)}, u32[]{:S(2)}, u32[]{:S(2)}) collective-permute-start(bf16[128,1664]{1,0:T(8,128)(2,1)S(1)} %get-tuple-element.51), channel_id=1, source_target_pairs={{0,2},{2,4},{4,6},{6,8},{8,10},{10,12},{12,14},{14,0},{1,3},{3,5},... | collective-permute-start | bytes 1277960 | tf_op jit(solution)/shard_map/ppermute | solution.py:238
  114.1 19.6 %collective-permute-start.8 = (bf16[128,1664]{1,0:T(8,128)(2,1)S(1)}, bf16[128,1664]{1,0:T(8,128)(2,1)S(1)}, u32[]{:S(2)}, u32[]{:S(2)}) collective-permute-start(bf16[128,1664]{1,0:T(8,128)(2,1)S(1)} %get-tuple-element.47), channel_id=1, source_target_pairs={{0,14},{2,0},{4,2},{6,4},{8,6},{10,8},{12,10},{14,12},{1,15},{3,1}... | collective-permute-start | bytes 1277960 | tf_op jit(solution)/shard_map/ppermute | solution.py:241
  130.9 0.8 copy-start.10
  133.7 1.5 copy-start.8
  136.1 5.9 %copy-start.12 = (f32[128,12]{1,0:T(8,128)S(1)}, f32[128,12]{1,0:T(8,128)}, u32[]{:S(2)}) copy-start(f32[128,12]{1,0:T(8,128)} %get-tuple-element.40) | copy-start | bytes 18436
  138.3 4.1 %copy-start.11 = (f32[128,12]{1,0:T(8,128)S(1)}, f32[128,12]{1,0:T(8,128)}, u32[]{:S(2)}) copy-start(f32[128,12]{1,0:T(8,128)} %get-tuple-element.41) | copy-start | bytes 18436
  140.1 14.8 %collective-permute-start.5 = (bf16[128,1664]{1,0:T(8,128)(2,1)}, bf16[128,1664]{1,0:T(8,128)(2,1)}, u32[]{:S(2)}, u32[]{:S(2)}) collective-permute-start(bf16[128,1664]{1,0:T(8,128)(2,1)} %concatenate.44), channel_id=1, source_target_pairs={{0,2},{2,4},{4,6},{6,8},{8,10},{10,12},{12,14},{14,0},{1,3},{3,5},... | collective-permute-start | bytes 1277960 | tf_op jit(solution)/shard_map/ppermute | solution.py:238
  142.8 1.3 copy-start.14
  142.8 1.3 copy-start.15
  144.3 13.7 %collective-permute-start.9 = (bf16[128,1664]{1,0:T(8,128)(2,1)S(1)}, bf16[128,1664]{1,0:T(8,128)(2,1)S(1)}, u32[]{:S(2)}, u32[]{:S(2)}) collective-permute-start(bf16[128,1664]{1,0:T(8,128)(2,1)S(1)} %concatenate.47), channel_id=1, source_target_pairs={{0,14},{2,0},{4,2},{6,4},{8,6},{10,8},{12,10},{14,12},{1,15},{3,1}... | collective-permute-start | bytes 1277960 | tf_op jit(solution)/shard_map/ppermute | solution.py:241
  158.1 0.9 copy-start.9
  159.8 2.3 %copy-start.13 = (bf16[128,12]{1,0:T(8,128)(2,1)S(1)}, bf16[128,12]{1,0:T(8,128)(2,1)}, u32[]{:S(2)}) copy-start(bf16[128,12]{1,0:T(8,128)(2,1)} %max.70) | copy-start | bytes 9220
  159.8 2.3 %copy-start.18 = (bf16[128,12]{1,0:T(8,128)(2,1)S(1)}, bf16[128,12]{1,0:T(8,128)(2,1)}, u32[]{:S(2)}) copy-start(bf16[128,12]{1,0:T(8,128)(2,1)} %get-tuple-element.64) | copy-start | bytes 9220
  159.8 2.3 %copy-start.19 = (bf16[128,12]{1,0:T(8,128)(2,1)S(1)}, bf16[128,12]{1,0:T(8,128)(2,1)}, u32[]{:S(2)}) copy-start(bf16[128,12]{1,0:T(8,128)(2,1)} %get-tuple-element.65) | copy-start | bytes 9220
  163.0 14.4 %collective-permute-start.6 = (bf16[128,1664]{1,0:T(8,128)(2,1)}, bf16[128,1664]{1,0:T(8,128)(2,1)}, u32[]{:S(2)}, u32[]{:S(2)}) collective-permute-start(bf16[128,1664]{1,0:T(8,128)(2,1)} %concatenate.45), channel_id=1, source_target_pairs={{0,2},{2,4},{4,6},{6,8},{8,10},{10,12},{12,14},{14,0},{1,3},{3,5},... | collective-permute-start | bytes 1277960 | tf_op jit(solution)/shard_map/ppermute | solution.py:238
  165.6 1.6 copy-start.16
  165.6 1.6 copy-start.17
  168.1 14.5 %collective-permute-start.10 = (bf16[128,1664]{1,0:T(8,128)(2,1)}, bf16[128,1664]{1,0:T(8,128)(2,1)}, u32[]{:S(2)}, u32[]{:S(2)}) collective-permute-start(bf16[128,1664]{1,0:T(8,128)(2,1)} %concatenate.48), channel_id=1, source_target_pairs={{0,14},{2,0},{4,2},{6,4},{8,6},{10,8},{12,10},{14,12},{1,15},{3,1}... | collective-permute-start | bytes 1277960 | tf_op jit(solution)/shard_map/ppermute | solution.py:245
  180.6 12.8 %collective-permute-start.7 = (bf16[128,1664]{1,0:T(8,128)(2,1)S(1)}, bf16[128,1664]{1,0:T(8,128)(2,1)S(1)}, u32[]{:S(2)}, u32[]{:S(2)}) collective-permute-start(bf16[128,1664]{1,0:T(8,128)(2,1)S(1)} %concatenate.46), channel_id=1, source_target_pairs={{0,2},{2,4},{4,6},{6,8},{8,10},{10,12},{12,14},{14,0},{1,3},{3,5},... | collective-permute-start | bytes 1277960 | tf_op jit(solution)/shard_map/ppermute | solution.py:243
  193.4 0.8 copy-start.7
Sparse Core Ops, SparseCore 0:
  10.3 54.9 all-gather.1

commit v11 on v9

--- a/solution.py
+++ b/solution.py
@@ -103,7 +103,9 @@
         num_scalar_prefetch=1,
         grid=(sources,),
         in_specs=[
-            pl.BlockSpec((block_len, row_q.shape[1]), lambda t, info_ref: (t, 0)),
+            pl.BlockSpec(
+                (block_len, row_q.shape[1]), lambda t, info_ref: ((t - info_ref[0]) % sources, 0)
+            ),
             pl.BlockSpec(key_window.shape, lambda t, info_ref: (0, 0, 0)),
             pl.BlockSpec(value_window.shape, lambda t, info_ref: (0, 0, 0)),
         ],
@@ -160,11 +162,25 @@
     marks = jnp.any(listed, axis=2).reshape(1, -1).astype(jnp.bfloat16)
     spare = jnp.zeros((block_len, DH), jnp.bfloat16)
     spare = lax.dynamic_update_slice(spare, marks, (0, 0))
-    row_q = lax.all_gather(
-        jnp.concatenate([queries, spare], axis=1), "z", axis=0, tiled=True
-    )
-    marks_all = row_q.reshape(chips, block_len, -1)[:, 0, feature_width : feature_width + stripe_count * LAGS]
-    marks_all = marks_all.reshape(chips, stripe_count, LAGS).astype(jnp.int32)
+    own_q = jnp.concatenate([queries, spare], axis=1)
+    rightward = [(z, (z + 1) % chips) for z in range(chips)]
+    leftward = [(z, (z - 1) % chips) for z in range(chips)]
+    reach_r = chips // 2
+    reach_l = chips - 1 - reach_r
+    slots = [None] * chips
+    slots[0] = own_q
+    moving_r = own_q
+    moving_l = own_q
+    for step in range(1, reach_r + 1):
+        moving_r = lax.ppermute(moving_r, "z", rightward)
+        slots[(chips - step) % chips] = moving_r
+        if step <= reach_l:
+            moving_l = lax.ppermute(moving_l, "z", leftward)
+            slots[step] = moving_l
+    row_q = jnp.concatenate(slots, axis=0)
+    marks_rel = row_q.reshape(chips, block_len, -1)[:, 0, feature_width : feature_width + stripe_count * LAGS]
+    marks_rel = marks_rel.reshape(chips, stripe_count, LAGS).astype(jnp.int32)
+    marks_all = jnp.roll(marks_rel, chip, axis=0)
     mine = [
         lax.dynamic_index_in_dim(marks_all, 2 * chip + (core + j) % 2, axis=1, keepdims=False)
         for j in range(2)
@@ -207,10 +223,6 @@
     def block_for(offset):
         return lax.dynamic_index_in_dim(pair_out, (chip + offset) % chips, axis=0, keepdims=False)
 
-    rightward = [(z, (z + 1) % chips) for z in range(chips)]
-    leftward = [(z, (z - 1) % chips) for z in range(chips)]
-    reach_r = chips // 2
-    reach_l = chips - 1 - reach_r
     acc_r = block_for(reach_r)
     acc_l = block_for(-reach_l)
     for step in range(1, reach_r):

time: 187 us -> 198 us (1.059)
  the two profiles are of different devices: /device:TPU:50 before, /device:TPU:58 now
where the time goes in v11:
time: 198 us; the launch traced here: 197 us
  starting transfers between devices  68.1 us (34%)
  waiting for transfers between devices  58 us (29%)
  Pallas kernels  32.3 us (16%)
  local copies, waits for them, and re-layouts  19.8 us (10%)
  other arithmetic  17.2 us (9%)
    pallas_call x1, Pallas kernels, pair_partials(): pl.pallas_call(pair_kernel, grid_spec=grid_spec, out_shape=jax.ShapeDtype...  32.3 us
    ppermute x3, starting transfers between devices, per_device(): moving_l = lax.ppermute(moving_l, 'z', leftward)  25.2 us
    ppermute x4, waiting for transfers between devices, per_device(): moving_r = lax.ppermute(moving_r, 'z', rightward)  18.3 us
    ppermute x2, waiting for transfers between devices, passed_along(): return lax.ppermute(block, axis, route)  15.3 us
    ppermute x2, starting transfers between devices, per_device(): lax.ppermute(acc_l, 'z', leftward)  10.3 us
    ppermute x4, starting transfers between devices, per_device(): moving_r = lax.ppermute(moving_r, 'z', rightward)  10 us
    ppermute x3, waiting for transfers between devices, per_device(): lax.ppermute(acc_r, 'z', rightward)  8.53 us
    ppermute x1, waiting for transfers between devices, per_device(): final = [block_for(0), lax.ppermute(acc_r, 'z', rightward)]  7.91 us
  transfers between devices with their start and end apart: 18, of which 10 were waited for; matrix products, arithmetic and copies ran while one was open for 13% of the time, Pallas kernels for 0%

profile of v11, /device:TPU:58, one launch (start us, length us, event | category | flops | bytes accessed | tf_op | source)
XLA Modules:
  0.0 196.8 jit_solution(18301212296321518371)
XLA Ops:
  0.0 1.2 pad_maximum_fusion.3
  1.2 3.4 %collective-permute-start.7 = (bf16[2,128,1536]{2,1,0:T(8,128)(2,1)S(1)}, bf16[2,128,1536]{2,1,0:T(8,128)(2,1)S(1)}, u32[]{:S(2)}, u32[]{:S(2)}) collective-permute-start(bf16[2,128,1536]{2,1,0:T(8,128)(2,1)S(1)} %pad_maximum_fusion.3), channel_id=1, source_target_pairs={{0,16},{16,32},{32,48},{48,64},{64,80},{80,96},{96,112},{112,128},... | collective-permute-start | bytes 2359304 | tf_op jit(solution)/shard_map/ppermute | solution.py:21
  4.6 1.9 collective-permute-start.8
  7.3 0.9 and_reduce_fusion
  8.4 1.8 pad_maximum_fusion.4
  10.2 10.9 %collective-permute-start = (bf16[128,1664]{1,0:T(8,128)(2,1)S(1)}, bf16[128,1664]{1,0:T(8,128)(2,1)}, u32[]{:S(2)}, u32[]{:S(2)}) collective-permute-start(bf16[128,1664]{1,0:T(8,128)(2,1)S(1)} %get-tuple-element.62), channel_id=1, source_target_pairs={{0,14},{2,0},{4,2},{6,4},{8,6},{10,8},{12,10},{14,12},{1,15},{3,1}... | collective-permute-start | bytes 1277960 | tf_op jit(solution)/shard_map/ppermute | solution.py:178
  21.1 1.9 collective-permute-start.3
  23.1 1.9 collective-permute-start.9
  25.2 4.8 %collective-permute-done = bf16[128,1664]{1,0:T(8,128)(2,1)} collective-permute-done((bf16[128,1664]{1,0:T(8,128)(2,1)S(1)}, bf16[128,1664]{1,0:T(8,128)(2,1)}, u32[]{:S(2)}, u32[]{:S(2)}) %collective-permute-start) | collective-permute-done | bytes 426016 | tf_op jit(solution)/shard_map/ppermute | solution.py:178
  29.9 5.7 %collective-permute-start.1 = (bf16[128,1664]{1,0:T(8,128)(2,1)}, bf16[128,1664]{1,0:T(8,128)(2,1)S(1)}, u32[]{:S(2)}, u32[]{:S(2)}) collective-permute-start(bf16[128,1664]{1,0:T(8,128)(2,1)} %collective-permute-done), channel_id=1, source_target_pairs={{0,14},{2,0},{4,2},{6,4},{8,6},{10,8},{12,10},{14,12},{1,15},{3,1}... | collective-permute-start | bytes 1277960 | tf_op jit(solution)/shard_map/ppermute | solution.py:178
  35.6 1.9 collective-permute-start.4
  37.6 1.8 constant_dynamic-update-slice_fusion.6
  39.4 15.3 %collective-permute-done.8 = bf16[2,128,1536]{2,1,0:T(8,128)(2,1)S(1)} collective-permute-done((bf16[2,128,1536]{2,1,0:T(8,128)(2,1)S(1)}, bf16[2,128,1536]{2,1,0:T(8,128)(2,1)S(1)}, u32[]{:S(2)}, u32[]{:S(2)}) %collective-permute-start.8) | collective-permute-done | bytes 786464 | tf_op jit(solution)/shard_map/ppermute | solution.py:21
  54.7 1.3 pad_maximum_fusion.2
  56.0 2.0 %collective-permute-start.10 = (bf16[2,2,128,1536]{3,2,1,0:T(8,128)(2,1)}, bf16[2,2,128,1536]{3,2,1,0:T(8,128)(2,1)}, u32[]{:S(2)}, u32[]{:S(2)}) collective-permute-start(bf16[2,2,128,1536]{3,2,1,0:T(8,128)(2,1)} %pad_maximum_fusion.2), channel_id=1, source_target_pairs={{0,1},{1,0},{2,3},{3,2},{4,5},{5,4},{6,7},{7,6},{8,9},{9,8},{10,11... | collective-permute-start | bytes 4718600 | tf_op jit(solution)/shard_map/ppermute | solution.py:145
  58.2 4.3 %collective-permute-start.5 = (bf16[128,1664]{1,0:T(8,128)(2,1)S(1)}, bf16[128,1664]{1,0:T(8,128)(2,1)S(1)}, u32[]{:S(2)}, u32[]{:S(2)}) collective-permute-start(bf16[128,1664]{1,0:T(8,128)(2,1)S(1)} %collective-permute-done.4), channel_id=1, source_target_pairs={{0,2},{2,4},{4,6},{6,8},{8,10},{10,12},{12,14},{14,0},{1,3},{3,5},... | collective-permute-start | bytes 1277960 | tf_op jit(solution)/shard_map/ppermute | solution.py:175
  62.5 1.2 slice_bitcast_fusion.2
  63.7 8.6 %collective-permute-start.2 = (bf16[128,1664]{1,0:T(8,128)(2,1)S(1)}, bf16[128,1664]{1,0:T(8,128)(2,1)S(1)}, u32[]{:S(2)}, u32[]{:S(2)}) collective-permute-start(bf16[128,1664]{1,0:T(8,128)(2,1)S(1)} %collective-permute-done.1), channel_id=1, source_target_pairs={{0,14},{2,0},{4,2},{6,4},{8,6},{10,8},{12,10},{14,12},{1,15},{3,1}... | collective-permute-start | bytes 1277960 | tf_op jit(solution)/shard_map/ppermute | solution.py:178
  72.4 7.2 %collective-permute-done.5 = bf16[128,1664]{1,0:T(8,128)(2,1)S(1)} collective-permute-done((bf16[128,1664]{1,0:T(8,128)(2,1)S(1)}, bf16[128,1664]{1,0:T(8,128)(2,1)S(1)}, u32[]{:S(2)}, u32[]{:S(2)}) %collective-permute-start.5) | collective-permute-done | bytes 426016 | tf_op jit(solution)/shard_map/ppermute | solution.py:175
  79.6 1.9 collective-permute-start.6
  81.5 0.8 constant_dynamic-update-slice_fusion.5
  82.3 0.8 constant_dynamic-update-slice_fusion.4
  83.1 11.2 %collective-permute-done.6 = bf16[128,1664]{1,0:T(8,128)(2,1)S(1)} collective-permute-done((bf16[128,1664]{1,0:T(8,128)(2,1)S(1)}, bf16[128,1664]{1,0:T(8,128)(2,1)S(1)}, u32[]{:S(2)}, u32[]{:S(2)}) %collective-permute-start.6) | collective-permute-done | bytes 426016 | tf_op jit(solution)/shard_map/ppermute | solution.py:175
  94.3 0.8 constant_dynamic-update-slice_fusion.3
  95.1 0.8 constant_dynamic-update-slice_fusion.2
  95.9 0.8 constant_dynamic-update-slice_fusion.1
  96.7 0.8 constant_dynamic-update-slice_fusion.q_ref
  97.5 0.7 slice.509
  98.7 0.6 pad_add_fusion.1.info_ref
  99.4 1.5 slice_bitcast_fusion.1
  101.0 1.6 pad_maximum_fusion.1.v_ref
  102.6 1.7 pad_maximum_fusion.k_ref
  104.3 32.3 %shard_map.55 = bf16[1024,1664]{1,0:T(8,128)(2,1)} custom-call(s32[50]{0:T(128)} %pad_add_fusion.1.info_ref, bf16[1024,1664]{1,0:T(8,128)(2,1)} %constant_dynamic-update-slice_fusion.q_ref, bf16[2,384,1536]{2,1,0:T(8,128)(2,1)} %pad_maximum_fusion.k_ref, bf16[2,384,1536]{2,1,0:T(8,128)(2,1)} %pad_maximum_fusion.1.v_ref), custom_call_target="tpu_custom_call" | custom-call | flops 3221225472 | bytes 11534336 | tf_op jit(solution)/shard_map/pallas_call | solution.py:115
  136.6 2.2 %constant_dynamic-slice_fusion.7 = (bf16[1,128,1664]{2,1,0:T(8,128)(2,1)S(1)}, bf16[1,128,1664]{2,1,0:T(8,128)(2,1)S(1)}, bf16[1,128,1664]{2,1,0:T(8,128)(2,1)S(...) fusion(bf16[8,128,1664]{2,1,0:T(8,128)(2,1)} %bitcast.119, ...), kind=kLoop, calls=%fused_computation.171 | loop fusion | bytes 6815776 | tf_op jit(solution)/shard_map/jit(dynamic_index_in_dim)/dynamic_slice | solution.py:224
  138.8 1.0 copy.21
  139.8 1.9 collective-permute-start.11
  142.0 0.6 slice_convert_fusion.10
  143.2 0.3 copy.25
  143.5 5.1 %collective-permute-start.15 = (bf16[128,1664]{0,1:T(8,128)(2,1)S(1)}, bf16[128,1664]{0,1:T(8,128)(2,1)}, u32[]{:S(2)}, u32[]{:S(2)}) collective-permute-start(bf16[128,1664]{0,1:T(8,128)(2,1)S(1)} %bitcast.136), channel_id=1, source_target_pairs={{0,14},{2,0},{4,2},{6,4},{8,6},{10,8},{12,10},{14,12},{1,15},{3,1}... | collective-permute-start | bytes 1277960 | tf_op jit(solution)/shard_map/ppermute | solution.py:232
  148.9 0.3 copy.27
  149.5 0.6 slice_convert_fusion.3
  150.1 3.9 %collective-permute-done.11 = bf16[128,1664]{0,1:T(8,128)(2,1)} collective-permute-done((bf16[128,1664]{0,1:T(8,128)(2,1)}, bf16[128,1664]{0,1:T(8,128)(2,1)}, u32[]{:S(2)}, u32[]{:S(2)}) %collective-permute-start.11) | collective-permute-done | bytes 426016 | tf_op jit(solution)/shard_map/ppermute | solution.py:229
  154.0 0.7 slice_convert_fusion.11
  154.7 0.8 fusion.31
  155.5 1.2 fusion.12
  156.7 0.6 concatenate.57
  157.3 1.9 collective-permute-start.12
  159.3 0.7 slice_convert_fusion.4
  160.0 0.8 fusion.22
  160.8 1.2 fusion.6
  162.0 0.6 concatenate.60
  162.6 5.1 %collective-permute-start.16 = (bf16[128,1664]{0,1:T(8,128)(2,1)S(1)}, bf16[128,1664]{0,1:T(8,128)(2,1)S(1)}, u32[]{:S(2)}, u32[]{:S(2)}) collective-permute-start(bf16[128,1664]{0,1:T(8,128)(2,1)S(1)} %concatenate.60), channel_id=1, source_target_pairs={{0,14},{2,0},{4,2},{6,4},{8,6},{10,8},{12,10},{14,12},{1,15},{3,1}... | collective-permute-start | bytes 1277960 | tf_op jit(solution)/shard_map/ppermute | solution.py:232
  167.8 2.6 %collective-permute-done.12 = bf16[128,1664]{0,1:T(8,128)(2,1)S(1)} collective-permute-done((bf16[128,1664]{0,1:T(8,128)(2,1)S(1)}, bf16[128,1664]{0,1:T(8,128)(2,1)S(1)}, u32[]{:S(2)}, u32[]{:S(2)}) %collective-permute-start.12) | collective-permute-done | bytes 426016 | tf_op jit(solution)/shard_map/ppermute | solution.py:229
  170.6 0.6 concatenate.58
  171.2 1.9 collective-permute-start.13
  173.2 1.8 collective-permute-done.16
  175.1 0.6 concatenate.61
  175.8 5.6 %collective-permute-start.17 = (bf16[128,1664]{0,1:T(8,128)(2,1)S(1)}, bf16[128,1664]{0,1:T(8,128)(2,1)S(1)}, u32[]{:S(2)}, u32[]{:S(2)}) collective-permute-start(bf16[128,1664]{0,1:T(8,128)(2,1)S(1)} %concatenate.61), channel_id=1, source_target_pairs={{0,14},{2,0},{4,2},{6,4},{8,6},{10,8},{12,10},{14,12},{1,15},{3,1}... | collective-permute-start | bytes 1277960 | tf_op jit(solution)/shard_map/ppermute | solution.py:236
  181.4 2.0 %collective-permute-done.13 = bf16[128,1664]{0,1:T(8,128)(2,1)S(1)} collective-permute-done((bf16[128,1664]{0,1:T(8,128)(2,1)S(1)}, bf16[128,1664]{0,1:T(8,128)(2,1)S(1)}, u32[]{:S(2)}, u32[]{:S(2)}) %collective-permute-start.13) | collective-permute-done | bytes 426016 | tf_op jit(solution)/shard_map/ppermute | solution.py:229
  183.6 0.6 concatenate.59
  184.3 1.9 collective-permute-start.14
  186.2 1.5 collective-permute-done.17
  187.7 7.9 %collective-permute-done.14 = bf16[128,1664]{0,1:T(8,128)(2,1)S(1)} collective-permute-done((bf16[128,1664]{0,1:T(8,128)(2,1)S(1)}, bf16[128,1664]{0,1:T(8,128)(2,1)S(1)}, u32[]{:S(2)}, u32[]{:S(2)}) %collective-permute-start.14) | collective-permute-done | bytes 426016 | tf_op jit(solution)/shard_map/ppermute | solution.py:234
  195.9 0.9 copy.28
  (71 shorter events, 3.6 us)
Async XLA Ops:
  1.2 38.2 %collective-permute-start.7 = (bf16[2,128,1536]{2,1,0:T(8,128)(2,1)S(1)}, bf16[2,128,1536]{2,1,0:T(8,128)(2,1)S(1)}, u32[]{:S(2)}, u32[]{:S(2)}) collective-permute-start(bf16[2,128,1536]{2,1,0:T(8,128)(2,1)S(1)} %pad_maximum_fusion.3), channel_id=1, source_target_pairs={{0,16},{16,32},{32,48},{48,64},{64,80},{80,96},{96,112},{112,128},... | collective-permute-start | bytes 2359304 | tf_op jit(solution)/shard_map/ppermute | solution.py:21
  4.6 50.1 %collective-permute-start.8 = (bf16[2,128,1536]{2,1,0:T(8,128)(2,1)S(1)}, bf16[2,128,1536]{2,1,0:T(8,128)(2,1)S(1)}, u32[]{:S(2)}, u32[]{:S(2)}) collective-permute-start(bf16[2,128,1536]{2,1,0:T(8,128)(2,1)S(1)} %pad_maximum_fusion.3), channel_id=1, source_target_pairs={{0,32},{16,48},{32,64},{48,80},{64,96},{80,112},{96,128},{112,144}... | collective-permute-start | bytes 2359304 | tf_op jit(solution)/shard_map/ppermute | solution.py:21
  10.2 19.7 %collective-permute-start = (bf16[128,1664]{1,0:T(8,128)(2,1)S(1)}, bf16[128,1664]{1,0:T(8,128)(2,1)}, u32[]{:S(2)}, u32[]{:S(2)}) collective-permute-start(bf16[128,1664]{1,0:T(8,128)(2,1)S(1)} %get-tuple-element.62), channel_id=1, source_target_pairs={{0,14},{2,0},{4,2},{6,4},{8,6},{10,8},{12,10},{14,12},{1,15},{3,1}... | collective-permute-start | bytes 1277960 | tf_op jit(solution)/shard_map/ppermute | solution.py:178
  21.1 14.5 %collective-permute-start.3 = (bf16[128,1664]{1,0:T(8,128)(2,1)S(1)}, bf16[128,1664]{1,0:T(8,128)(2,1)S(1)}, u32[]{:S(2)}, u32[]{:S(2)}) collective-permute-start(bf16[128,1664]{1,0:T(8,128)(2,1)S(1)} %get-tuple-element.62), channel_id=1, source_target_pairs={{0,2},{2,4},{4,6},{6,8},{8,10},{10,12},{12,14},{14,0},{1,3},{3,5},... | collective-permute-start | bytes 1277960 | tf_op jit(solution)/shard_map/ppermute | solution.py:175
  23.1 39.4 %collective-permute-start.9 = (bf16[2,128,1536]{2,1,0:T(8,128)(2,1)S(1)}, bf16[2,128,1536]{2,1,0:T(8,128)(2,1)}, u32[]{:S(2)}, u32[]{:S(2)}) collective-permute-start(bf16[2,128,1536]{2,1,0:T(8,128)(2,1)S(1)} %pad_maximum_fusion.3), channel_id=1, source_target_pairs={{0,1},{1,0},{2,3},{3,2},{4,5},{5,4},{6,7},{7,6},{8,9},{9,8},{10,11... | collective-permute-start | bytes 2359304 | tf_op jit(solution)/shard_map/ppermute | solution.py:144
  29.9 33.7 %collective-permute-start.1 = (bf16[128,1664]{1,0:T(8,128)(2,1)}, bf16[128,1664]{1,0:T(8,128)(2,1)S(1)}, u32[]{:S(2)}, u32[]{:S(2)}) collective-permute-start(bf16[128,1664]{1,0:T(8,128)(2,1)} %collective-permute-done), channel_id=1, source_target_pairs={{0,14},{2,0},{4,2},{6,4},{8,6},{10,8},{12,10},{14,12},{1,15},{3,1}... | collective-permute-start | bytes 1277960 | tf_op jit(solution)/shard_map/ppermute | solution.py:178
  35.6 22.5 %copy-start.2 = (bf16[128,1664]{1,0:T(8,128)(2,1)}, bf16[128,1664]{1,0:T(8,128)(2,1)S(1)}, u32[]{:S(2)}) copy-start(bf16[128,1664]{1,0:T(8,128)(2,1)S(1)} %collective-permute-done.3) | copy-start | bytes 1277956
  35.6 22.5 %collective-permute-start.4 = (bf16[128,1664]{1,0:T(8,128)(2,1)S(1)}, bf16[128,1664]{1,0:T(8,128)(2,1)S(1)}, u32[]{:S(2)}, u32[]{:S(2)}) collective-permute-start(bf16[128,1664]{1,0:T(8,128)(2,1)S(1)} %collective-permute-done.3), channel_id=1, source_target_pairs={{0,2},{2,4},{4,6},{6,8},{8,10},{10,12},{12,14},{14,0},{1,3},{3,5},... | collective-permute-start | bytes 1277960 | tf_op jit(solution)/shard_map/ppermute | solution.py:175
  56.0 16.3 %copy-start = (bf16[128,1536]{1,0:T(8,128)(2,1)S(1)}, bf16[128,1536]{1,0:T(8,128)(2,1)}, u32[]{:S(2)}) copy-start(bf16[128,1536]{1,0:T(8,128)(2,1)} %param.7) | copy-start | bytes 1179652
  56.0 16.3 %copy-start.1 = (bf16[128,1536]{1,0:T(8,128)(2,1)S(1)}, bf16[128,1536]{1,0:T(8,128)(2,1)}, u32[]{:S(2)}) copy-start(bf16[128,1536]{1,0:T(8,128)(2,1)} %param.6) | copy-start | bytes 1179652
  56.0 43.4 %collective-permute-start.10 = (bf16[2,2,128,1536]{3,2,1,0:T(8,128)(2,1)}, bf16[2,2,128,1536]{3,2,1,0:T(8,128)(2,1)}, u32[]{:S(2)}, u32[]{:S(2)}) collective-permute-start(bf16[2,2,128,1536]{3,2,1,0:T(8,128)(2,1)} %pad_maximum_fusion.2), channel_id=1, source_target_pairs={{0,1},{1,0},{2,3},{3,2},{4,5},{5,4},{6,7},{7,6},{8,9},{9,8},{10,11... | collective-permute-start | bytes 4718600 | tf_op jit(solution)/shard_map/ppermute | solution.py:145
  58.2 21.4 %collective-permute-start.5 = (bf16[128,1664]{1,0:T(8,128)(2,1)S(1)}, bf16[128,1664]{1,0:T(8,128)(2,1)S(1)}, u32[]{:S(2)}, u32[]{:S(2)}) collective-permute-start(bf16[128,1664]{1,0:T(8,128)(2,1)S(1)} %collective-permute-done.4), channel_id=1, source_target_pairs={{0,2},{2,4},{4,6},{6,8},{8,10},{10,12},{12,14},{14,0},{1,3},{3,5},... | collective-permute-start | bytes 1277960 | tf_op jit(solution)/shard_map/ppermute | solution.py:175
  63.7 18.7 %collective-permute-start.2 = (bf16[128,1664]{1,0:T(8,128)(2,1)S(1)}, bf16[128,1664]{1,0:T(8,128)(2,1)S(1)}, u32[]{:S(2)}, u32[]{:S(2)}) collective-permute-start(bf16[128,1664]{1,0:T(8,128)(2,1)S(1)} %collective-permute-done.1), channel_id=1, source_target_pairs={{0,14},{2,0},{4,2},{6,4},{8,6},{10,8},{12,10},{14,12},{1,15},{3,1}... | collective-permute-start | bytes 1277960 | tf_op jit(solution)/shard_map/ppermute | solution.py:178
  72.4 24.3 %copy-start.3 = (bf16[128,1664]{1,0:T(8,128)(2,1)S(1)}, bf16[128,1664]{1,0:T(8,128)(2,1)}, u32[]{:S(2)}) copy-start(bf16[128,1664]{1,0:T(8,128)(2,1)} %copy-done.2) | copy-start | bytes 1277956
  79.6 14.7 %collective-permute-start.6 = (bf16[128,1664]{1,0:T(8,128)(2,1)S(1)}, bf16[128,1664]{1,0:T(8,128)(2,1)S(1)}, u32[]{:S(2)}, u32[]{:S(2)}) collective-permute-start(bf16[128,1664]{1,0:T(8,128)(2,1)S(1)} %collective-permute-done.5), channel_id=1, source_target_pairs={{0,2},{2,4},{4,6},{6,8},{8,10},{10,12},{12,14},{14,0},{1,3},{3,5},... | collective-permute-start | bytes 1277960 | tf_op jit(solution)/shard_map/ppermute | solution.py:175
  139.8 14.2 %collective-permute-start.11 = (bf16[128,1664]{0,1:T(8,128)(2,1)}, bf16[128,1664]{0,1:T(8,128)(2,1)}, u32[]{:S(2)}, u32[]{:S(2)}) collective-permute-start(bf16[128,1664]{0,1:T(8,128)(2,1)} %bitcast.137), channel_id=1, source_target_pairs={{0,2},{2,4},{4,6},{6,8},{8,10},{10,12},{12,14},{14,0},{1,3},{3,5},... | collective-permute-start | bytes 1277960 | tf_op jit(solution)/shard_map/ppermute | solution.py:229
  143.5 15.8 %collective-permute-start.15 = (bf16[128,1664]{0,1:T(8,128)(2,1)S(1)}, bf16[128,1664]{0,1:T(8,128)(2,1)}, u32[]{:S(2)}, u32[]{:S(2)}) collective-permute-start(bf16[128,1664]{0,1:T(8,128)(2,1)S(1)} %bitcast.136), channel_id=1, source_target_pairs={{0,14},{2,0},{4,2},{6,4},{8,6},{10,8},{12,10},{14,12},{1,15},{3,1}... | collective-permute-start | bytes 1277960 | tf_op jit(solution)/shard_map/ppermute | solution.py:232
  157.3 13.0 %collective-permute-start.12 = (bf16[128,1664]{0,1:T(8,128)(2,1)S(1)}, bf16[128,1664]{0,1:T(8,128)(2,1)S(1)}, u32[]{:S(2)}, u32[]{:S(2)}) collective-permute-start(bf16[128,1664]{0,1:T(8,128)(2,1)S(1)} %concatenate.57), channel_id=1, source_target_pairs={{0,2},{2,4},{4,6},{6,8},{8,10},{10,12},{12,14},{14,0},{1,3},{3,5},... | collective-permute-start | bytes 1277960 | tf_op jit(solution)/shard_map/ppermute | solution.py:229
  162.6 12.3 %collective-permute-start.16 = (bf16[128,1664]{0,1:T(8,128)(2,1)S(1)}, bf16[128,1664]{0,1:T(8,128)(2,1)S(1)}, u32[]{:S(2)}, u32[]{:S(2)}) collective-permute-start(bf16[128,1664]{0,1:T(8,128)(2,1)S(1)} %concatenate.60), channel_id=1, source_target_pairs={{0,14},{2,0},{4,2},{6,4},{8,6},{10,8},{12,10},{14,12},{1,15},{3,1}... | collective-permute-start | bytes 1277960 | tf_op jit(solution)/shard_map/ppermute | solution.py:232
  171.2 12.2 %collective-permute-start.13 = (bf16[128,1664]{0,1:T(8,128)(2,1)S(1)}, bf16[128,1664]{0,1:T(8,128)(2,1)S(1)}, u32[]{:S(2)}, u32[]{:S(2)}) collective-permute-start(bf16[128,1664]{0,1:T(8,128)(2,1)S(1)} %concatenate.58), channel_id=1, source_target_pairs={{0,2},{2,4},{4,6},{6,8},{8,10},{10,12},{12,14},{14,0},{1,3},{3,5},... | collective-permute-start | bytes 1277960 | tf_op jit(solution)/shard_map/ppermute | solution.py:229
  175.8 11.9 %collective-permute-start.17 = (bf16[128,1664]{0,1:T(8,128)(2,1)S(1)}, bf16[128,1664]{0,1:T(8,128)(2,1)S(1)}, u32[]{:S(2)}, u32[]{:S(2)}) collective-permute-start(bf16[128,1664]{0,1:T(8,128)(2,1)S(1)} %concatenate.61), channel_id=1, source_target_pairs={{0,14},{2,0},{4,2},{6,4},{8,6},{10,8},{12,10},{14,12},{1,15},{3,1}... | collective-permute-start | bytes 1277960 | tf_op jit(solution)/shard_map/ppermute | solution.py:236
  184.3 11.3 %collective-permute-start.14 = (bf16[128,1664]{0,1:T(8,128)(2,1)S(1)}, bf16[128,1664]{0,1:T(8,128)(2,1)S(1)}, u32[]{:S(2)}, u32[]{:S(2)}) collective-permute-start(bf16[128,1664]{0,1:T(8,128)(2,1)S(1)} %concatenate.59), channel_id=1, source_target_pairs={{0,2},{2,4},{4,6},{6,8},{8,10},{10,12},{12,14},{14,0},{1,3},{3,5},... | collective-permute-start | bytes 1277960 | tf_op jit(solution)/shard_map/ppermute | solution.py:234

commit v12 on v9

--- a/solution.py
+++ b/solution.py
@@ -37,12 +37,14 @@
     return total
 
 
-def pair_kernel(info_ref, q_ref, k_ref, v_ref, out_ref, stat_ref):
+def pair_kernel(info_ref, q_ref, k0_ref, k1_ref, v0_ref, v1_ref, out_ref, stat_ref):
     t = pl.program_id(0)
     chip = info_ref[0]
     core = info_ref[1]
     block_len = out_ref.shape[0]
-    feature_width = k_ref.shape[2]
+    feature_width = k0_ref.shape[1]
+    k_refs = (k0_ref, k1_ref)
+    v_refs = (v0_ref, v1_ref)
     head_count = feature_width // DH
     column = 2 * t + core
     q_pos = lax.broadcasted_iota(jnp.int32, (block_len, 2 * block_len), 0)
@@ -70,7 +72,7 @@
         q = q_ref[:, cols]
         scores = []
         for j in range(2):
-            keys = k_ref[j, pl.ds(starts[j], 2 * block_len), cols]
+            keys = k_refs[j][pl.ds(starts[j], 2 * block_len), cols]
             s = lax.dot_general(q, keys, nt, preferred_element_type=jnp.float32)
             scores.append(jnp.where(masks[j], s * scaling, NEG_FILL))
         highest = jnp.maximum(
@@ -83,7 +85,7 @@
             part_total = jnp.sum(w, axis=1, keepdims=True)
             part = jnp.dot(
                 w.astype(jnp.bfloat16),
-                v_ref[j, pl.ds(starts[j], 2 * block_len), cols],
+                v_refs[j][pl.ds(starts[j], 2 * block_len), cols],
                 preferred_element_type=jnp.float32,
             )
             total = part_total if total is None else total + part_total
@@ -95,17 +97,19 @@
 
 
 def pair_partials(info, row_q, key_window, value_window):
-    block_len = key_window.shape[1] // LAGS
+    block_len = key_window[0].shape[0] // LAGS
     sources = row_q.shape[0] // block_len
-    feature_width = key_window.shape[2]
+    feature_width = key_window[0].shape[1]
     head_count = feature_width // DH
     grid_spec = pltpu.PrefetchScalarGridSpec(
         num_scalar_prefetch=1,
         grid=(sources,),
         in_specs=[
             pl.BlockSpec((block_len, row_q.shape[1]), lambda t, info_ref: (t, 0)),
-            pl.BlockSpec(key_window.shape, lambda t, info_ref: (0, 0, 0)),
-            pl.BlockSpec(value_window.shape, lambda t, info_ref: (0, 0, 0)),
+            pl.BlockSpec(key_window[0].shape, lambda t, info_ref: (0, 0)),
+            pl.BlockSpec(key_window[0].shape, lambda t, info_ref: (0, 0)),
+            pl.BlockSpec(key_window[0].shape, lambda t, info_ref: (0, 0)),
+            pl.BlockSpec(key_window[0].shape, lambda t, info_ref: (0, 0)),
         ],
         out_specs=pl.BlockSpec((block_len, row_q.shape[1]), lambda t, info_ref: (t, 0)),
         scratch_shapes=[pltpu.VMEM((block_len, row_q.shape[1] - feature_width), jnp.float32)],
@@ -120,7 +124,7 @@
             bytes_accessed=2 * sources * block_len * row_q.shape[1] * 2
             + 2 * 2 * LAGS * block_len * feature_width * 2,
         ),
-    )(info, row_q, key_window, value_window)
+    )(info, row_q, *key_window, *value_window)
 
 
 def per_device(queries, keys, values, adjacency, counts):
@@ -138,17 +142,11 @@
 
     swap = [(0, 1), (1, 0)]
     lag_1 = passed_along(stacked, "pb", 1)
-    lag_2 = passed_along(stacked, "pb", 2)
-    partner_0 = lax.ppermute(stacked, "core", swap)
-    partner_12 = lax.ppermute(jnp.stack([lag_1, lag_2]), "core", swap)
+    lag_2 = passed_along(lag_1, "pb", 1)
     own = [stacked, lag_1, lag_2]
-    partner = [partner_0, partner_12[0], partner_12[1]]
-    key_window = jnp.stack(
-        [jnp.concatenate([x[0] for x in own]), jnp.concatenate([x[0] for x in partner])]
-    )
-    value_window = jnp.stack(
-        [jnp.concatenate([x[1] for x in own]), jnp.concatenate([x[1] for x in partner])]
-    )
+    partner = [lax.ppermute(x, "core", swap) for x in own]
+    key_window = [jnp.concatenate([x[0] for x in side]) for side in (own, partner)]
+    value_window = [jnp.concatenate([x[1] for x in side]) for side in (own, partner)]
 
     lag_ids = jnp.arange(LAGS, dtype=jnp.int32)
     class_ids = jnp.arange(stripe_count, dtype=jnp.int32)

time: 187 us -> 178 us (0.952)
  the two profiles are of different devices: /device:TPU:50 before, /device:TPU:32 now
where the time goes in v12:
time: 178 us; the launch traced here: 177 us
  waiting for transfers between devices  64.4 us (36%)
  starting transfers between devices  40.2 us (23%)
  Pallas kernels  32.2 us (18%)
  other arithmetic  15.3 us (9%)
  between operations  14.6 us (8%)
  local copies, waits for them, and re-layouts  10.6 us (6%)
    ppermute x2, waiting for transfers between devices, passed_along(): return lax.ppermute(block, axis, route)  38.6 us
    pallas_call x1, Pallas kernels, pair_partials(): pl.pallas_call(pair_kernel, grid_spec=grid_spec, out_shape=jax.ShapeDtype...  32.2 us
    ppermute x2, starting transfers between devices, per_device(): lax.ppermute(acc_l, 'z', leftward)  13.7 us
    ppermute x3, waiting for transfers between devices, per_device(): lax.ppermute(acc_r, 'z', rightward)  12.6 us
    ppermute x1, waiting for transfers between devices, per_device(): final = [block_for(0), lax.ppermute(acc_r, 'z', rightward)]  9.27 us
    ppermute x3, starting transfers between devices, per_device(): lax.ppermute(acc_r, 'z', rightward)  7.93 us
    ppermute x3, starting transfers between devices, per_device(): partner = [lax.ppermute(x, 'core', swap) for x in own]  5.75 us
    ppermute x1, starting transfers between devices, per_device(): final.append(lax.ppermute(acc_l, 'z', leftward))  5.6 us
  transfers between devices with their start and end apart: 13, of which 10 were waited for; matrix products, arithmetic and copies ran while one was open for 10% of the time, Pallas kernels for 0%

profile of v12, /device:TPU:32, one launch (start us, length us, event | category | flops | bytes accessed | tf_op | source)
XLA Modules:
  0.0 177.4 jit_solution(8423220508526334062)
XLA Ops:
  6.5 0.1 iota_add_fusion
  7.3 0.9 and_reduce_fusion
  8.1 0.1 copy.17
  8.3 0.1 convert_element_type.194
  8.4 1.8 %pad_maximum_fusion.5 = bf16[128,1664]{1,0:T(8,128)(2,1)} fusion(bf16[128,128]{1,0:T(8,128)(2,1)S(1)} %pad_convert_fusion, bf16[128,1536]{1,0:T(8,128)(2,1)} %param.5), kind=kLoop, calls=%fused_computation.32 | loop fusion | flops 851968 | bytes 851968 | tf_op jit(solution)/shard_map/concatenate | solution.py:162
  10.2 1.2 pad_maximum_fusion.4
  11.4 3.4 %collective-permute-start = (bf16[2,128,1536]{2,1,0:T(8,128)(2,1)S(1)}, bf16[2,128,1536]{2,1,0:T(8,128)(2,1)S(1)}, u32[]{:S(2)}, u32[]{:S(2)}) collective-permute-start(bf16[2,128,1536]{2,1,0:T(8,128)(2,1)S(1)} %pad_maximum_fusion.4), channel_id=1, source_target_pairs={{0,16},{16,32},{32,48},{48,64},{64,80},{80,96},{96,112},{112,128},... | collective-permute-start | bytes 2359304 | tf_op jit(solution)/shard_map/ppermute | solution.py:21
  14.8 1.9 %collective-permute-start.2 = (bf16[2,128,1536]{2,1,0:T(8,128)(2,1)S(1)}, bf16[2,128,1536]{2,1,0:T(8,128)(2,1)S(1)}, u32[]{:S(2)}, u32[]{:S(2)}) collective-permute-start(bf16[2,128,1536]{2,1,0:T(8,128)(2,1)S(1)} %pad_maximum_fusion.4), channel_id=1, source_target_pairs={{0,1},{1,0},{2,3},{3,2},{4,5},{5,4},{6,7},{7,6},{8,9},{9,8},{10,11... | collective-permute-start | bytes 2359304 | tf_op jit(solution)/shard_map/ppermute | solution.py:147
  16.9 19.0 %collective-permute-done = bf16[2,128,1536]{2,1,0:T(8,128)(2,1)S(1)} collective-permute-done((bf16[2,128,1536]{2,1,0:T(8,128)(2,1)S(1)}, bf16[2,128,1536]{2,1,0:T(8,128)(2,1)S(1)}, u32[]{:S(2)}, u32[]{:S(2)}) %collective-permute-start) | collective-permute-done | bytes 786464 | tf_op jit(solution)/shard_map/ppermute | solution.py:21
  35.9 1.9 %collective-permute-start.1 = (bf16[2,128,1536]{2,1,0:T(8,128)(2,1)S(1)}, bf16[2,128,1536]{2,1,0:T(8,128)(2,1)S(1)}, u32[]{:S(2)}, u32[]{:S(2)}) collective-permute-start(bf16[2,128,1536]{2,1,0:T(8,128)(2,1)S(1)} %collective-permute-done), channel_id=1, source_target_pairs={{0,16},{16,32},{32,48},{48,64},{64,80},{80,96},{96,112},{112,128},... | collective-permute-start | bytes 2359304 | tf_op jit(solution)/shard_map/ppermute | solution.py:21
  37.8 1.9 %collective-permute-start.3 = (bf16[2,128,1536]{2,1,0:T(8,128)(2,1)S(1)}, bf16[2,128,1536]{2,1,0:T(8,128)(2,1)S(1)}, u32[]{:S(2)}, u32[]{:S(2)}) collective-permute-start(bf16[2,128,1536]{2,1,0:T(8,128)(2,1)S(1)} %collective-permute-done), channel_id=1, source_target_pairs={{0,1},{1,0},{2,3},{3,2},{4,5},{5,4},{6,7},{7,6},{8,9},{9,8},{10,11... | collective-permute-start | bytes 2359304 | tf_op jit(solution)/shard_map/ppermute | solution.py:147
  39.8 19.7 %collective-permute-done.1 = bf16[2,128,1536]{2,1,0:T(8,128)(2,1)S(1)} collective-permute-done((bf16[2,128,1536]{2,1,0:T(8,128)(2,1)S(1)}, bf16[2,128,1536]{2,1,0:T(8,128)(2,1)S(1)}, u32[]{:S(2)}, u32[]{:S(2)}) %collective-permute-start.1) | collective-permute-done | bytes 786464 | tf_op jit(solution)/shard_map/ppermute | solution.py:21
  59.5 1.9 %collective-permute-start.4 = (bf16[2,128,1536]{2,1,0:T(8,128)(2,1)S(1)}, bf16[2,128,1536]{2,1,0:T(8,128)(2,1)S(1)}, u32[]{:S(2)}, u32[]{:S(2)}) collective-permute-start(bf16[2,128,1536]{2,1,0:T(8,128)(2,1)S(1)} %collective-permute-done.1), channel_id=1, source_target_pairs={{0,1},{1,0},{2,3},{3,2},{4,5},{5,4},{6,7},{7,6},{8,9},{9,8},{10,11... | collective-permute-start | bytes 2359304 | tf_op jit(solution)/shard_map/ppermute | solution.py:147
  61.4 0.1 slice_bitcast_fusion.3
  61.5 1.6 pad_maximum_fusion
  63.2 0.5 collective-permute-done.4
  63.7 1.5 pad_maximum_fusion.1
  65.3 0.2 all-gather.2.cloned.1.call-done.q_ref
  65.4 0.7 slice.499
  66.2 0.1 copy.29
  66.3 0.1 copy.19
  66.4 0.1 reshape.106
  66.5 0.6 pad_add_fusion.1.info_ref
  67.1 32.2 %shard_map.55 = bf16[1024,1664]{1,0:T(8,128)(2,1)} custom-call(s32[50]{0:T(128)} %pad_add_fusion.1.info_ref, bf16[1024,1664]{1,0:T(8,128)(2,1)} %all-gather.2.cloned.1.call-done.q_ref, bf16[384,1536]{1,0:T(8,128)(2,1)} %get-tuple-element.74.k0_ref, bf16[384,1536]{1,0:T(8,128)(2,1)} %get-tuple-element.76.k1_ref, bf16[384,1536]{1,0:T(8,128)(2,1)} %get-tuple-element.75.v0_ref, ...), custom_call_target="tpu_custom_call" | custom-call | flops 3221225472 | bytes 11534336 | tf_op jit(solution)/shard_map/pallas_call | solution.py:117
  99.4 2.2 %constant_dynamic-slice_fusion.7 = (bf16[1,128,1664]{2,1,0:T(8,128)(2,1)S(1)}, bf16[1,128,1664]{2,1,0:T(8,128)(2,1)S(1)}, bf16[1,128,1664]{2,1,0:T(8,128)(2,1)S(...) fusion(bf16[8,128,1664]{2,1,0:T(8,128)(2,1)} %bitcast.109, ...), kind=kLoop, calls=%fused_computation.159 | loop fusion | bytes 6815776 | tf_op jit(solution)/shard_map/jit(dynamic_index_in_dim)/dynamic_slice | solution.py:206
  101.5 1.0 copy.21
  102.5 4.1 %collective-permute-start.5 = (bf16[128,1664]{0,1:T(8,128)(2,1)}, bf16[128,1664]{0,1:T(8,128)(2,1)}, u32[]{:S(2)}, u32[]{:S(2)}) collective-permute-start(bf16[128,1664]{0,1:T(8,128)(2,1)} %bitcast.125), channel_id=1, source_target_pairs={{0,2},{2,4},{4,6},{6,8},{8,10},{10,12},{12,14},{14,0},{1,3},{3,5},... | collective-permute-start | bytes 1277960 | tf_op jit(solution)/shard_map/ppermute | solution.py:215
  106.6 0.3 copy.22
  106.9 0.6 slice_convert_fusion.10
  107.5 0.3 copy.23
  107.8 0.3 copy.24
  108.1 0.3 copy.25
  108.4 8.6 %collective-permute-start.9 = (bf16[128,1664]{0,1:T(8,128)(2,1)S(1)}, bf16[128,1664]{0,1:T(8,128)(2,1)}, u32[]{:S(2)}, u32[]{:S(2)}) collective-permute-start(bf16[128,1664]{0,1:T(8,128)(2,1)S(1)} %bitcast.124), channel_id=1, source_target_pairs={{0,14},{2,0},{4,2},{6,4},{8,6},{10,8},{12,10},{14,12},{1,15},{3,1}... | collective-permute-start | bytes 1277960 | tf_op jit(solution)/shard_map/ppermute | solution.py:218
  117.0 0.3 copy.26
  117.2 0.3 copy.27
  117.5 0.3 copy.20
  117.8 0.6 slice_convert_fusion.3
  118.4 5.2 %collective-permute-done.5 = bf16[128,1664]{0,1:T(8,128)(2,1)} collective-permute-done((bf16[128,1664]{0,1:T(8,128)(2,1)}, bf16[128,1664]{0,1:T(8,128)(2,1)}, u32[]{:S(2)}, u32[]{:S(2)}) %collective-permute-start.5) | collective-permute-done | bytes 426016 | tf_op jit(solution)/shard_map/ppermute | solution.py:215
  123.7 0.7 slice_convert_fusion.11
  124.4 0.8 fusion.31
  125.2 1.2 fusion.12
  126.4 0.6 concatenate.44
  127.0 1.9 %collective-permute-start.6 = (bf16[128,1664]{0,1:T(8,128)(2,1)S(1)}, bf16[128,1664]{0,1:T(8,128)(2,1)S(1)}, u32[]{:S(2)}, u32[]{:S(2)}) collective-permute-start(bf16[128,1664]{0,1:T(8,128)(2,1)S(1)} %concatenate.44), channel_id=1, source_target_pairs={{0,2},{2,4},{4,6},{6,8},{8,10},{10,12},{12,14},{14,0},{1,3},{3,5},... | collective-permute-start | bytes 1277960 | tf_op jit(solution)/shard_map/ppermute | solution.py:215
  129.0 0.7 slice_convert_fusion.4
  129.7 0.8 fusion.22
  130.5 1.2 fusion.6
  131.7 0.6 concatenate.47
  132.3 5.1 %collective-permute-start.10 = (bf16[128,1664]{0,1:T(8,128)(2,1)S(1)}, bf16[128,1664]{0,1:T(8,128)(2,1)S(1)}, u32[]{:S(2)}, u32[]{:S(2)}) collective-permute-start(bf16[128,1664]{0,1:T(8,128)(2,1)S(1)} %concatenate.47), channel_id=1, source_target_pairs={{0,14},{2,0},{4,2},{6,4},{8,6},{10,8},{12,10},{14,12},{1,15},{3,1}... | collective-permute-start | bytes 1277960 | tf_op jit(solution)/shard_map/ppermute | solution.py:218
  137.5 4.0 %collective-permute-done.6 = bf16[128,1664]{0,1:T(8,128)(2,1)S(1)} collective-permute-done((bf16[128,1664]{0,1:T(8,128)(2,1)S(1)}, bf16[128,1664]{0,1:T(8,128)(2,1)S(1)}, u32[]{:S(2)}, u32[]{:S(2)}) %collective-permute-start.6) | collective-permute-done | bytes 426016 | tf_op jit(solution)/shard_map/ppermute | solution.py:215
  141.5 0.2 fusion.10
  141.7 0.6 concatenate.45
  142.3 1.9 %collective-permute-start.7 = (bf16[128,1664]{0,1:T(8,128)(2,1)S(1)}, bf16[128,1664]{0,1:T(8,128)(2,1)S(1)}, u32[]{:S(2)}, u32[]{:S(2)}) collective-permute-start(bf16[128,1664]{0,1:T(8,128)(2,1)S(1)} %concatenate.45), channel_id=1, source_target_pairs={{0,2},{2,4},{4,6},{6,8},{8,10},{10,12},{12,14},{14,0},{1,3},{3,5},... | collective-permute-start | bytes 1277960 | tf_op jit(solution)/shard_map/ppermute | solution.py:215
  144.2 1.8 collective-permute-done.10
  146.0 0.2 fusion.4
  146.2 0.6 concatenate.48
  146.8 5.6 %collective-permute-start.11 = (bf16[128,1664]{0,1:T(8,128)(2,1)S(1)}, bf16[128,1664]{0,1:T(8,128)(2,1)S(1)}, u32[]{:S(2)}, u32[]{:S(2)}) collective-permute-start(bf16[128,1664]{0,1:T(8,128)(2,1)S(1)} %concatenate.48), channel_id=1, source_target_pairs={{0,14},{2,0},{4,2},{6,4},{8,6},{10,8},{12,10},{14,12},{1,15},{3,1}... | collective-permute-start | bytes 1277960 | tf_op jit(solution)/shard_map/ppermute | solution.py:222
  152.4 3.4 %collective-permute-done.7 = bf16[128,1664]{0,1:T(8,128)(2,1)S(1)} collective-permute-done((bf16[128,1664]{0,1:T(8,128)(2,1)S(1)}, bf16[128,1664]{0,1:T(8,128)(2,1)S(1)}, u32[]{:S(2)}, u32[]{:S(2)}) %collective-permute-start.7) | collective-permute-done | bytes 426016 | tf_op jit(solution)/shard_map/ppermute | solution.py:215
  155.9 0.2 fusion.8
  156.0 0.6 concatenate.46
  156.7 1.9 %collective-permute-start.8 = (bf16[128,1664]{0,1:T(8,128)(2,1)S(1)}, bf16[128,1664]{0,1:T(8,128)(2,1)S(1)}, u32[]{:S(2)}, u32[]{:S(2)}) collective-permute-start(bf16[128,1664]{0,1:T(8,128)(2,1)S(1)} %concatenate.46), channel_id=1, source_target_pairs={{0,2},{2,4},{4,6},{6,8},{8,10},{10,12},{12,14},{14,0},{1,3},{3,5},... | collective-permute-start | bytes 1277960 | tf_op jit(solution)/shard_map/ppermute | solution.py:220
  158.6 1.5 collective-permute-done.11
  160.1 9.3 %collective-permute-done.8 = bf16[128,1664]{0,1:T(8,128)(2,1)S(1)} collective-permute-done((bf16[128,1664]{0,1:T(8,128)(2,1)S(1)}, bf16[128,1664]{0,1:T(8,128)(2,1)S(1)}, u32[]{:S(2)}, u32[]{:S(2)}) %collective-permute-start.8) | collective-permute-done | bytes 426016 | tf_op jit(solution)/shard_map/ppermute | solution.py:220
  169.4 0.3 fusion
  169.6 0.9 copy.28
  (49 shorter events, 0.5 us)
Async XLA Ops:
  6.5 58.9 %all-gather.2.cloned.1.call-start = ((), (), s32[]{:S(2)}) async-start(), calls=%async_computation | async-start | bytes 3833856 | tf_op jit(solution)/shard_map/all_gather | solution.py:161
  11.4 24.5 %collective-permute-start = (bf16[2,128,1536]{2,1,0:T(8,128)(2,1)S(1)}, bf16[2,128,1536]{2,1,0:T(8,128)(2,1)S(1)}, u32[]{:S(2)}, u32[]{:S(2)}) collective-permute-start(bf16[2,128,1536]{2,1,0:T(8,128)(2,1)S(1)} %pad_maximum_fusion.4), channel_id=1, source_target_pairs={{0,16},{16,32},{32,48},{48,64},{64,80},{80,96},{96,112},{112,128},... | collective-permute-start | bytes 2359304 | tf_op jit(solution)/shard_map/ppermute | solution.py:21
  14.8 25.0 %collective-permute-start.2 = (bf16[2,128,1536]{2,1,0:T(8,128)(2,1)S(1)}, bf16[2,128,1536]{2,1,0:T(8,128)(2,1)S(1)}, u32[]{:S(2)}, u32[]{:S(2)}) collective-permute-start(bf16[2,128,1536]{2,1,0:T(8,128)(2,1)S(1)} %pad_maximum_fusion.4), channel_id=1, source_target_pairs={{0,1},{1,0},{2,3},{3,2},{4,5},{5,4},{6,7},{7,6},{8,9},{9,8},{10,11... | collective-permute-start | bytes 2359304 | tf_op jit(solution)/shard_map/ppermute | solution.py:147
  16.9 44.6 %copy-start = (bf16[128,1536]{1,0:T(8,128)(2,1)S(1)}, bf16[128,1536]{1,0:T(8,128)(2,1)}, u32[]{:S(2)}) copy-start(bf16[128,1536]{1,0:T(8,128)(2,1)} %param.7) | copy-start | bytes 1179652
  16.9 44.6 %copy-start.1 = (bf16[128,1536]{1,0:T(8,128)(2,1)S(1)}, bf16[128,1536]{1,0:T(8,128)(2,1)}, u32[]{:S(2)}) copy-start(bf16[128,1536]{1,0:T(8,128)(2,1)} %param.6) | copy-start | bytes 1179652
  35.9 23.6 %collective-permute-start.1 = (bf16[2,128,1536]{2,1,0:T(8,128)(2,1)S(1)}, bf16[2,128,1536]{2,1,0:T(8,128)(2,1)S(1)}, u32[]{:S(2)}, u32[]{:S(2)}) collective-permute-start(bf16[2,128,1536]{2,1,0:T(8,128)(2,1)S(1)} %collective-permute-done), channel_id=1, source_target_pairs={{0,16},{16,32},{32,48},{48,64},{64,80},{80,96},{96,112},{112,128},... | collective-permute-start | bytes 2359304 | tf_op jit(solution)/shard_map/ppermute | solution.py:21
  37.8 25.3 %collective-permute-start.3 = (bf16[2,128,1536]{2,1,0:T(8,128)(2,1)S(1)}, bf16[2,128,1536]{2,1,0:T(8,128)(2,1)S(1)}, u32[]{:S(2)}, u32[]{:S(2)}) collective-permute-start(bf16[2,128,1536]{2,1,0:T(8,128)(2,1)S(1)} %collective-permute-done), channel_id=1, source_target_pairs={{0,1},{1,0},{2,3},{3,2},{4,5},{5,4},{6,7},{7,6},{8,9},{9,8},{10,11... | collective-permute-start | bytes 2359304 | tf_op jit(solution)/shard_map/ppermute | solution.py:147
  59.5 4.2 %collective-permute-start.4 = (bf16[2,128,1536]{2,1,0:T(8,128)(2,1)S(1)}, bf16[2,128,1536]{2,1,0:T(8,128)(2,1)S(1)}, u32[]{:S(2)}, u32[]{:S(2)}) collective-permute-start(bf16[2,128,1536]{2,1,0:T(8,128)(2,1)S(1)} %collective-permute-done.1), channel_id=1, source_target_pairs={{0,1},{1,0},{2,3},{3,2},{4,5},{5,4},{6,7},{7,6},{8,9},{9,8},{10,11... | collective-permute-start | bytes 2359304 | tf_op jit(solution)/shard_map/ppermute | solution.py:147
  102.5 21.2 %collective-permute-start.5 = (bf16[128,1664]{0,1:T(8,128)(2,1)}, bf16[128,1664]{0,1:T(8,128)(2,1)}, u32[]{:S(2)}, u32[]{:S(2)}) collective-permute-start(bf16[128,1664]{0,1:T(8,128)(2,1)} %bitcast.125), channel_id=1, source_target_pairs={{0,2},{2,4},{4,6},{6,8},{8,10},{10,12},{12,14},{14,0},{1,3},{3,5},... | collective-permute-start | bytes 1277960 | tf_op jit(solution)/shard_map/ppermute | solution.py:215
  108.4 20.6 %collective-permute-start.9 = (bf16[128,1664]{0,1:T(8,128)(2,1)S(1)}, bf16[128,1664]{0,1:T(8,128)(2,1)}, u32[]{:S(2)}, u32[]{:S(2)}) collective-permute-start(bf16[128,1664]{0,1:T(8,128)(2,1)S(1)} %bitcast.124), channel_id=1, source_target_pairs={{0,14},{2,0},{4,2},{6,4},{8,6},{10,8},{12,10},{14,12},{1,15},{3,1}... | collective-permute-start | bytes 1277960 | tf_op jit(solution)/shard_map/ppermute | solution.py:218
  127.0 14.4 %collective-permute-start.6 = (bf16[128,1664]{0,1:T(8,128)(2,1)S(1)}, bf16[128,1664]{0,1:T(8,128)(2,1)S(1)}, u32[]{:S(2)}, u32[]{:S(2)}) collective-permute-start(bf16[128,1664]{0,1:T(8,128)(2,1)S(1)} %concatenate.44), channel_id=1, source_target_pairs={{0,2},{2,4},{4,6},{6,8},{8,10},{10,12},{12,14},{14,0},{1,3},{3,5},... | collective-permute-start | bytes 1277960 | tf_op jit(solution)/shard_map/ppermute | solution.py:215
  132.3 13.6 %collective-permute-start.10 = (bf16[128,1664]{0,1:T(8,128)(2,1)S(1)}, bf16[128,1664]{0,1:T(8,128)(2,1)S(1)}, u32[]{:S(2)}, u32[]{:S(2)}) collective-permute-start(bf16[128,1664]{0,1:T(8,128)(2,1)S(1)} %concatenate.47), channel_id=1, source_target_pairs={{0,14},{2,0},{4,2},{6,4},{8,6},{10,8},{12,10},{14,12},{1,15},{3,1}... | collective-permute-start | bytes 1277960 | tf_op jit(solution)/shard_map/ppermute | solution.py:218
  142.3 13.5 %collective-permute-start.7 = (bf16[128,1664]{0,1:T(8,128)(2,1)S(1)}, bf16[128,1664]{0,1:T(8,128)(2,1)S(1)}, u32[]{:S(2)}, u32[]{:S(2)}) collective-permute-start(bf16[128,1664]{0,1:T(8,128)(2,1)S(1)} %concatenate.45), channel_id=1, source_target_pairs={{0,2},{2,4},{4,6},{6,8},{8,10},{10,12},{12,14},{14,0},{1,3},{3,5},... | collective-permute-start | bytes 1277960 | tf_op jit(solution)/shard_map/ppermute | solution.py:215
  146.8 13.3 %collective-permute-start.11 = (bf16[128,1664]{0,1:T(8,128)(2,1)S(1)}, bf16[128,1664]{0,1:T(8,128)(2,1)S(1)}, u32[]{:S(2)}, u32[]{:S(2)}) collective-permute-start(bf16[128,1664]{0,1:T(8,128)(2,1)S(1)} %concatenate.48), channel_id=1, source_target_pairs={{0,14},{2,0},{4,2},{6,4},{8,6},{10,8},{12,10},{14,12},{1,15},{3,1}... | collective-permute-start | bytes 1277960 | tf_op jit(solution)/shard_map/ppermute | solution.py:222
  156.7 12.7 %collective-permute-start.8 = (bf16[128,1664]{0,1:T(8,128)(2,1)S(1)}, bf16[128,1664]{0,1:T(8,128)(2,1)S(1)}, u32[]{:S(2)}, u32[]{:S(2)}) collective-permute-start(bf16[128,1664]{0,1:T(8,128)(2,1)S(1)} %concatenate.46), channel_id=1, source_target_pairs={{0,2},{2,4},{4,6},{6,8},{8,10},{10,12},{12,14},{14,0},{1,3},{3,5},... | collective-permute-start | bytes 1277960 | tf_op jit(solution)/shard_map/ppermute | solution.py:220
Sparse Core Ops, SparseCore 0:
  10.3 55.0 all-gather.1

commit v13 on v12

--- a/solution.py
+++ b/solution.py
@@ -138,15 +138,15 @@
     core = lax.axis_index("core")
     row_index = lax.axis_index("pb")
 
-    stacked = jnp.stack([keys, values])
-
     swap = [(0, 1), (1, 0)]
-    lag_1 = passed_along(stacked, "pb", 1)
-    lag_2 = passed_along(lag_1, "pb", 1)
-    own = [stacked, lag_1, lag_2]
-    partner = [lax.ppermute(x, "core", swap) for x in own]
-    key_window = [jnp.concatenate([x[0] for x in side]) for side in (own, partner)]
-    value_window = [jnp.concatenate([x[1] for x in side]) for side in (own, partner)]
+    windows = []
+    for block in (keys, values):
+        lag_1 = passed_along(block, "pb", 1)
+        lag_2 = passed_along(lag_1, "pb", 1)
+        own = [block, lag_1, lag_2]
+        partner = [lax.ppermute(x, "core", swap) for x in own]
+        windows.append([jnp.concatenate(side) for side in (own, partner)])
+    key_window, value_window = windows
 
     lag_ids = jnp.arange(LAGS, dtype=jnp.int32)
     class_ids = jnp.arange(stripe_count, dtype=jnp.int32)

time: 178 us -> 170 us (0.955)
  the two profiles are of different devices: /device:TPU:32 before, /device:TPU:2 now
where the time goes in v13:
time: 170 us; the launch traced here: 169 us
  waiting for transfers between devices  49.1 us (29%)
  starting transfers between devices  46.3 us (27%)
  Pallas kernels  32.2 us (19%)
  other arithmetic  16.5 us (10%)
  between operations  14.7 us (9%)
  local copies, waits for them, and re-layouts  10.4 us (6%)
    pallas_call x1, Pallas kernels, pair_partials(): pl.pallas_call(pair_kernel, grid_spec=grid_spec, out_shape=jax.ShapeDtype...  32.2 us
    ppermute x4, waiting for transfers between devices, passed_along(): return lax.ppermute(block, axis, route)  16.7 us
    ppermute x6, starting transfers between devices, per_device(): partner = [lax.ppermute(x, 'core', swap) for x in own]  12.5 us
    ppermute x3, waiting for transfers between devices, per_device(): lax.ppermute(acc_r, 'z', rightward)  10.4 us
    all_gather x1, waiting for transfers between devices, per_device(): lax.all_gather(jnp.concatenate([queries, spare], axis=1), 'z', axis=0, ti...  10.3 us
    ppermute x4, starting transfers between devices, passed_along(): return lax.ppermute(block, axis, route)  10.3 us
    ppermute x2, starting transfers between devices, per_device(): lax.ppermute(acc_l, 'z', leftward)  9.98 us
    ppermute x1, waiting for transfers between devices, per_device(): final = [block_for(0), lax.ppermute(acc_r, 'z', rightward)]  8.53 us
  transfers between devices with their start and end apart: 18, of which 10 were waited for; matrix products, arithmetic and copies ran while one was open for 11% of the time, Pallas kernels for 0%

profile of v13, /device:TPU:2, one launch (start us, length us, event | category | flops | bytes accessed | tf_op | source)
XLA Modules:
  0.0 169.2 jit_solution(17132264355502858186)
XLA Ops:
  7.3 0.9 and_reduce_fusion
  8.3 0.1 convert_element_type.194
  8.4 1.8 %pad_maximum_fusion.4 = bf16[128,1664]{1,0:T(8,128)(2,1)} fusion(bf16[128,128]{1,0:T(8,128)(2,1)S(1)} %pad_convert_fusion, bf16[128,1536]{1,0:T(8,128)(2,1)} %param.5), kind=kLoop, calls=%fused_computation.31 | loop fusion | flops 851968 | bytes 851968 | tf_op jit(solution)/shard_map/concatenate | solution.py:162
  10.2 3.4 %collective-permute-start = (bf16[128,1536]{1,0:T(8,128)(2,1)}, bf16[128,1536]{1,0:T(8,128)(2,1)S(1)}, u32[]{:S(2)}, u32[]{:S(2)}) collective-permute-start(bf16[128,1536]{1,0:T(8,128)(2,1)} %param.6), channel_id=1, source_target_pairs={{0,16},{16,32},{32,48},{48,64},{64,80},{80,96},{96,112},{112,128},... | collective-permute-start | bytes 1179656 | tf_op jit(solution)/shard_map/ppermute | solution.py:21
  13.6 3.1 %collective-permute-start.5 = (bf16[128,1536]{1,0:T(8,128)(2,1)}, bf16[128,1536]{1,0:T(8,128)(2,1)S(1)}, u32[]{:S(2)}, u32[]{:S(2)}) collective-permute-start(bf16[128,1536]{1,0:T(8,128)(2,1)} %param.7), channel_id=1, source_target_pairs={{0,16},{16,32},{32,48},{48,64},{64,80},{80,96},{96,112},{112,128},... | collective-permute-start | bytes 1179656 | tf_op jit(solution)/shard_map/ppermute | solution.py:21
  16.7 10.8 %collective-permute-done = bf16[128,1536]{1,0:T(8,128)(2,1)S(1)} collective-permute-done((bf16[128,1536]{1,0:T(8,128)(2,1)}, bf16[128,1536]{1,0:T(8,128)(2,1)S(1)}, u32[]{:S(2)}, u32[]{:S(2)}) %collective-permute-start) | collective-permute-done | bytes 393248 | tf_op jit(solution)/shard_map/ppermute | solution.py:21
  27.6 1.9 %collective-permute-start.1 = (bf16[128,1536]{1,0:T(8,128)(2,1)S(1)}, bf16[128,1536]{1,0:T(8,128)(2,1)S(1)}, u32[]{:S(2)}, u32[]{:S(2)}) collective-permute-start(bf16[128,1536]{1,0:T(8,128)(2,1)S(1)} %collective-permute-done), channel_id=1, source_target_pairs={{0,16},{16,32},{32,48},{48,64},{64,80},{80,96},{96,112},{112,128},... | collective-permute-start | bytes 1179656 | tf_op jit(solution)/shard_map/ppermute | solution.py:21
  29.5 1.9 %collective-permute-start.2 = (bf16[128,1536]{1,0:T(8,128)(2,1)}, bf16[128,1536]{1,0:T(8,128)(2,1)S(1)}, u32[]{:S(2)}, u32[]{:S(2)}) collective-permute-start(bf16[128,1536]{1,0:T(8,128)(2,1)} %param.6), channel_id=1, source_target_pairs={{0,1},{1,0},{2,3},{3,2},{4,5},{5,4},{6,7},{7,6},{8,9},{9,8},{10,11... | collective-permute-start | bytes 1179656 | tf_op jit(solution)/shard_map/ppermute | solution.py:147
  31.4 4.4 %collective-permute-done.5 = bf16[128,1536]{1,0:T(8,128)(2,1)S(1)} collective-permute-done((bf16[128,1536]{1,0:T(8,128)(2,1)}, bf16[128,1536]{1,0:T(8,128)(2,1)S(1)}, u32[]{:S(2)}, u32[]{:S(2)}) %collective-permute-start.5) | collective-permute-done | bytes 393248 | tf_op jit(solution)/shard_map/ppermute | solution.py:21
  35.8 1.9 %collective-permute-start.6 = (bf16[128,1536]{1,0:T(8,128)(2,1)S(1)}, bf16[128,1536]{1,0:T(8,128)(2,1)S(1)}, u32[]{:S(2)}, u32[]{:S(2)}) collective-permute-start(bf16[128,1536]{1,0:T(8,128)(2,1)S(1)} %collective-permute-done.5), channel_id=1, source_target_pairs={{0,16},{16,32},{32,48},{48,64},{64,80},{80,96},{96,112},{112,128},... | collective-permute-start | bytes 1179656 | tf_op jit(solution)/shard_map/ppermute | solution.py:21
  37.7 1.9 %collective-permute-start.7 = (bf16[128,1536]{1,0:T(8,128)(2,1)}, bf16[128,1536]{1,0:T(8,128)(2,1)S(1)}, u32[]{:S(2)}, u32[]{:S(2)}) collective-permute-start(bf16[128,1536]{1,0:T(8,128)(2,1)} %param.7), channel_id=1, source_target_pairs={{0,1},{1,0},{2,3},{3,2},{4,5},{5,4},{6,7},{7,6},{8,9},{9,8},{10,11... | collective-permute-start | bytes 1179656 | tf_op jit(solution)/shard_map/ppermute | solution.py:147
  39.8 2.4 %collective-permute-start.3 = (bf16[128,1536]{1,0:T(8,128)(2,1)S(1)}, bf16[128,1536]{1,0:T(8,128)(2,1)S(1)}, u32[]{:S(2)}, u32[]{:S(2)}) collective-permute-start(bf16[128,1536]{1,0:T(8,128)(2,1)S(1)} %collective-permute-done), channel_id=1, source_target_pairs={{0,1},{1,0},{2,3},{3,2},{4,5},{5,4},{6,7},{7,6},{8,9},{9,8},{10,11... | collective-permute-start | bytes 1179656 | tf_op jit(solution)/shard_map/ppermute | solution.py:147
  42.2 1.4 collective-permute-done.1
  43.7 1.9 %collective-permute-start.4 = (bf16[128,1536]{1,0:T(8,128)(2,1)S(1)}, bf16[128,1536]{1,0:T(8,128)(2,1)S(1)}, u32[]{:S(2)}, u32[]{:S(2)}) collective-permute-start(bf16[128,1536]{1,0:T(8,128)(2,1)S(1)} %collective-permute-done.1), channel_id=1, source_target_pairs={{0,1},{1,0},{2,3},{3,2},{4,5},{5,4},{6,7},{7,6},{8,9},{9,8},{10,11... | collective-permute-start | bytes 1179656 | tf_op jit(solution)/shard_map/ppermute | solution.py:147
  45.6 2.1 %pad_maximum_fusion.k0_ref = bf16[384,1536]{1,0:T(8,128)(2,1)} fusion(bf16[128,1536]{1,0:T(8,128)(2,1)S(1)} %collective-permute-done.1, bf16[128,1536]{1,0:T(8,128)(2,1)S(1)} %collective-permute-done, bf16[128,1536]{1,0:T(8,128)(2,1)} %param.6), kind=kLoop, calls=%fused_computation | loop fusion | flops 3538944 | bytes 2359296 | tf_op jit(solution)/shard_map/concatenate | solution.py:148
  47.7 2.4 %collective-permute-start.8 = (bf16[128,1536]{1,0:T(8,128)(2,1)S(1)}, bf16[128,1536]{1,0:T(8,128)(2,1)S(1)}, u32[]{:S(2)}, u32[]{:S(2)}) collective-permute-start(bf16[128,1536]{1,0:T(8,128)(2,1)S(1)} %collective-permute-done.5), channel_id=1, source_target_pairs={{0,1},{1,0},{2,3},{3,2},{4,5},{5,4},{6,7},{7,6},{8,9},{9,8},{10,11... | collective-permute-start | bytes 1179656 | tf_op jit(solution)/shard_map/ppermute | solution.py:147
  50.1 1.9 %collective-permute-start.9 = (bf16[128,1536]{1,0:T(8,128)(2,1)S(1)}, bf16[128,1536]{1,0:T(8,128)(2,1)S(1)}, u32[]{:S(2)}, u32[]{:S(2)}) collective-permute-start(bf16[128,1536]{1,0:T(8,128)(2,1)S(1)} %collective-permute-done.6), channel_id=1, source_target_pairs={{0,1},{1,0},{2,3},{3,2},{4,5},{5,4},{6,7},{7,6},{8,9},{9,8},{10,11... | collective-permute-start | bytes 1179656 | tf_op jit(solution)/shard_map/ppermute | solution.py:147
  52.1 1.1 pad_maximum_fusion.2.v0_ref
  53.2 1.2 pad_maximum_fusion.1.k1_ref
  54.4 1.1 pad_maximum_fusion.3.v1_ref
  55.5 10.3 %all-gather.2.cloned.1.call-done.q_ref = bf16[1024,1664]{1,0:T(8,128)(2,1)} async-done(((bf16[128,1664]{1,0:T(8,128)(2,1)}), bf16[1024,1664]{1,0:T(8,128)(2,1)}) %all-gather.2.cloned.1.call-update) | async-done | bytes 3407888 | tf_op jit(solution)/shard_map/all_gather | solution.py:161
  65.8 0.7 slice.459
  66.9 0.6 pad_add_fusion.1.info_ref
  67.5 32.2 %shard_map.55 = bf16[1024,1664]{1,0:T(8,128)(2,1)} custom-call(s32[50]{0:T(128)} %pad_add_fusion.1.info_ref, bf16[1024,1664]{1,0:T(8,128)(2,1)} %all-gather.2.cloned.1.call-done.q_ref, bf16[384,1536]{1,0:T(8,128)(2,1)} %pad_maximum_fusion.k0_ref, bf16[384,1536]{1,0:T(8,128)(2,1)} %pad_maximum_fusion.1.k1_ref, bf16[384,1536]{1,0:T(8,128)(2,1)} %pad_maximum_fusion.2.v0_ref, ...), custom_call_target="tpu_custom_call" | custom-call | flops 3221225472 | bytes 11534336 | tf_op jit(solution)/shard_map/pallas_call | solution.py:117
  99.8 2.2 %constant_dynamic-slice_fusion.7 = (bf16[1,128,1664]{2,1,0:T(8,128)(2,1)S(1)}, bf16[1,128,1664]{2,1,0:T(8,128)(2,1)S(1)}, bf16[1,128,1664]{2,1,0:T(8,128)(2,1)S(...) fusion(bf16[8,128,1664]{2,1,0:T(8,128)(2,1)} %bitcast.87, ...), kind=kLoop, calls=%fused_computation.148 | loop fusion | bytes 6815776 | tf_op jit(solution)/shard_map/jit(dynamic_index_in_dim)/dynamic_slice | solution.py:206
  101.9 1.0 copy.21
  102.9 2.2 %collective-permute-start.10 = (bf16[128,1664]{0,1:T(8,128)(2,1)}, bf16[128,1664]{0,1:T(8,128)(2,1)}, u32[]{:S(2)}, u32[]{:S(2)}) collective-permute-start(bf16[128,1664]{0,1:T(8,128)(2,1)} %bitcast.101), channel_id=1, source_target_pairs={{0,2},{2,4},{4,6},{6,8},{8,10},{10,12},{12,14},{14,0},{1,3},{3,5},... | collective-permute-start | bytes 1277960 | tf_op jit(solution)/shard_map/ppermute | solution.py:215
  105.1 0.3 copy.22
  105.4 0.6 slice_convert_fusion.10
  106.1 0.3 copy.23
  106.3 0.3 copy.24
  106.6 0.3 copy.25
  106.9 4.8 %collective-permute-start.14 = (bf16[128,1664]{0,1:T(8,128)(2,1)S(1)}, bf16[128,1664]{0,1:T(8,128)(2,1)}, u32[]{:S(2)}, u32[]{:S(2)}) collective-permute-start(bf16[128,1664]{0,1:T(8,128)(2,1)S(1)} %bitcast.100), channel_id=1, source_target_pairs={{0,14},{2,0},{4,2},{6,4},{8,6},{10,8},{12,10},{14,12},{1,15},{3,1}... | collective-permute-start | bytes 1277960 | tf_op jit(solution)/shard_map/ppermute | solution.py:218
  111.8 0.3 copy.26
  112.0 0.3 copy.27
  112.3 0.3 copy.20
  112.6 0.6 slice_convert_fusion.3
  113.2 4.5 %collective-permute-done.10 = bf16[128,1664]{0,1:T(8,128)(2,1)} collective-permute-done((bf16[128,1664]{0,1:T(8,128)(2,1)}, bf16[128,1664]{0,1:T(8,128)(2,1)}, u32[]{:S(2)}, u32[]{:S(2)}) %collective-permute-start.10) | collective-permute-done | bytes 426016 | tf_op jit(solution)/shard_map/ppermute | solution.py:215
  117.7 0.7 slice_convert_fusion.11
  118.5 0.8 fusion.31
  119.3 1.2 fusion.12
  120.5 0.6 concatenate.44
  121.1 1.9 %collective-permute-start.11 = (bf16[128,1664]{0,1:T(8,128)(2,1)S(1)}, bf16[128,1664]{0,1:T(8,128)(2,1)S(1)}, u32[]{:S(2)}, u32[]{:S(2)}) collective-permute-start(bf16[128,1664]{0,1:T(8,128)(2,1)S(1)} %concatenate.44), channel_id=1, source_target_pairs={{0,2},{2,4},{4,6},{6,8},{8,10},{10,12},{12,14},{14,0},{1,3},{3,5},... | collective-permute-start | bytes 1277960 | tf_op jit(solution)/shard_map/ppermute | solution.py:215
  123.0 0.7 slice_convert_fusion.4
  123.8 0.8 fusion.22
  124.6 1.2 fusion.6
  125.8 0.6 concatenate.47
  126.4 5.1 %collective-permute-start.15 = (bf16[128,1664]{0,1:T(8,128)(2,1)S(1)}, bf16[128,1664]{0,1:T(8,128)(2,1)S(1)}, u32[]{:S(2)}, u32[]{:S(2)}) collective-permute-start(bf16[128,1664]{0,1:T(8,128)(2,1)S(1)} %concatenate.47), channel_id=1, source_target_pairs={{0,14},{2,0},{4,2},{6,4},{8,6},{10,8},{12,10},{14,12},{1,15},{3,1}... | collective-permute-start | bytes 1277960 | tf_op jit(solution)/shard_map/ppermute | solution.py:218
  131.5 3.2 %collective-permute-done.11 = bf16[128,1664]{0,1:T(8,128)(2,1)S(1)} collective-permute-done((bf16[128,1664]{0,1:T(8,128)(2,1)S(1)}, bf16[128,1664]{0,1:T(8,128)(2,1)S(1)}, u32[]{:S(2)}, u32[]{:S(2)}) %collective-permute-start.11) | collective-permute-done | bytes 426016 | tf_op jit(solution)/shard_map/ppermute | solution.py:215
  134.8 0.2 fusion.10
  135.0 0.6 concatenate.45
  135.6 1.9 %collective-permute-start.12 = (bf16[128,1664]{0,1:T(8,128)(2,1)S(1)}, bf16[128,1664]{0,1:T(8,128)(2,1)S(1)}, u32[]{:S(2)}, u32[]{:S(2)}) collective-permute-start(bf16[128,1664]{0,1:T(8,128)(2,1)S(1)} %concatenate.45), channel_id=1, source_target_pairs={{0,2},{2,4},{4,6},{6,8},{8,10},{10,12},{12,14},{14,0},{1,3},{3,5},... | collective-permute-start | bytes 1277960 | tf_op jit(solution)/shard_map/ppermute | solution.py:215
  137.5 1.7 %collective-permute-done.15 = bf16[128,1664]{0,1:T(8,128)(2,1)S(1)} collective-permute-done((bf16[128,1664]{0,1:T(8,128)(2,1)S(1)}, bf16[128,1664]{0,1:T(8,128)(2,1)S(1)}, u32[]{:S(2)}, u32[]{:S(2)}) %collective-permute-start.15) | collective-permute-done | bytes 426016 | tf_op jit(solution)/shard_map/ppermute | solution.py:218
  139.3 0.2 fusion.4
  139.5 0.6 concatenate.48
  140.1 5.6 %collective-permute-start.16 = (bf16[128,1664]{0,1:T(8,128)(2,1)S(1)}, bf16[128,1664]{0,1:T(8,128)(2,1)S(1)}, u32[]{:S(2)}, u32[]{:S(2)}) collective-permute-start(bf16[128,1664]{0,1:T(8,128)(2,1)S(1)} %concatenate.48), channel_id=1, source_target_pairs={{0,14},{2,0},{4,2},{6,4},{8,6},{10,8},{12,10},{14,12},{1,15},{3,1}... | collective-permute-start | bytes 1277960 | tf_op jit(solution)/shard_map/ppermute | solution.py:222
  145.7 2.6 %collective-permute-done.12 = bf16[128,1664]{0,1:T(8,128)(2,1)S(1)} collective-permute-done((bf16[128,1664]{0,1:T(8,128)(2,1)S(1)}, bf16[128,1664]{0,1:T(8,128)(2,1)S(1)}, u32[]{:S(2)}, u32[]{:S(2)}) %collective-permute-start.12) | collective-permute-done | bytes 426016 | tf_op jit(solution)/shard_map/ppermute | solution.py:215
  148.4 0.2 fusion.8
  148.6 0.6 concatenate.46
  149.2 1.9 %collective-permute-start.13 = (bf16[128,1664]{0,1:T(8,128)(2,1)S(1)}, bf16[128,1664]{0,1:T(8,128)(2,1)S(1)}, u32[]{:S(2)}, u32[]{:S(2)}) collective-permute-start(bf16[128,1664]{0,1:T(8,128)(2,1)S(1)} %concatenate.46), channel_id=1, source_target_pairs={{0,2},{2,4},{4,6},{6,8},{8,10},{10,12},{12,14},{14,0},{1,3},{3,5},... | collective-permute-start | bytes 1277960 | tf_op jit(solution)/shard_map/ppermute | solution.py:220
  151.2 1.5 collective-permute-done.16
  152.6 8.5 %collective-permute-done.13 = bf16[128,1664]{0,1:T(8,128)(2,1)S(1)} collective-permute-done((bf16[128,1664]{0,1:T(8,128)(2,1)S(1)}, bf16[128,1664]{0,1:T(8,128)(2,1)S(1)}, u32[]{:S(2)}, u32[]{:S(2)}) %collective-permute-start.13) | collective-permute-done | bytes 426016 | tf_op jit(solution)/shard_map/ppermute | solution.py:220
  161.2 0.3 fusion
  161.4 0.9 copy.28
  (51 shorter events, 0.8 us)
Async XLA Ops:
  6.5 45.5 %copy-start = (bf16[128,1536]{1,0:T(8,128)(2,1)S(1)}, bf16[128,1536]{1,0:T(8,128)(2,1)}, u32[]{:S(2)}) copy-start(bf16[128,1536]{1,0:T(8,128)(2,1)} %param.7) | copy-start | bytes 1179652
  6.5 59.3 %all-gather.2.cloned.1.call-start = ((), (), s32[]{:S(2)}) async-start(), calls=%async_computation | async-start | bytes 3833856 | tf_op jit(solution)/shard_map/all_gather | solution.py:161
  10.2 17.3 %collective-permute-start = (bf16[128,1536]{1,0:T(8,128)(2,1)}, bf16[128,1536]{1,0:T(8,128)(2,1)S(1)}, u32[]{:S(2)}, u32[]{:S(2)}) collective-permute-start(bf16[128,1536]{1,0:T(8,128)(2,1)} %param.6), channel_id=1, source_target_pairs={{0,16},{16,32},{32,48},{48,64},{64,80},{80,96},{96,112},{112,128},... | collective-permute-start | bytes 1179656 | tf_op jit(solution)/shard_map/ppermute | solution.py:21
  13.6 22.2 %collective-permute-start.5 = (bf16[128,1536]{1,0:T(8,128)(2,1)}, bf16[128,1536]{1,0:T(8,128)(2,1)S(1)}, u32[]{:S(2)}, u32[]{:S(2)}) collective-permute-start(bf16[128,1536]{1,0:T(8,128)(2,1)} %param.7), channel_id=1, source_target_pairs={{0,16},{16,32},{32,48},{48,64},{64,80},{80,96},{96,112},{112,128},... | collective-permute-start | bytes 1179656 | tf_op jit(solution)/shard_map/ppermute | solution.py:21
  27.6 16.1 %collective-permute-start.1 = (bf16[128,1536]{1,0:T(8,128)(2,1)S(1)}, bf16[128,1536]{1,0:T(8,128)(2,1)S(1)}, u32[]{:S(2)}, u32[]{:S(2)}) collective-permute-start(bf16[128,1536]{1,0:T(8,128)(2,1)S(1)} %collective-permute-done), channel_id=1, source_target_pairs={{0,16},{16,32},{32,48},{48,64},{64,80},{80,96},{96,112},{112,128},... | collective-permute-start | bytes 1179656 | tf_op jit(solution)/shard_map/ppermute | solution.py:21
  29.5 18.3 %collective-permute-start.2 = (bf16[128,1536]{1,0:T(8,128)(2,1)}, bf16[128,1536]{1,0:T(8,128)(2,1)S(1)}, u32[]{:S(2)}, u32[]{:S(2)}) collective-permute-start(bf16[128,1536]{1,0:T(8,128)(2,1)} %param.6), channel_id=1, source_target_pairs={{0,1},{1,0},{2,3},{3,2},{4,5},{5,4},{6,7},{7,6},{8,9},{9,8},{10,11... | collective-permute-start | bytes 1179656 | tf_op jit(solution)/shard_map/ppermute | solution.py:147
  35.8 14.3 %collective-permute-start.6 = (bf16[128,1536]{1,0:T(8,128)(2,1)S(1)}, bf16[128,1536]{1,0:T(8,128)(2,1)S(1)}, u32[]{:S(2)}, u32[]{:S(2)}) collective-permute-start(bf16[128,1536]{1,0:T(8,128)(2,1)S(1)} %collective-permute-done.5), channel_id=1, source_target_pairs={{0,16},{16,32},{32,48},{48,64},{64,80},{80,96},{96,112},{112,128},... | collective-permute-start | bytes 1179656 | tf_op jit(solution)/shard_map/ppermute | solution.py:21
  37.7 16.6 %collective-permute-start.7 = (bf16[128,1536]{1,0:T(8,128)(2,1)}, bf16[128,1536]{1,0:T(8,128)(2,1)S(1)}, u32[]{:S(2)}, u32[]{:S(2)}) collective-permute-start(bf16[128,1536]{1,0:T(8,128)(2,1)} %param.7), channel_id=1, source_target_pairs={{0,1},{1,0},{2,3},{3,2},{4,5},{5,4},{6,7},{7,6},{8,9},{9,8},{10,11... | collective-permute-start | bytes 1179656 | tf_op jit(solution)/shard_map/ppermute | solution.py:147
  39.8 13.4 %collective-permute-start.3 = (bf16[128,1536]{1,0:T(8,128)(2,1)S(1)}, bf16[128,1536]{1,0:T(8,128)(2,1)S(1)}, u32[]{:S(2)}, u32[]{:S(2)}) collective-permute-start(bf16[128,1536]{1,0:T(8,128)(2,1)S(1)} %collective-permute-done), channel_id=1, source_target_pairs={{0,1},{1,0},{2,3},{3,2},{4,5},{5,4},{6,7},{7,6},{8,9},{9,8},{10,11... | collective-permute-start | bytes 1179656 | tf_op jit(solution)/shard_map/ppermute | solution.py:147
  43.7 9.5 %collective-permute-start.4 = (bf16[128,1536]{1,0:T(8,128)(2,1)S(1)}, bf16[128,1536]{1,0:T(8,128)(2,1)S(1)}, u32[]{:S(2)}, u32[]{:S(2)}) collective-permute-start(bf16[128,1536]{1,0:T(8,128)(2,1)S(1)} %collective-permute-done.1), channel_id=1, source_target_pairs={{0,1},{1,0},{2,3},{3,2},{4,5},{5,4},{6,7},{7,6},{8,9},{9,8},{10,11... | collective-permute-start | bytes 1179656 | tf_op jit(solution)/shard_map/ppermute | solution.py:147
  47.7 6.7 %collective-permute-start.8 = (bf16[128,1536]{1,0:T(8,128)(2,1)S(1)}, bf16[128,1536]{1,0:T(8,128)(2,1)S(1)}, u32[]{:S(2)}, u32[]{:S(2)}) collective-permute-start(bf16[128,1536]{1,0:T(8,128)(2,1)S(1)} %collective-permute-done.5), channel_id=1, source_target_pairs={{0,1},{1,0},{2,3},{3,2},{4,5},{5,4},{6,7},{7,6},{8,9},{9,8},{10,11... | collective-permute-start | bytes 1179656 | tf_op jit(solution)/shard_map/ppermute | solution.py:147
  50.1 4.2 %collective-permute-start.9 = (bf16[128,1536]{1,0:T(8,128)(2,1)S(1)}, bf16[128,1536]{1,0:T(8,128)(2,1)S(1)}, u32[]{:S(2)}, u32[]{:S(2)}) collective-permute-start(bf16[128,1536]{1,0:T(8,128)(2,1)S(1)} %collective-permute-done.6), channel_id=1, source_target_pairs={{0,1},{1,0},{2,3},{3,2},{4,5},{5,4},{6,7},{7,6},{8,9},{9,8},{10,11... | collective-permute-start | bytes 1179656 | tf_op jit(solution)/shard_map/ppermute | solution.py:147
  102.9 14.8 %collective-permute-start.10 = (bf16[128,1664]{0,1:T(8,128)(2,1)}, bf16[128,1664]{0,1:T(8,128)(2,1)}, u32[]{:S(2)}, u32[]{:S(2)}) collective-permute-start(bf16[128,1664]{0,1:T(8,128)(2,1)} %bitcast.101), channel_id=1, source_target_pairs={{0,2},{2,4},{4,6},{6,8},{8,10},{10,12},{12,14},{14,0},{1,3},{3,5},... | collective-permute-start | bytes 1277960 | tf_op jit(solution)/shard_map/ppermute | solution.py:215
  106.9 16.1 %collective-permute-start.14 = (bf16[128,1664]{0,1:T(8,128)(2,1)S(1)}, bf16[128,1664]{0,1:T(8,128)(2,1)}, u32[]{:S(2)}, u32[]{:S(2)}) collective-permute-start(bf16[128,1664]{0,1:T(8,128)(2,1)S(1)} %bitcast.100), channel_id=1, source_target_pairs={{0,14},{2,0},{4,2},{6,4},{8,6},{10,8},{12,10},{14,12},{1,15},{3,1}... | collective-permute-start | bytes 1277960 | tf_op jit(solution)/shard_map/ppermute | solution.py:218
  121.1 13.6 %collective-permute-start.11 = (bf16[128,1664]{0,1:T(8,128)(2,1)S(1)}, bf16[128,1664]{0,1:T(8,128)(2,1)S(1)}, u32[]{:S(2)}, u32[]{:S(2)}) collective-permute-start(bf16[128,1664]{0,1:T(8,128)(2,1)S(1)} %concatenate.44), channel_id=1, source_target_pairs={{0,2},{2,4},{4,6},{6,8},{8,10},{10,12},{12,14},{14,0},{1,3},{3,5},... | collective-permute-start | bytes 1277960 | tf_op jit(solution)/shard_map/ppermute | solution.py:215
  126.4 12.9 %collective-permute-start.15 = (bf16[128,1664]{0,1:T(8,128)(2,1)S(1)}, bf16[128,1664]{0,1:T(8,128)(2,1)S(1)}, u32[]{:S(2)}, u32[]{:S(2)}) collective-permute-start(bf16[128,1664]{0,1:T(8,128)(2,1)S(1)} %concatenate.47), channel_id=1, source_target_pairs={{0,14},{2,0},{4,2},{6,4},{8,6},{10,8},{12,10},{14,12},{1,15},{3,1}... | collective-permute-start | bytes 1277960 | tf_op jit(solution)/shard_map/ppermute | solution.py:218
  135.6 12.8 %collective-permute-start.12 = (bf16[128,1664]{0,1:T(8,128)(2,1)S(1)}, bf16[128,1664]{0,1:T(8,128)(2,1)S(1)}, u32[]{:S(2)}, u32[]{:S(2)}) collective-permute-start(bf16[128,1664]{0,1:T(8,128)(2,1)S(1)} %concatenate.45), channel_id=1, source_target_pairs={{0,2},{2,4},{4,6},{6,8},{8,10},{10,12},{12,14},{14,0},{1,3},{3,5},... | collective-permute-start | bytes 1277960 | tf_op jit(solution)/shard_map/ppermute | solution.py:215
  140.1 12.5 %collective-permute-start.16 = (bf16[128,1664]{0,1:T(8,128)(2,1)S(1)}, bf16[128,1664]{0,1:T(8,128)(2,1)S(1)}, u32[]{:S(2)}, u32[]{:S(2)}) collective-permute-start(bf16[128,1664]{0,1:T(8,128)(2,1)S(1)} %concatenate.48), channel_id=1, source_target_pairs={{0,14},{2,0},{4,2},{6,4},{8,6},{10,8},{12,10},{14,12},{1,15},{3,1}... | collective-permute-start | bytes 1277960 | tf_op jit(solution)/shard_map/ppermute | solution.py:222
  149.2 11.9 %collective-permute-start.13 = (bf16[128,1664]{0,1:T(8,128)(2,1)S(1)}, bf16[128,1664]{0,1:T(8,128)(2,1)S(1)}, u32[]{:S(2)}, u32[]{:S(2)}) collective-permute-start(bf16[128,1664]{0,1:T(8,128)(2,1)S(1)} %concatenate.46), channel_id=1, source_target_pairs={{0,2},{2,4},{4,6},{6,8},{8,10},{10,12},{12,14},{14,0},{1,3},{3,5},... | collective-permute-start | bytes 1277960 | tf_op jit(solution)/shard_map/ppermute | solution.py:220
Sparse Core Ops, SparseCore 0:
  10.3 55.4 all-gather.1
